TPU v7x, 512 devices: a whole 4x8x8 slice. The times are simulated.
512 devices in a mesh: ctx: 64 (over z_hi, y, core), head: 8 (over x, z_lo).
Axes of the slice: x: 4, y: 8, z: 8 (z_hi: 4, z_lo: 2; z = z_hi * 2 + z_lo), core: 2. Of those that a mesh axis runs over, the one named last changes fastest.
Arguments:
- queries: bfloat16 [65536, 8192], P(('ctx', 'head')), may hold values from -13 to 13
- keys: bfloat16 [65536, 1024], P(('ctx', 'head')), may hold values from -13 to 13
- values: bfloat16 [65536, 1024], P(('ctx', 'head')), may hold values from -6 to 6
- doc_ids: int32 [65536], replicated, may hold values from 0 to 63, never falling along the last dimension, each value on 1 to 1280 neighbouring positions
Outputs:
- attended: bfloat16 [65536, 8192], P(('ctx', 'head'))
Inputs may be any that keep to these rules, and one draw needn't show every extreme that they name: `doc_ids`: document numbers never fall along the sequence; every document has 1 to 1280 tokens and one has exactly 1280; every number of 0 to 63 occurs.
All inputs are finite; a program needn't handle non-finite values.
Results may differ from a plain program's by a relative error of at most 0.0025.
Values may be sent and summed in bfloat16 or wider, within the bound.
No kernel may reach another device: no remote copies, remote signals or barrier semaphores. Data moves between devices by JAX's collectives and lax.ppermute only.
A program may use at most 64 MiB of HBM per device.

v0:
```python
import jax
import jax.numpy as jnp
from jax import lax
from jax.sharding import PartitionSpec as P

HD = 128
QH = 64
KVH = 8
BLOCK = 256
DOC_BLOCKS = 5
QBLK_DEV = 4
PREV = 2


floor_score = -1e30


def from_behind(value, axis, steps):
    count = lax.axis_size(axis)
    leading, last = (max(0, -steps), min(count, count - steps))
    return lax.ppermute(value, axis, [(source, source + steps) for source in range(leading, last)])


def attend_tile(running, query_block, key_tile, value_tile, allowed):
    maxima, totals, accum = running
    scores = jnp.einsum(
        "qgjd,kgd->qgjk", query_block, key_tile, preferred_element_type=jnp.float32
    ) * HD ** (-0.5)
    scores = jnp.where(allowed[:, None, None, :], scores, floor_score)
    fresh = jnp.maximum(maxima, jnp.max(scores, axis=-1))
    factor = jnp.exp(maxima - fresh)
    weights = jnp.exp(scores - fresh[..., None])
    totals = totals * factor + jnp.sum(weights, axis=-1)
    accum = accum * factor[..., None] + jnp.einsum(
        "qgjk,kgd->qgjd",
        weights.astype(jnp.bfloat16),
        value_tile,
        preferred_element_type=jnp.float32,
    )
    return (fresh, totals, accum)


def key_window(paired):
    pieces = []
    for offset in range(1, PREV + 1):
        pieces.append(from_behind(paired, "ctx", offset))
    return jnp.concatenate(pieces[::-1] + [paired], axis=1)


def shards(queries, keys, values, doc_ids):
    per_group = QH // KVH
    range_rows = QBLK_DEV * BLOCK
    ctx_pos = lax.axis_index("ctx")
    local_queries, local_keys, local_values = (
        lax.all_to_all(queries, "head", split_axis=1, concat_axis=0, tiled=True),
        lax.all_to_all(keys, "head", split_axis=1, concat_axis=0, tiled=True),
        lax.all_to_all(values, "head", split_axis=1, concat_axis=0, tiled=True),
    )
    window = key_window(jnp.stack([local_keys, local_values]))
    groups = local_keys.shape[1] // HD
    window_keys = window[0].reshape(-1, groups, HD)
    window_values = window[1].reshape(-1, groups, HD)
    padded_ids = jnp.concatenate([jnp.full((PREV * range_rows,), -1, jnp.int32), doc_ids])
    window_ids = lax.dynamic_slice_in_dim(padded_ids, ctx_pos * range_rows, (PREV + 1) * range_rows)
    range_ids = lax.dynamic_slice_in_dim(doc_ids, ctx_pos * range_rows, range_rows)
    window_base = (ctx_pos - PREV) * range_rows
    offsets = jnp.arange(BLOCK, dtype=jnp.int32)
    shaped_queries = local_queries.reshape(range_rows, groups, per_group, HD)
    outputs = []
    for block_index in range(QBLK_DEV):
        query_block = shaped_queries[block_index * BLOCK : (block_index + 1) * BLOCK]
        block_ids = range_ids[block_index * BLOCK : (block_index + 1) * BLOCK]
        query_pos = ctx_pos * range_rows + block_index * BLOCK + offsets

        def visit(running, tile, query_block=query_block, block_ids=block_ids, query_pos=query_pos):
            start = tile * BLOCK
            key_tile = lax.dynamic_slice_in_dim(window_keys, start, BLOCK, 0)
            value_tile = lax.dynamic_slice_in_dim(window_values, start, BLOCK, 0)
            tile_ids = lax.dynamic_slice_in_dim(window_ids, start, BLOCK)
            key_pos = window_base + start + offsets
            allowed = (block_ids[:, None] == tile_ids[None, :]) & (
                key_pos[None, :] <= query_pos[:, None]
            )
            return attend_tile(running, query_block, key_tile, value_tile, allowed)

        initial = (
            jnp.full((BLOCK, groups, per_group), floor_score, jnp.float32),
            jnp.zeros((BLOCK, groups, per_group), jnp.float32),
            jnp.zeros((BLOCK, groups, per_group, HD), jnp.float32),
        )
        diagonal = PREV * QBLK_DEV + block_index
        running = visit(initial, diagonal)

        def backward(offset, running, visit=visit, block_ids=block_ids, diagonal=diagonal):
            tile = diagonal - offset
            return visit(running, tile)

        running = lax.fori_loop(1, DOC_BLOCKS + 1, backward, running)
        maxima, totals, accum = running
        outputs.append(
            (accum / totals[..., None]).astype(jnp.bfloat16).reshape(BLOCK, groups * per_group * HD)
        )
    local_out = jnp.concatenate(outputs, axis=0)
    return lax.all_to_all(local_out, "head", split_axis=0, concat_axis=1, tiled=True)


def solution(mesh):
    in_specs = (P(("ctx", "head"), None), P(("ctx", "head"), None), P(("ctx", "head"), None), P())
    out_specs = P(("ctx", "head"), None)
    return jax.shard_map(shards, mesh=mesh, in_specs=in_specs, out_specs=out_specs, check_vma=False)
```

profile of v0, /device:TPU:128, one launch (start us, length us, event | category | flops | bytes accessed | tf_op | source)
XLA Modules:
  0.0 223.2 jit_solution(8170471879626285882)
XLA Ops:
  0.0 0.9 copy-done
  1.7 6.1 %all-to-all-start = ((bf16[128,8,128]{2,0,1:T(8,128)(2,1)}), bf16[128,8,128]{2,0,1:T(8,128)(2,1)S(1)}, u32[]{:S(2)}, u32[]{:S(2)}) async-start(bf16[128,8,128]{2,0,1:T(8,128)(2,1)} %copy_bitcast_fusion.2), calls=%async_computation | async-start | bytes 524288 | tf_op jit(solution)/shard_map/all_to_all | solution.py:56
  7.8 1.7 copy_bitcast_fusion.1
  9.5 5.6 %all-to-all-done = bf16[128,8,128]{2,0,1:T(8,128)(2,1)S(1)} async-done(((bf16[128,8,128]{2,0,1:T(8,128)(2,1)}), bf16[128,8,128]{2,0,1:T(8,128)(2,1)S(1)}, u32[]{:S(2)}, u32[]{:S(2)}) %all-to-all-start) | async-done | bytes 262176 | tf_op jit(solution)/shard_map/all_to_all | solution.py:56
  15.1 3.4 %all-to-all-start.2 = ((bf16[128,8,128]{2,0,1:T(8,128)(2,1)}), bf16[128,8,128]{2,0,1:T(8,128)(2,1)S(1)}, u32[]{:S(2)}, u32[]{:S(2)}) async-start(bf16[128,8,128]{2,0,1:T(8,128)(2,1)} %copy_bitcast_fusion.1), calls=%async_computation.2 | async-start | bytes 524288 | tf_op jit(solution)/shard_map/all_to_all | solution.py:57
  18.5 1.6 copy.129
  20.1 5.7 %all-to-all-done.2 = bf16[128,8,128]{2,0,1:T(8,128)(2,1)S(1)} async-done(((bf16[128,8,128]{2,0,1:T(8,128)(2,1)}), bf16[128,8,128]{2,0,1:T(8,128)(2,1)S(1)}, u32[]{:S(2)}, u32[]{:S(2)}) %all-to-all-start.2) | async-done | bytes 262176 | tf_op jit(solution)/shard_map/all_to_all | solution.py:57
  25.7 3.7 %all-to-all-start.1 = ((bf16[128,8,1024]{2,0,1:T(8,128)(2,1)}), bf16[128,8,1024]{2,0,1:T(8,128)(2,1)S(1)}, u32[]{:S(2)}, u32[]{:S(2)}) async-start(bf16[128,8,1024]{2,0,1:T(8,128)(2,1)} %bitcast.405), calls=%async_computation.1 | async-start | bytes 4194304 | tf_op jit(solution)/shard_map/all_to_all | solution.py:55
  30.4 3.5 %collective-permute-start = (bf16[2,1024,128]{2,1,0:T(8,128)(2,1)S(1)}, bf16[2,1024,128]{2,1,0:T(8,128)(2,1)S(1)}, u32[]{:S(2)}, u32[]{:S(2)}) collective-permute-start(bf16[2,1024,128]{2,1,0:T(8,128)(2,1)S(1)} %pad_maximum_fusion.1), channel_id=1, source_target_pairs={{0,16},{8,24},{16,32},{24,40},{32,48},{40,56},{48,64},{56,72},{64,... | collective-permute-start | bytes 1572872 | tf_op jit(solution)/shard_map/ppermute | solution.py:21
  33.9 1.9 collective-permute-start.1
  35.8 0.9 compare_and_fusion.6
  36.9 28.3 %collective-permute-done = bf16[2,1024,128]{2,1,0:T(8,128)(2,1)S(1)} collective-permute-done((bf16[2,1024,128]{2,1,0:T(8,128)(2,1)S(1)}, bf16[2,1024,128]{2,1,0:T(8,128)(2,1)S(1)}, u32[]{:S(2)}, u32[]{:S(2)}) %collective-permute-start) | collective-permute-done | bytes 524320 | tf_op jit(solution)/shard_map/ppermute | solution.py:21
  65.2 3.8 %collective-permute-done.1 = bf16[2,1024,128]{2,1,0:T(8,128)(2,1)S(1)} collective-permute-done((bf16[2,1024,128]{2,1,0:T(8,128)(2,1)S(1)}, bf16[2,1024,128]{2,1,0:T(8,128)(2,1)S(1)}, u32[]{:S(2)}, u32[]{:S(2)}) %collective-permute-start.1) | collective-permute-done | bytes 524320 | tf_op jit(solution)/shard_map/ppermute | solution.py:21
  69.1 1.3 slice_bitcast_fusion
  70.4 1.4 copy.65
  71.8 11.9 %all-to-all-done.1 = bf16[128,8,1024]{2,0,1:T(8,128)(2,1)S(1)} async-done(((bf16[128,8,1024]{2,0,1:T(8,128)(2,1)}), bf16[128,8,1024]{2,0,1:T(8,128)(2,1)S(1)}, u32[]{:S(2)}, u32[]{:S(2)}) %all-to-all-start.1) | async-done | bytes 2097184 | tf_op jit(solution)/shard_map/all_to_all | solution.py:55
  83.7 1.2 fusion.112
  85.8 2.5 %fusion.81 = f32[256,1,8,128]{3,0,2,1:T(8,128)} fusion(f32[256,1,8,256]{0,3,2,1:T(8,128)S(1)} %get-tuple-element.1194, f32[256,8]{0,1:T(8,128)S(1)} %get-tuple-element.1173, f32[256,8]{0,1:T(8,128)S(1)} %get-tuple-element.1171, bf16[1,1024,128]{2,1,0:T(8,128)(2,1)} %bitcast.433), kind=kOutput, calls=%fused_computation.120 | convolution fusion | flops 135528448 | bytes 3227648 | tf_op jit(solution)/shard_map/qgjk,kgd->qgjd/dot_general | solution.py:34
  88.3 1.6 copy.63
  89.9 19.6 %while.72 = (s32[]{:T(128)}, f32[256,1,8]{0,2,1:T(8,128)S(1)}, f32[256,1,8]{0,2,1:T(8,128)S(1)}, f32[256,1,8,128]{0,3,2,1:T(8,128)S(1)}, s32[256]{0:T(256)}, /*i...) while((s32[]{:T(128)}, f32[256,1,8]{0,2,1:T(8,128)S(1)}, ...), condition=%wide.region_5.6_spmd.clone, body=%wide.region_2.5_spmd.clone.sunk | while | flops 272833024 | bytes 9314543 | solution.py:98
  91.6 1.3 fusion.146
  95.5 1.3 fusion.146
  99.4 1.3 fusion.146
  103.3 1.3 fusion.146
  107.2 1.3 fusion.146
  109.6 1.0 copy.95
  110.6 1.1 copy.104
  111.8 1.3 fusion.116
  113.4 2.5 %fusion.83 = f32[256,1,8,128]{3,0,2,1:T(8,128)} fusion(f32[256,1,8,256]{0,3,2,1:T(8,128)S(1)} %get-tuple-element.1192, f32[256,8]{0,1:T(8,128)S(1)} %get-tuple-element.1176, f32[256,8]{0,1:T(8,128)S(1)} %get-tuple-element.1174, bf16[1,1024,128]{2,1,0:T(8,128)(2,1)} %bitcast.434), kind=kOutput, calls=%fused_computation.122 | convolution fusion | flops 135528448 | bytes 3227648 | tf_op jit(solution)/shard_map/qgjk,kgd->qgjd/dot_general | solution.py:34
  115.9 1.6 copy.69
  117.5 19.7 %while.73 = (s32[]{:T(128)}, f32[256,1,8]{0,2,1:T(8,128)S(1)}, f32[256,1,8]{0,2,1:T(8,128)S(1)}, f32[256,1,8,128]{0,3,2,1:T(8,128)S(1)}, s32[256]{0:T(256)}, /*i...) while((s32[]{:T(128)}, f32[256,1,8]{0,2,1:T(8,128)S(1)}, ...), condition=%wide.region_11.12_spmd.clone, body=%wide.region_8.11_spmd.clone.sunk | while | flops 272833024 | bytes 9314543 | solution.py:98
  118.3 0.8 compare_and_fusion.13
  119.1 1.3 fusion.152
  122.3 0.8 compare_and_fusion.13
  123.1 1.3 fusion.152
  126.2 0.8 compare_and_fusion.13
  127.0 1.3 fusion.152
  130.9 1.3 fusion.152
  134.1 0.8 compare_and_fusion.13
  134.9 1.3 fusion.152
  137.3 1.0 copy.96
  138.4 1.1 copy.106
  140.3 2.5 %fusion.85 = f32[256,1,8,128]{3,0,2,1:T(8,128)} fusion(f32[256,1,8,256]{0,3,2,1:T(8,128)S(1)} %get-tuple-element.1190, f32[256,8]{0,1:T(8,128)S(1)} %get-tuple-element.1179, f32[256,8]{0,1:T(8,128)S(1)} %get-tuple-element.1177, bf16[1,1024,128]{2,1,0:T(8,128)(2,1)} %bitcast.435), kind=kOutput, calls=%fused_computation.124 | convolution fusion | flops 135528448 | bytes 3227648 | tf_op jit(solution)/shard_map/qgjk,kgd->qgjd/dot_general | solution.py:34
  142.8 1.6 copy.75
  144.5 16.4 %while.74 = (s32[]{:T(128)}, f32[256,1,8]{0,2,1:T(8,128)S(1)}, f32[256,1,8]{0,2,1:T(8,128)S(1)}, f32[256,1,8,128]{0,3,2,1:T(8,128)S(1)}, s32[256]{0:T(256)S(1)},...) while((s32[]{:T(128)}, f32[256,1,8]{0,2,1:T(8,128)S(1)}, ...), condition=%wide.region_17.18_spmd.clone, body=%wide.region_14.17_spmd.clone.sunk | while | flops 272833024 | bytes 9314543 | solution.py:98
  145.4 1.3 fusion.158
  148.7 1.3 fusion.158
  152.0 1.3 fusion.158
  155.2 1.3 fusion.158
  158.5 1.3 fusion.158
  161.0 1.0 copy.97
  162.0 1.1 copy.108
  163.9 2.5 %fusion.87 = f32[256,1,8,128]{3,0,2,1:T(8,128)} fusion(f32[256,1,8,256]{0,3,2,1:T(8,128)S(1)} %get-tuple-element.1188, f32[256,8]{0,1:T(8,128)S(1)} %get-tuple-element.1182, f32[256,8]{0,1:T(8,128)S(1)} %get-tuple-element.1180, bf16[1,1024,128]{2,1,0:T(8,128)(2,1)} %bitcast.436), kind=kOutput, calls=%fused_computation.126 | convolution fusion | flops 135528448 | bytes 3227648 | tf_op jit(solution)/shard_map/qgjk,kgd->qgjd/dot_general | solution.py:34
  166.4 1.6 copy.81
  168.1 16.6 %while.75 = (s32[]{:T(128)}, f32[256,1,8]{0,2,1:T(8,128)S(1)}, f32[256,1,8]{0,2,1:T(8,128)S(1)}, f32[256,1,8,128]{0,3,2,1:T(8,128)S(1)}, s32[256]{0:T(256)S(1)},...) while((s32[]{:T(128)}, f32[256,1,8]{0,2,1:T(8,128)S(1)}, ...), condition=%wide.region_23.24_spmd.clone, body=%wide.region_20.23_spmd.clone.sunk | while | flops 272833024 | bytes 9314543 | solution.py:98
  169.2 1.3 fusion.164
  172.5 1.3 fusion.164
  175.8 1.3 fusion.164
  179.1 1.3 fusion.164
  182.3 1.3 fusion.164
  185.9 1.2 pad_maximum_fusion
  187.1 29.6 %all_to_all.67 = bf16[8,128,1024]{2,1,0:T(8,128)(2,1)S(1)} all-to-all(bf16[8,128,1024]{2,1,0:T(8,128)(2,1)S(1)} %bitcast.406), channel_id=1, replica_groups=mesh['ctx'=64,'head'=8] {'head'}, dimensions={0} | all-to-all | bytes 4194304 | tf_op jit(solution)/shard_map/all_to_all | solution.py:104
  216.8 2.4 %copy.85 = bf16[128,8,1024]{0,2,1:T(8,128)(2,1)} copy(bf16[128,8,1024]{2,0,1:T(8,128)(2,1)S(1)} %bitcast.407) | data formatting | bytes 4194304 | tf_op jit(solution)/shard_map/all_to_all | solution.py:104
  219.1 4.1 %copy.86 = bf16[128,8192]{1,0:T(8,128)(2,1)} copy(bf16[128,8192]{0,1:T(8,128)(2,1)} %bitcast.408) | data formatting | bytes 4194304 | tf_op jit(solution)/shard_map/all_to_all | solution.py:104
  (222 shorter events, 47.6 us)
Async XLA Ops:
  0.0 1.0 copy-start
  0.0 18.5 %copy-start.2 = (bf16[128,8192]{1,0:T(8,128)(2,1)S(1)}, bf16[128,8192]{1,0:T(8,128)(2,1)}, u32[]{:S(2)}) copy-start(bf16[128,8192]{1,0:T(8,128)(2,1)} %param.12) | copy-start | bytes 6291460
  1.7 13.4 %all-to-all-start = ((bf16[128,8,128]{2,0,1:T(8,128)(2,1)}), bf16[128,8,128]{2,0,1:T(8,128)(2,1)S(1)}, u32[]{:S(2)}, u32[]{:S(2)}) async-start(bf16[128,8,128]{2,0,1:T(8,128)(2,1)} %copy_bitcast_fusion.2), calls=%async_computation | async-start | bytes 524288 | tf_op jit(solution)/shard_map/all_to_all | solution.py:56
  15.1 10.6 %all-to-all-start.2 = ((bf16[128,8,128]{2,0,1:T(8,128)(2,1)}), bf16[128,8,128]{2,0,1:T(8,128)(2,1)S(1)}, u32[]{:S(2)}, u32[]{:S(2)}) async-start(bf16[128,8,128]{2,0,1:T(8,128)(2,1)} %copy_bitcast_fusion.1), calls=%async_computation.2 | async-start | bytes 524288 | tf_op jit(solution)/shard_map/all_to_all | solution.py:57
  25.7 43.3 %copy-start.1 = (bf16[128,8,128]{2,0,1:T(8,128)(2,1)}, bf16[128,8,128]{2,0,1:T(8,128)(2,1)S(1)}, u32[]{:S(2)}) copy-start(bf16[128,8,128]{2,0,1:T(8,128)(2,1)S(1)} %all-to-all-done.2) | copy-start | bytes 786436
  25.7 3.8 %copy-start.5 = (s32[65536]{0:T(1024)S(1)}, s32[65536]{0:T(1024)}, u32[]{:S(2)}) copy-start(s32[65536]{0:T(1024)} %param.15) | copy-start | bytes 786436
  25.7 57.9 %all-to-all-start.1 = ((bf16[128,8,1024]{2,0,1:T(8,128)(2,1)}), bf16[128,8,1024]{2,0,1:T(8,128)(2,1)S(1)}, u32[]{:S(2)}, u32[]{:S(2)}) async-start(bf16[128,8,1024]{2,0,1:T(8,128)(2,1)} %bitcast.405), calls=%async_computation.1 | async-start | bytes 4194304 | tf_op jit(solution)/shard_map/all_to_all | solution.py:55
  30.3 34.9 %copy-start.11 = (s32[256]{0:T(256)}, s32[256]{0:T(256)S(1)}, u32[]{:S(2)}) copy-start(s32[256]{0:T(256)S(1)} %get-tuple-element.1615) | copy-start | bytes 3076
  30.3 34.9 %copy-start.12 = (s32[256]{0:T(256)}, s32[256]{0:T(256)S(1)}, u32[]{:S(2)}) copy-start(s32[256]{0:T(256)S(1)} %get-tuple-element.1663) | copy-start | bytes 3076
  30.3 38.8 %copy-start.7 = (s32[256]{0:T(256)}, s32[256]{0:T(256)S(1)}, u32[]{:S(2)}) copy-start(s32[256]{0:T(256)S(1)} %get-tuple-element.1519) | copy-start | bytes 3076
  30.3 38.8 %copy-start.9 = (s32[256]{0:T(256)}, s32[256]{0:T(256)S(1)}, u32[]{:S(2)}) copy-start(s32[256]{0:T(256)S(1)} %get-tuple-element.1567) | copy-start | bytes 3076
  30.4 34.8 %collective-permute-start = (bf16[2,1024,128]{2,1,0:T(8,128)(2,1)S(1)}, bf16[2,1024,128]{2,1,0:T(8,128)(2,1)S(1)}, u32[]{:S(2)}, u32[]{:S(2)}) collective-permute-start(bf16[2,1024,128]{2,1,0:T(8,128)(2,1)S(1)} %pad_maximum_fusion.1), channel_id=1, source_target_pairs={{0,16},{8,24},{16,32},{24,40},{32,48},{40,56},{48,64},{56,72},{64,... | collective-permute-start | bytes 1572872 | tf_op jit(solution)/shard_map/ppermute | solution.py:21
  33.9 35.1 %collective-permute-start.1 = (bf16[2,1024,128]{2,1,0:T(8,128)(2,1)S(1)}, bf16[2,1024,128]{2,1,0:T(8,128)(2,1)S(1)}, u32[]{:S(2)}, u32[]{:S(2)}) collective-permute-start(bf16[2,1024,128]{2,1,0:T(8,128)(2,1)S(1)} %pad_maximum_fusion.1), channel_id=1, source_target_pairs={{0,8},{8,16},{16,24},{24,32},{32,40},{40,48},{48,56},{56,64},{64,7... | collective-permute-start | bytes 1572872 | tf_op jit(solution)/shard_map/ppermute | solution.py:21
  83.7 1.3 copy-start.6
  142.8 1.7 copy-start.10
  166.4 1.7 copy-start.8
  184.7 1.0 copy-start.3
  184.7 1.2 copy-start.4
where the time goes:
time: 226 us; the launch traced here: 223 us
  waiting for transfers between devices  55.2 us (24%)
  matrix products  52.6 us (23%)
  local copies, waits for them, and re-layouts  45.3 us (20%)
  blocking collectives  29.6 us (13%)
  other arithmetic  19.5 us (9%)
  starting transfers between devices  18.7 us (8%)
    ppermute x2, waiting for transfers between devices, from_behind(): lax.ppermute(value, axis, [(source, source + steps) for source in range(l...  32.1 us
    all_to_all x1, blocking collectives, shards(): lax.all_to_all(local_out, 'head', split_axis=0, concat_axis=1, tiled=True)  29.6 us
    dot_general x24, matrix products, attend_tile(): jnp.einsum('qgjd,kgd->qgjk', query_block, key_tile, preferred_element_typ...  28.9 us
    dot_general x24, matrix products, attend_tile(): jnp.einsum('qgjk,kgd->qgjd', weights.astype(jnp.bfloat16), value_tile, pr...  23.6 us
    dynamic_slice x21, local copies, waits for them, and re-layouts, visit(): tile_ids = lax.dynamic_slice_in_dim(window_ids, start, BLOCK)  15.2 us
    unnamed x39, local copies, waits for them, and re-layouts  13.2 us
    all_to_all x1, waiting for transfers between devices, shards(): lax.all_to_all(queries, 'head', split_axis=1, concat_axis=0, tiled=True)  11.9 us
    and x22, other arithmetic, visit(): (block_ids[:, None] == tile_ids[None, :]) & (key_pos[None, :] <= query_po...  10.1 us
  transfers between devices with their start and end apart: 5, of which 5 were waited for; matrix products, arithmetic and copies ran while one was open for 4% of the time, Pallas kernels for 0%

commit v1 on v0

v1 whole, which is shorter than its diff:
```python
import functools

import jax
import jax.numpy as jnp
from jax import lax
from jax.experimental import pallas as pl
from jax.experimental.pallas import tpu as pltpu
from jax.sharding import PartitionSpec as P

HD = 128
QH = 64
KVH = 8
BLOCK = 256
DOC_BLOCKS = 5
QBLK_DEV = 4
PREV = 2


floor_score = -1e30


def from_behind(value, axis, steps):
    count = lax.axis_size(axis)
    leading, last = (max(0, -steps), min(count, count - steps))
    return lax.ppermute(value, axis, [(source, source + steps) for source in range(leading, last)])


def key_window(paired):
    pieces = []
    for offset in range(1, PREV + 1):
        pieces.append(from_behind(paired, "ctx", offset))
    return jnp.concatenate(pieces[::-1] + [paired], axis=1)


def attend_kernel(nback_ref, q_ref, k_ref, v_ref, qid_ref, kid_ref, o_ref, m_scr, l_scr, acc_scr, *, heads):
    qb = pl.program_id(0)
    step = pl.program_id(1)
    last = pl.num_programs(1) - 1

    @pl.when(step == 0)
    def _init():
        m_scr[...] = jnp.full(m_scr.shape, floor_score, jnp.float32)
        l_scr[...] = jnp.zeros(l_scr.shape, jnp.float32)
        acc_scr[...] = jnp.zeros(acc_scr.shape, jnp.float32)

    @pl.when(step <= nback_ref[qb])
    def _compute():
        allowed = qid_ref[...] == kid_ref[...]
        rows = lax.broadcasted_iota(jnp.int32, (BLOCK, BLOCK), 0)
        cols = lax.broadcasted_iota(jnp.int32, (BLOCK, BLOCK), 1)
        allowed = allowed & ((cols <= rows) | (step > 0))
        k = k_ref[...]
        v = v_ref[...]
        for j in range(heads):
            q = q_ref[:, j * HD:(j + 1) * HD]
            s = lax.dot_general(q, k, (((1,), (1,)), ((), ())), preferred_element_type=jnp.float32)
            s = s * HD ** (-0.5)
            s = jnp.where(allowed, s, floor_score)
            m_old = m_scr[j]
            m_new = jnp.maximum(m_old, jnp.max(s, axis=-1, keepdims=True))
            factor = jnp.exp(m_old - m_new)
            p = jnp.exp(s - m_new)
            l_scr[j] = l_scr[j] * factor + jnp.sum(p, axis=-1, keepdims=True)
            acc_scr[j] = acc_scr[j] * factor + jnp.dot(
                p.astype(jnp.bfloat16), v, preferred_element_type=jnp.float32)
            m_scr[j] = m_new

    @pl.when(step == last)
    def _finish():
        for j in range(heads):
            o_ref[:, j * HD:(j + 1) * HD] = (acc_scr[j] / l_scr[j]).astype(o_ref.dtype)


def attend(nback, queries, keys, values, qids, kids):
    rows, width = queries.shape
    heads = width // HD
    n_q = rows // BLOCK
    base = keys.shape[0] // BLOCK - n_q
    n_steps = DOC_BLOCKS + 1

    def kv_map(qb, step, nback_ref):
        return (base + qb - jnp.minimum(step, nback_ref[qb]), 0)

    def kid_map(qb, step, nback_ref):
        return (0, base + qb - jnp.minimum(step, nback_ref[qb]))

    grid_spec = pltpu.PrefetchScalarGridSpec(
        num_scalar_prefetch=1,
        grid=(n_q, n_steps),
        in_specs=[
            pl.BlockSpec((BLOCK, width), lambda qb, step, nb: (qb, 0)),
            pl.BlockSpec((BLOCK, HD), kv_map),
            pl.BlockSpec((BLOCK, HD), kv_map),
            pl.BlockSpec((BLOCK, 1), lambda qb, step, nb: (qb, 0)),
            pl.BlockSpec((1, BLOCK), kid_map),
        ],
        out_specs=pl.BlockSpec((BLOCK, width), lambda qb, step, nb: (qb, 0)),
        scratch_shapes=[
            pltpu.VMEM((heads, BLOCK, 1), jnp.float32),
            pltpu.VMEM((heads, BLOCK, 1), jnp.float32),
            pltpu.VMEM((heads, BLOCK, HD), jnp.float32),
        ],
    )
    flops = 4 * rows * keys.shape[0] // 2 * HD * heads
    return pl.pallas_call(
        functools.partial(attend_kernel, heads=heads),
        out_shape=jax.ShapeDtypeStruct((rows, width), queries.dtype),
        grid_spec=grid_spec,
        compiler_params=pltpu.CompilerParams(dimension_semantics=("arbitrary", "arbitrary")),
        cost_estimate=pl.CostEstimate(
            flops=flops, transcendentals=flops // (2 * HD), bytes_accessed=4 * rows * width),
    )(nback, queries, keys, values, qids, kids)


def shards(queries, keys, values, doc_ids):
    range_rows = QBLK_DEV * BLOCK
    ctx_pos = lax.axis_index("ctx")
    local_queries, local_keys, local_values = (
        lax.all_to_all(queries, "head", split_axis=1, concat_axis=0, tiled=True),
        lax.all_to_all(keys, "head", split_axis=1, concat_axis=0, tiled=True),
        lax.all_to_all(values, "head", split_axis=1, concat_axis=0, tiled=True),
    )
    window = key_window(jnp.stack([local_keys, local_values]))
    padded_ids = jnp.concatenate([jnp.full((PREV * range_rows,), -1, jnp.int32), doc_ids])
    window_ids = lax.dynamic_slice_in_dim(padded_ids, ctx_pos * range_rows, (PREV + 1) * range_rows)
    range_ids = lax.dynamic_slice_in_dim(doc_ids, ctx_pos * range_rows, range_rows)
    tile_last = window_ids.reshape(-1, BLOCK)[:, BLOCK - 1]
    first_q = range_ids.reshape(-1, BLOCK)[:, 0]
    n_q = range_rows // BLOCK
    base = PREV * n_q
    counts = []
    for qb in range(n_q):
        back = tile_last[base + qb - DOC_BLOCKS:base + qb]
        counts.append(jnp.sum((back == first_q[qb]).astype(jnp.int32)))
    nback = jnp.stack(counts)
    local_out = attend(
        nback, local_queries, window[0], window[1],
        range_ids.reshape(range_rows, 1), window_ids.reshape(1, -1))
    return lax.all_to_all(local_out, "head", split_axis=0, concat_axis=1, tiled=True)


def solution(mesh):
    in_specs = (P(("ctx", "head"), None), P(("ctx", "head"), None), P(("ctx", "head"), None), P())
    out_specs = P(("ctx", "head"), None)
    return jax.shard_map(shards, mesh=mesh, in_specs=in_specs, out_specs=out_specs, check_vma=False)
```

time: 226 us -> 186 us (0.82)
  the two profiles are of different devices: /device:TPU:128 before, /device:TPU:256 now
where the time goes in v1:
time: 186 us; the launch traced here: 185 us
  Pallas kernels  65.5 us (35%)
  waiting for transfers between devices  47.9 us (26%)
  blocking collectives  33.8 us (18%)
  starting transfers between devices  17.6 us (9%)
  local copies, waits for them, and re-layouts  12.1 us (7%)
  other arithmetic  7.78 us (4%)
    pallas_call x1, Pallas kernels, attend(): pl.pallas_call(functools.partial(attend_kernel, heads=heads), out_shape=j...  65.5 us
    all_to_all x1, blocking collectives, shards(): lax.all_to_all(local_out, 'head', split_axis=0, concat_axis=1, tiled=True)  33.8 us
    ppermute x2, waiting for transfers between devices, from_behind(): lax.ppermute(value, axis, [(source, source + steps) for source in range(l...  22.5 us
    all_to_all x1, waiting for transfers between devices, shards(): lax.all_to_all(queries, 'head', split_axis=1, concat_axis=0, tiled=True)  14.2 us
    all_to_all x1, waiting for transfers between devices, shards(): lax.all_to_all(keys, 'head', split_axis=1, concat_axis=0, tiled=True)  5.65 us
    all_to_all x1, waiting for transfers between devices, shards(): lax.all_to_all(values, 'head', split_axis=1, concat_axis=0, tiled=True)  5.59 us
    ppermute x2, starting transfers between devices, from_behind(): lax.ppermute(value, axis, [(source, source + steps) for source in range(l...  5.41 us
    all_to_all x1, starting transfers between devices, shards(): lax.all_to_all(values, 'head', split_axis=1, concat_axis=0, tiled=True)  5.21 us
  transfers between devices with their start and end apart: 5, of which 5 were waited for; matrix products, arithmetic and copies ran while one was open for 8% of the time, Pallas kernels for 0%

profile of v1, /device:TPU:256, one launch (start us, length us, event | category | flops | bytes accessed | tf_op | source)
XLA Modules:
  0.0 184.9 jit_solution(12519715804460549959)
XLA Ops:
  0.0 0.0 copy-start
  0.0 0.0 copy-start.1
  0.0 0.9 copy-done
  1.0 0.8 copy_bitcast_fusion.1
  1.7 5.2 %all-to-all-start.2 = ((bf16[128,8,128]{2,0,1:T(8,128)(2,1)}), bf16[128,8,128]{2,0,1:T(8,128)(2,1)S(1)}, u32[]{:S(2)}, u32[]{:S(2)}) async-start(bf16[128,8,128]{2,0,1:T(8,128)(2,1)} %copy_bitcast_fusion.1), calls=%async_computation.2 | async-start | bytes 524288 | tf_op jit(solution)/shard_map/all_to_all | solution.py:121
  6.9 1.7 copy_bitcast_fusion.2
  8.6 5.6 %all-to-all-done.2 = bf16[128,8,128]{2,0,1:T(8,128)(2,1)S(1)} async-done(((bf16[128,8,128]{2,0,1:T(8,128)(2,1)}), bf16[128,8,128]{2,0,1:T(8,128)(2,1)S(1)}, u32[]{:S(2)}, u32[]{:S(2)}) %all-to-all-start.2) | async-done | bytes 262176 | tf_op jit(solution)/shard_map/all_to_all | solution.py:121
  14.2 3.4 %all-to-all-start.1 = ((bf16[128,8,128]{2,0,1:T(8,128)(2,1)}), bf16[128,8,128]{2,0,1:T(8,128)(2,1)S(1)}, u32[]{:S(2)}, u32[]{:S(2)}) async-start(bf16[128,8,128]{2,0,1:T(8,128)(2,1)} %copy_bitcast_fusion.2), calls=%async_computation.1 | async-start | bytes 524288 | tf_op jit(solution)/shard_map/all_to_all | solution.py:120
  17.6 0.0 copy-done.1
  17.6 1.6 copy.39
  19.2 5.6 %all-to-all-done.1 = bf16[128,8,128]{2,0,1:T(8,128)(2,1)S(1)} async-done(((bf16[128,8,128]{2,0,1:T(8,128)(2,1)}), bf16[128,8,128]{2,0,1:T(8,128)(2,1)S(1)}, u32[]{:S(2)}, u32[]{:S(2)}) %all-to-all-start.1) | async-done | bytes 262176 | tf_op jit(solution)/shard_map/all_to_all | solution.py:120
  24.8 3.6 %all-to-all-start = ((bf16[128,8,1024]{2,0,1:T(8,128)(2,1)}), bf16[128,8,1024]{2,0,1:T(8,128)(2,1)S(1)}, u32[]{:S(2)}, u32[]{:S(2)}) async-start(bf16[128,8,1024]{2,0,1:T(8,128)(2,1)} %bitcast.40), calls=%async_computation | async-start | bytes 4194304 | tf_op jit(solution)/shard_map/all_to_all | solution.py:119
  28.4 0.1 pad_maximum_fusion
  28.5 1.9 %collective-permute-start.1 = (bf16[2,1024,128]{2,1,0:T(8,128)(2,1)S(1)}, bf16[2,1024,128]{2,1,0:T(8,128)(2,1)}, u32[]{:S(2)}, u32[]{:S(2)}) collective-permute-start(bf16[2,1024,128]{2,1,0:T(8,128)(2,1)S(1)} %pad_maximum_fusion), channel_id=1, source_target_pairs={{0,8},{8,16},{16,24},{24,32},{32,40},{40,48},{48,56},{56,64},{64,7... | collective-permute-start | bytes 1572872 | tf_op jit(solution)/shard_map/ppermute | solution.py:25
  30.4 3.5 %collective-permute-start = (bf16[2,1024,128]{2,1,0:T(8,128)(2,1)S(1)}, bf16[2,1024,128]{2,1,0:T(8,128)(2,1)}, u32[]{:S(2)}, u32[]{:S(2)}) collective-permute-start(bf16[2,1024,128]{2,1,0:T(8,128)(2,1)S(1)} %pad_maximum_fusion), channel_id=1, source_target_pairs={{0,16},{8,24},{16,32},{24,40},{32,48},{40,56},{48,64},{56,72},{64,... | collective-permute-start | bytes 1572872 | tf_op jit(solution)/shard_map/ppermute | solution.py:25
  33.9 0.7 pad_dynamic-slice_fusion
  34.7 0.0 copy-start.3
  34.7 0.7 dynamic_slice.7
  35.4 1.0 copy.26.qid_ref
  36.4 0.6 fusion
  37.0 3.3 %convert_reduce_fusion.3 = (s32[]{:T(128)}, s32[]{:T(128)}, s32[]{:T(128)}, s32[]{:T(128)}) fusion(s32[12,256]{1,0:T(8,128)S(1)} %reshape.50, s32[]{:T(128)} %bitcast, s32[]{:T(128)} %bitcast.6, s32[]{:T(128)} %bitcast.4, s32[]{:T(128)} %bitcast.2), kind=kLoop, calls=%fused_computation.15 | loop fusion | flops 56 | bytes 112 | tf_op jit(solution)/shard_map/reduce_sum | solution.py:134
  40.2 3.2 %pad_add_fusion.nback_ref = s32[4]{0:T(128)} fusion(s32[1]{0:T(128)} %bitcast.7, s32[1]{0:T(128)} %bitcast.5, s32[1]{0:T(128)} %bitcast.3, s32[1]{0:T(128)} %bitcast.1), kind=kLoop, calls=%fused_computation.16 | loop fusion | flops 12 | bytes 32 | tf_op jit(solution)/shard_map/stack | solution.py:135
  43.4 13.1 %collective-permute-done.1 = bf16[2,1024,128]{2,1,0:T(8,128)(2,1)} collective-permute-done((bf16[2,1024,128]{2,1,0:T(8,128)(2,1)S(1)}, bf16[2,1024,128]{2,1,0:T(8,128)(2,1)}, u32[]{:S(2)}, u32[]{:S(2)}) %collective-permute-start.1) | collective-permute-done | bytes 524320 | tf_op jit(solution)/shard_map/ppermute | solution.py:25
  56.5 9.4 %collective-permute-done = bf16[2,1024,128]{2,1,0:T(8,128)(2,1)} collective-permute-done((bf16[2,1024,128]{2,1,0:T(8,128)(2,1)S(1)}, bf16[2,1024,128]{2,1,0:T(8,128)(2,1)}, u32[]{:S(2)}, u32[]{:S(2)}) %collective-permute-start) | collective-permute-done | bytes 524320 | tf_op jit(solution)/shard_map/ppermute | solution.py:25
  65.9 1.3 maximum_maximum_fusion
  67.2 1.3 slice_bitcast_fusion
  68.4 0.0 copy-done.3
  68.4 14.2 %all-to-all-done = bf16[128,8,1024]{2,0,1:T(8,128)(2,1)S(1)} async-done(((bf16[128,8,1024]{2,0,1:T(8,128)(2,1)}), bf16[128,8,1024]{2,0,1:T(8,128)(2,1)S(1)}, u32[]{:S(2)}, u32[]{:S(2)}) %all-to-all-start) | async-done | bytes 2097184 | tf_op jit(solution)/shard_map/all_to_all | solution.py:119
  82.6 0.0 copy-start.2
  82.6 1.3 copy-done.2
  84.0 65.5 %shard_map.46 = bf16[1024,1024]{1,0:T(8,128)(2,1)} custom-call(s32[4]{0:T(128)} %pad_add_fusion.nback_ref, bf16[1024,1024]{1,0:T(8,128)(2,1)} %bitcast.47, bf16[3072,128]{1,0:T(8,128)(2,1)} %get-tuple-element.10.k_ref, bf16[3072,128]{1,0:T(8,128)(2,1)} %get-tuple-element.9.v_ref, s32[1024,1]{1,0:T(8,128)} %copy.26.qid_ref, s32[1,3072]{1,0:T(1,128)} %bitcast.49), custom_call_target="tpu_custom_call" | custom-call | flops 6442450944 | bytes 4194304 | tf_op jit(solution)/shard_map/pallas_call | solution.py:105
  149.5 33.8 %all_to_all.70 = bf16[8,128,1024]{2,1,0:T(8,128)(2,1)S(1)} all-to-all(bf16[8,128,1024]{2,1,0:T(8,128)(2,1)} %bitcast.48), channel_id=1, replica_groups=mesh['ctx'=64,'head'=8] {'head'}, dimensions={0} | all-to-all | bytes 4194304 | tf_op jit(solution)/shard_map/all_to_all | solution.py:139
  183.3 1.6 copy.35
  (2 shorter events, 0.0 us)
Async XLA Ops:
  0.0 1.0 copy-start
  0.0 17.6 %copy-start.1 = (bf16[128,8192]{1,0:T(8,128)(2,1)S(1)}, bf16[128,8192]{1,0:T(8,128)(2,1)}, u32[]{:S(2)}) copy-start(bf16[128,8192]{1,0:T(8,128)(2,1)} %param.4) | copy-start | bytes 6291460
  1.7 12.5 %all-to-all-start.2 = ((bf16[128,8,128]{2,0,1:T(8,128)(2,1)}), bf16[128,8,128]{2,0,1:T(8,128)(2,1)S(1)}, u32[]{:S(2)}, u32[]{:S(2)}) async-start(bf16[128,8,128]{2,0,1:T(8,128)(2,1)} %copy_bitcast_fusion.1), calls=%async_computation.2 | async-start | bytes 524288 | tf_op jit(solution)/shard_map/all_to_all | solution.py:121
  14.2 10.6 %all-to-all-start.1 = ((bf16[128,8,128]{2,0,1:T(8,128)(2,1)}), bf16[128,8,128]{2,0,1:T(8,128)(2,1)S(1)}, u32[]{:S(2)}, u32[]{:S(2)}) async-start(bf16[128,8,128]{2,0,1:T(8,128)(2,1)} %copy_bitcast_fusion.2), calls=%async_computation.1 | async-start | bytes 524288 | tf_op jit(solution)/shard_map/all_to_all | solution.py:120
  24.8 57.8 %all-to-all-start = ((bf16[128,8,1024]{2,0,1:T(8,128)(2,1)}), bf16[128,8,1024]{2,0,1:T(8,128)(2,1)S(1)}, u32[]{:S(2)}, u32[]{:S(2)}) async-start(bf16[128,8,1024]{2,0,1:T(8,128)(2,1)} %bitcast.40), calls=%async_computation | async-start | bytes 4194304 | tf_op jit(solution)/shard_map/all_to_all | solution.py:119
  28.5 28.0 %collective-permute-start.1 = (bf16[2,1024,128]{2,1,0:T(8,128)(2,1)S(1)}, bf16[2,1024,128]{2,1,0:T(8,128)(2,1)}, u32[]{:S(2)}, u32[]{:S(2)}) collective-permute-start(bf16[2,1024,128]{2,1,0:T(8,128)(2,1)S(1)} %pad_maximum_fusion), channel_id=1, source_target_pairs={{0,8},{8,16},{16,24},{24,32},{32,40},{40,48},{48,56},{56,64},{64,7... | collective-permute-start | bytes 1572872 | tf_op jit(solution)/shard_map/ppermute | solution.py:25
  30.4 35.4 %collective-permute-start = (bf16[2,1024,128]{2,1,0:T(8,128)(2,1)S(1)}, bf16[2,1024,128]{2,1,0:T(8,128)(2,1)}, u32[]{:S(2)}, u32[]{:S(2)}) collective-permute-start(bf16[2,1024,128]{2,1,0:T(8,128)(2,1)S(1)} %pad_maximum_fusion), channel_id=1, source_target_pairs={{0,16},{8,24},{16,32},{24,40},{32,48},{40,56},{48,64},{56,72},{64,... | collective-permute-start | bytes 1572872 | tf_op jit(solution)/shard_map/ppermute | solution.py:25
  34.7 33.8 %copy-start.3 = (s32[3072]{0:T(1024)}, s32[3072]{0:T(1024)S(1)}, u32[]{:S(2)}) copy-start(s32[3072]{0:T(1024)S(1)} %pad_dynamic-slice_fusion) | copy-start | bytes 36868
  82.6 1.3 copy-start.2

commit v2 on v1

--- a/solution.py
+++ b/solution.py
@@ -43,27 +43,32 @@
         l_scr[...] = jnp.zeros(l_scr.shape, jnp.float32)
         acc_scr[...] = jnp.zeros(acc_scr.shape, jnp.float32)
 
-    @pl.when(step <= nback_ref[qb])
-    def _compute():
-        allowed = qid_ref[...] == kid_ref[...]
-        rows = lax.broadcasted_iota(jnp.int32, (BLOCK, BLOCK), 0)
-        cols = lax.broadcasted_iota(jnp.int32, (BLOCK, BLOCK), 1)
-        allowed = allowed & ((cols <= rows) | (step > 0))
+    def body(masked):
         k = k_ref[...]
         v = v_ref[...]
+        if masked:
+            allowed = qid_ref[...] == kid_ref[...]
+            rows = lax.broadcasted_iota(jnp.int32, (BLOCK, BLOCK), 0)
+            cols = lax.broadcasted_iota(jnp.int32, (BLOCK, BLOCK), 1)
+            allowed = allowed & ((cols <= rows) | (step > 0))
         for j in range(heads):
             q = q_ref[:, j * HD:(j + 1) * HD]
             s = lax.dot_general(q, k, (((1,), (1,)), ((), ())), preferred_element_type=jnp.float32)
             s = s * HD ** (-0.5)
-            s = jnp.where(allowed, s, floor_score)
+            if masked:
+                s = jnp.where(allowed, s, floor_score)
             m_old = m_scr[j]
             m_new = jnp.maximum(m_old, jnp.max(s, axis=-1, keepdims=True))
             factor = jnp.exp(m_old - m_new)
-            p = jnp.exp(s - m_new)
+            p = jnp.exp(s - jnp.tile(m_new, (1, BLOCK // 128)))
             l_scr[j] = l_scr[j] * factor + jnp.sum(p, axis=-1, keepdims=True)
             acc_scr[j] = acc_scr[j] * factor + jnp.dot(
                 p.astype(jnp.bfloat16), v, preferred_element_type=jnp.float32)
             m_scr[j] = m_new
+
+    @pl.when(step <= nback_ref[qb])
+    def _compute():
+        body(True)
 
     @pl.when(step == last)
     def _finish():
@@ -96,8 +101,8 @@
         ],
         out_specs=pl.BlockSpec((BLOCK, width), lambda qb, step, nb: (qb, 0)),
         scratch_shapes=[
-            pltpu.VMEM((heads, BLOCK, 1), jnp.float32),
-            pltpu.VMEM((heads, BLOCK, 1), jnp.float32),
+            pltpu.VMEM((heads, BLOCK, 128), jnp.float32),
+            pltpu.VMEM((heads, BLOCK, 128), jnp.float32),
             pltpu.VMEM((heads, BLOCK, HD), jnp.float32),
         ],
     )
@@ -114,27 +119,33 @@
 
 def shards(queries, keys, values, doc_ids):
     range_rows = QBLK_DEV * BLOCK
+    rows = queries.shape[0]
+    heads_axis = lax.axis_size("head")
     ctx_pos = lax.axis_index("ctx")
-    local_queries, local_keys, local_values = (
-        lax.all_to_all(queries, "head", split_axis=1, concat_axis=0, tiled=True),
-        lax.all_to_all(keys, "head", split_axis=1, concat_axis=0, tiled=True),
-        lax.all_to_all(values, "head", split_axis=1, concat_axis=0, tiled=True),
-    )
-    window = key_window(jnp.stack([local_keys, local_values]))
-    padded_ids = jnp.concatenate([jnp.full((PREV * range_rows,), -1, jnp.int32), doc_ids])
-    window_ids = lax.dynamic_slice_in_dim(padded_ids, ctx_pos * range_rows, (PREV + 1) * range_rows)
+    paired = jnp.concatenate(
+        [keys.reshape(rows, heads_axis, -1), values.reshape(rows, heads_axis, -1)], axis=2)
+    local_pair = lax.all_to_all(paired, "head", split_axis=1, concat_axis=0, tiled=True)
+    local_queries = lax.all_to_all(queries, "head", split_axis=1, concat_axis=0, tiled=True)
+    local_pair = local_pair.reshape(range_rows, 2 * HD)
+    prev1 = from_behind(local_pair, "ctx", 1)
+    prev2 = from_behind(local_pair[range_rows - BLOCK:], "ctx", 2)
+    window = jnp.concatenate([prev2, prev1, local_pair], axis=0)
+    reach = BLOCK + range_rows
+    padded_ids = jnp.concatenate([jnp.full((reach,), -1, jnp.int32), doc_ids])
+    window_ids = lax.dynamic_slice_in_dim(padded_ids, ctx_pos * range_rows, reach + range_rows)
     range_ids = lax.dynamic_slice_in_dim(doc_ids, ctx_pos * range_rows, range_rows)
     tile_last = window_ids.reshape(-1, BLOCK)[:, BLOCK - 1]
     first_q = range_ids.reshape(-1, BLOCK)[:, 0]
     n_q = range_rows // BLOCK
-    base = PREV * n_q
+    base = reach // BLOCK
     counts = []
     for qb in range(n_q):
-        back = tile_last[base + qb - DOC_BLOCKS:base + qb]
+        lo = max(0, base + qb - DOC_BLOCKS)
+        back = tile_last[lo:base + qb]
         counts.append(jnp.sum((back == first_q[qb]).astype(jnp.int32)))
     nback = jnp.stack(counts)
     local_out = attend(
-        nback, local_queries, window[0], window[1],
+        nback, local_queries, window[:, :HD], window[:, HD:],
         range_ids.reshape(range_rows, 1), window_ids.reshape(1, -1))
     return lax.all_to_all(local_out, "head", split_axis=0, concat_axis=1, tiled=True)
 

time: 186 us -> 129 us (0.69)
  the two profiles are of different devices: /device:TPU:256 before, /device:TPU:128 now
where the time goes in v2:
time: 129 us
  blocking collectives  32.6 us (25%)
  Pallas kernels  31.9 us (25%)
  waiting for transfers between devices  28.5 us (22%)
  starting transfers between devices  15.1 us (12%)
  local copies, waits for them, and re-layouts  12.5 us (10%)
  other arithmetic  7.99 us (6%)
    all_to_all x1, blocking collectives, shards(): lax.all_to_all(local_out, 'head', split_axis=0, concat_axis=1, tiled=True)  32.6 us
    pallas_call x1, Pallas kernels, attend(): pl.pallas_call(functools.partial(attend_kernel, heads=heads), out_shape=j...  31.9 us
    all_to_all x1, waiting for transfers between devices, shards(): lax.all_to_all(queries, 'head', split_axis=1, concat_axis=0, tiled=True)  14.3 us
    all_to_all x1, waiting for transfers between devices, shards(): lax.all_to_all(paired, 'head', split_axis=1, concat_axis=0, tiled=True)  8.52 us
    all_to_all x1, starting transfers between devices, shards(): lax.all_to_all(paired, 'head', split_axis=1, concat_axis=0, tiled=True)  6.11 us
    ppermute x2, waiting for transfers between devices, from_behind(): lax.ppermute(value, axis, [(source, source + steps) for source in range(l...  5.7 us
    ppermute x2, starting transfers between devices, from_behind(): lax.ppermute(value, axis, [(source, source + steps) for source in range(l...  5.39 us
    reduce_sum x1, other arithmetic, shards(): counts.append(jnp.sum((back == first_q[qb]).astype(jnp.int32)))  4.03 us
  transfers between devices with their start and end apart: 4, of which 3 were waited for; matrix products, arithmetic and copies ran while one was open for 11% of the time, Pallas kernels for 0%

profile of v2, /device:TPU:128, one launch (start us, length us, event | category | flops | bytes accessed | tf_op | source)
XLA Modules:
  0.0 128.8 jit_solution(1772014598541140784)
XLA Ops:
  0.0 0.0 copy-start
  0.0 0.0 copy-start.1
  0.0 0.9 copy-done
  1.0 1.1 copy_bitcast_fusion.1
  2.0 0.8 pad_maximum_fusion.1
  2.9 6.1 %all-to-all-start.1 = ((bf16[128,8,256]{2,0,1:T(8,128)(2,1)}), bf16[128,8,256]{2,0,1:T(8,128)(2,1)S(1)}, u32[]{:S(2)}, u32[]{:S(2)}) async-start(bf16[128,8,256]{2,0,1:T(8,128)(2,1)} %pad_maximum_fusion.1), calls=%async_computation.1 | async-start | bytes 1048576 | tf_op jit(solution)/shard_map/all_to_all | solution.py:127
  9.0 0.0 copy-done.1
  9.0 1.6 %copy.39 = bf16[16,8,8,1024]{3,2,0,1:T(8,128)(2,1)} copy(bf16[16,8,8,1024]{3,2,1,0:T(8,128)(2,1)S(1)} %bitcast.40) | data formatting | bytes 4194304 | tf_op jit(solution)/shard_map/all_to_all | solution.py:128
  10.5 8.5 %all-to-all-done.1 = bf16[128,8,256]{2,0,1:T(8,128)(2,1)S(1)} async-done(((bf16[128,8,256]{2,0,1:T(8,128)(2,1)}), bf16[128,8,256]{2,0,1:T(8,128)(2,1)S(1)}, u32[]{:S(2)}, u32[]{:S(2)}) %all-to-all-start.1) | async-done | bytes 524320 | tf_op jit(solution)/shard_map/all_to_all | solution.py:127
  19.1 3.6 %all-to-all-start = ((bf16[128,8,1024]{2,0,1:T(8,128)(2,1)}), bf16[128,8,1024]{2,0,1:T(8,128)(2,1)S(1)}, u32[]{:S(2)}, u32[]{:S(2)}) async-start(bf16[128,8,1024]{2,0,1:T(8,128)(2,1)} %bitcast.35), calls=%async_computation | async-start | bytes 4194304 | tf_op jit(solution)/shard_map/all_to_all | solution.py:128
  22.7 1.9 %collective-permute-start.1 = (bf16[1024,256]{1,0:T(8,128)(2,1)S(1)}, bf16[1024,256]{1,0:T(8,128)(2,1)S(1)}, u32[]{:S(2)}, u32[]{:S(2)}) collective-permute-start(bf16[1024,256]{1,0:T(8,128)(2,1)S(1)} %bitcast.37), channel_id=1, source_target_pairs={{0,8},{8,16},{16,24},{24,32},{32,40},{40,48},{48,56},{56,64},{64,7... | collective-permute-start | bytes 1572872 | tf_op jit(solution)/shard_map/ppermute | solution.py:25
  24.6 0.8 pad_dynamic-slice_fusion
  25.4 0.6 reshape.53
  26.0 0.7 dynamic_slice.7
  26.7 0.6 fusion.1
  27.3 0.6 slice.74
  28.0 3.5 %collective-permute-start = (bf16[256,256]{1,0:T(8,128)(2,1)}, bf16[256,256]{1,0:T(8,128)(2,1)S(1)}, u32[]{:S(2)}, u32[]{:S(2)}) collective-permute-start(bf16[256,256]{1,0:T(8,128)(2,1)} %bitcast.12), channel_id=1, source_target_pairs={{0,16},{8,24},{16,32},{24,40},{32,48},{40,56},{48,64},{56,72},{64,... | collective-permute-start | bytes 393224 | tf_op jit(solution)/shard_map/ppermute | solution.py:25
  31.4 4.0 %convert_reduce_fusion.3 = (s32[]{:T(128)}, s32[]{:T(128)}, s32[]{:T(128)}, s32[]{:T(128)}) fusion(s32[9,256]{1,0:T(8,128)} %reshape.53, s32[]{:T(128)} %bitcast, s32[]{:T(128)} %bitcast.6, s32[]{:T(128)} %bitcast.4, s32[]{:T(128)} %bitcast.2), kind=kLoop, calls=%fused_computation.13 | loop fusion | flops 56 | bytes 112 | tf_op jit(solution)/shard_map/reduce_sum | solution.py:145
  35.5 0.6 reshape.59.kid_ref
  36.1 1.0 copy.26.qid_ref
  37.1 3.0 %pad_add_fusion.nback_ref = s32[4]{0:T(128)} fusion(s32[1]{0:T(128)} %bitcast.7, s32[1]{0:T(128)} %bitcast.5, s32[1]{0:T(128)} %bitcast.3, s32[1]{0:T(128)} %bitcast.1), kind=kLoop, calls=%fused_computation.14 | loop fusion | flops 12 | bytes 32 | tf_op jit(solution)/shard_map/stack | solution.py:146
  40.1 5.7 %collective-permute-done = bf16[256,256]{1,0:T(8,128)(2,1)S(1)} collective-permute-done((bf16[256,256]{1,0:T(8,128)(2,1)}, bf16[256,256]{1,0:T(8,128)(2,1)S(1)}, u32[]{:S(2)}, u32[]{:S(2)}) %collective-permute-start) | collective-permute-done | bytes 131104 | tf_op jit(solution)/shard_map/ppermute | solution.py:25
  45.8 0.0 collective-permute-done.1
  45.8 0.1 pad_maximum_fusion
  45.9 1.1 fusion
  47.0 14.3 %all-to-all-done = bf16[128,8,1024]{2,0,1:T(8,128)(2,1)S(1)} async-done(((bf16[128,8,1024]{2,0,1:T(8,128)(2,1)}), bf16[128,8,1024]{2,0,1:T(8,128)(2,1)S(1)}, u32[]{:S(2)}, u32[]{:S(2)}) %all-to-all-start) | async-done | bytes 2097184 | tf_op jit(solution)/shard_map/all_to_all | solution.py:128
  61.3 0.0 copy-start.2
  61.3 1.3 %copy-done.2 = bf16[128,8,1024]{2,0,1:T(8,128)(2,1)} copy-done((bf16[128,8,1024]{2,0,1:T(8,128)(2,1)}, bf16[128,8,1024]{2,0,1:T(8,128)(2,1)S(1)}, u32[]{:S(2)}) %copy-start.2) | copy-done | bytes 2097176
  62.7 31.9 %shard_map.46 = bf16[1024,1024]{1,0:T(8,128)(2,1)} custom-call(s32[4]{0:T(128)} %pad_add_fusion.nback_ref, bf16[1024,1024]{1,0:T(8,128)(2,1)} %bitcast.41, bf16[2304,128]{1,0:T(8,128)(2,1)} %get-tuple-element.10.k_ref, bf16[2304,128]{1,0:T(8,128)(2,1)} %get-tuple-element.9.v_ref, s32[1024,1]{1,0:T(8,128)} %copy.26.qid_ref, s32[1,2304]{1,0:T(1,128)} %reshape.59.kid_ref), custom_call_target="tpu_custom_call" | custom-call | flops 4831838208 | bytes 4194304 | tf_op jit(solution)/shard_map/pallas_call | solution.py:110
  94.6 32.6 %all_to_all.53 = bf16[8,128,1024]{2,1,0:T(8,128)(2,1)S(1)} all-to-all(bf16[8,128,1024]{2,1,0:T(8,128)(2,1)} %bitcast.42), channel_id=1, replica_groups=mesh['ctx'=64,'head'=8] {'head'}, dimensions={0} | all-to-all | bytes 4194304 | tf_op jit(solution)/shard_map/all_to_all | solution.py:150
  127.2 1.6 %copy.35 = bf16[8,16,8,1024]{3,2,0,1:T(8,128)(2,1)} copy(bf16[8,16,8,1024]{3,2,1,0:T(8,128)(2,1)S(1)} %bitcast.36) | data formatting | bytes 4194304 | tf_op jit(solution)/shard_map/all_to_all | solution.py:150
  (1 shorter events, 0.0 us)
Async XLA Ops:
  0.0 1.0 copy-start
  0.0 9.0 %copy-start.1 = (bf16[128,8192]{1,0:T(8,128)(2,1)S(1)}, bf16[128,8192]{1,0:T(8,128)(2,1)}, u32[]{:S(2)}) copy-start(bf16[128,8192]{1,0:T(8,128)(2,1)} %param.4) | copy-start | bytes 6291460
  2.9 16.2 %all-to-all-start.1 = ((bf16[128,8,256]{2,0,1:T(8,128)(2,1)}), bf16[128,8,256]{2,0,1:T(8,128)(2,1)S(1)}, u32[]{:S(2)}, u32[]{:S(2)}) async-start(bf16[128,8,256]{2,0,1:T(8,128)(2,1)} %pad_maximum_fusion.1), calls=%async_computation.1 | async-start | bytes 1048576 | tf_op jit(solution)/shard_map/all_to_all | solution.py:127
  19.1 42.3 %all-to-all-start = ((bf16[128,8,1024]{2,0,1:T(8,128)(2,1)}), bf16[128,8,1024]{2,0,1:T(8,128)(2,1)S(1)}, u32[]{:S(2)}, u32[]{:S(2)}) async-start(bf16[128,8,1024]{2,0,1:T(8,128)(2,1)} %bitcast.35), calls=%async_computation | async-start | bytes 4194304 | tf_op jit(solution)/shard_map/all_to_all | solution.py:128
  22.7 23.2 %collective-permute-start.1 = (bf16[1024,256]{1,0:T(8,128)(2,1)S(1)}, bf16[1024,256]{1,0:T(8,128)(2,1)S(1)}, u32[]{:S(2)}, u32[]{:S(2)}) collective-permute-start(bf16[1024,256]{1,0:T(8,128)(2,1)S(1)} %bitcast.37), channel_id=1, source_target_pairs={{0,8},{8,16},{16,24},{24,32},{32,40},{40,48},{48,56},{56,64},{64,7... | collective-permute-start | bytes 1572872 | tf_op jit(solution)/shard_map/ppermute | solution.py:25
  28.0 17.9 %collective-permute-start = (bf16[256,256]{1,0:T(8,128)(2,1)}, bf16[256,256]{1,0:T(8,128)(2,1)S(1)}, u32[]{:S(2)}, u32[]{:S(2)}) collective-permute-start(bf16[256,256]{1,0:T(8,128)(2,1)} %bitcast.12), channel_id=1, source_target_pairs={{0,16},{8,24},{16,32},{24,40},{32,48},{40,56},{48,64},{56,72},{64,... | collective-permute-start | bytes 393224 | tf_op jit(solution)/shard_map/ppermute | solution.py:25
  61.3 1.3 %copy-start.2 = (bf16[128,8,1024]{2,0,1:T(8,128)(2,1)}, bf16[128,8,1024]{2,0,1:T(8,128)(2,1)S(1)}, u32[]{:S(2)}) copy-start(bf16[128,8,1024]{2,0,1:T(8,128)(2,1)S(1)} %all-to-all-done) | copy-start | bytes 6291460

commit v3 on v2

--- a/solution.py
+++ b/solution.py
@@ -117,16 +117,44 @@
     )(nback, queries, keys, values, qids, kids)
 
 
+SPLIT = 2
+
+
+def exchange(pieces_for, axis):
+    count = lax.axis_size(axis)
+    got = [pieces_for(0)]
+    for d in range(1, count):
+        perm = [(src, (src + d) % count) for src in range(count)]
+        got.append(lax.ppermute(pieces_for(d), axis, perm))
+    return jnp.stack(got)
+
+
+def by_source(stacked, me, count):
+    order = (me - jnp.arange(count, dtype=jnp.int32)) % count
+    return jnp.take(stacked, order, axis=0)
+
+
 def shards(queries, keys, values, doc_ids):
     range_rows = QBLK_DEV * BLOCK
     rows = queries.shape[0]
-    heads_axis = lax.axis_size("head")
+    n_head = lax.axis_size("head")
+    me = lax.axis_index("head")
     ctx_pos = lax.axis_index("ctx")
+    per_group = QH // KVH
+    part = per_group // SPLIT
+    grouped_q = queries.reshape(rows, n_head, SPLIT, part * HD)
     paired = jnp.concatenate(
-        [keys.reshape(rows, heads_axis, -1), values.reshape(rows, heads_axis, -1)], axis=2)
-    local_pair = lax.all_to_all(paired, "head", split_axis=1, concat_axis=0, tiled=True)
-    local_queries = lax.all_to_all(queries, "head", split_axis=1, concat_axis=0, tiled=True)
+        [keys.reshape(rows, n_head, HD), values.reshape(rows, n_head, HD)], axis=2)
+
+    def group_piece(array, d):
+        return lax.dynamic_index_in_dim(array, (me + d) % n_head, axis=1, keepdims=False)
+
+    local_pair = by_source(exchange(lambda d: group_piece(paired, d), "head"), me, n_head)
     local_pair = local_pair.reshape(range_rows, 2 * HD)
+    local_qs = []
+    for s in range(SPLIT):
+        got = exchange(lambda d: group_piece(grouped_q[:, :, s], d), "head")
+        local_qs.append(by_source(got, me, n_head).reshape(range_rows, part * HD))
     prev1 = from_behind(local_pair, "ctx", 1)
     prev2 = from_behind(local_pair[range_rows - BLOCK:], "ctx", 2)
     window = jnp.concatenate([prev2, prev1, local_pair], axis=0)
@@ -144,10 +172,16 @@
         back = tile_last[lo:base + qb]
         counts.append(jnp.sum((back == first_q[qb]).astype(jnp.int32)))
     nback = jnp.stack(counts)
-    local_out = attend(
-        nback, local_queries, window[:, :HD], window[:, HD:],
-        range_ids.reshape(range_rows, 1), window_ids.reshape(1, -1))
-    return lax.all_to_all(local_out, "head", split_axis=0, concat_axis=1, tiled=True)
+    qids = range_ids.reshape(range_rows, 1)
+    kids = window_ids.reshape(1, -1)
+    outs = []
+    for s in range(SPLIT):
+        local_out = attend(nback, local_qs[s], window[:, :HD], window[:, HD:], qids, kids)
+        chunks = local_out.reshape(n_head, rows, part * HD)
+        got = exchange(lambda d: lax.dynamic_index_in_dim(chunks, (me + d) % n_head, 0, False), "head")
+        outs.append(by_source(got, me, n_head))
+    full = jnp.stack(outs, axis=2)
+    return jnp.transpose(full, (1, 0, 2, 3)).reshape(rows, QH * HD)
 
 
 def solution(mesh):

time: 129 us -> 264 us (2.05)
  starting transfers between devices: 15.1 us -> 129 us
  local copies, waits for them, and re-layouts: 12.5 us -> 61.7 us
  blocking collectives: 32.6 us -> 0 us
  waiting for transfers between devices: 28.5 us -> 7.91 us
  Pallas kernels: 31.9 us -> 49.4 us
  other arithmetic: 7.99 us -> 13.2 us
    ppermute x0 -> x35, starting transfers between devices: none -> 123 us  [exchange(): got.append(lax.ppermute(pieces_for(d), axis, perm))]
    all_to_all x1 -> x0, blocking collectives: 32.6 us -> none  [shards(): lax.all_to_all(local_out, 'head', split_axis=0, concat_axis=1, tiled=True)]
    unnamed x6 -> x46, local copies, waits for them, and re-layouts: 2.27 us -> 30 us
    all_to_all x2 -> x0, waiting for transfers between devices: 22.8 us -> none  [the longest x1 14.3 us: shards(): lax.all_to_all(queries, 'head', split_axis=1, concat_axis=0, tiled=True)]
    pallas_call x1 -> x2, Pallas kernels: 31.9 us -> 49.4 us  [attend(): pl.pallas_call(functools.partial(attend_kernel, heads=heads), out_shape=j...]
    dynamic_slice x0 -> x25, local copies, waits for them, and re-layouts: none -> 12.5 us  [group_piece(): lax.dynamic_index_in_dim(array, (me + d) % n_head, axis=1, keepdims=False)]
    all_to_all x2 -> x0, starting transfers between devices: 9.71 us -> none  [the longest x1 6.11 us: shards(): lax.all_to_all(paired, 'head', split_axis=1, concat_axis=0, tiled=True)]
    select_n x0 -> x5, other arithmetic: none -> 4.43 us  [by_source(): return jnp.take(stacked, order, axis=0)]
  transfers between devices with their start and end apart: 4 -> 37, of which waited for: 3 -> 3; matrix products, arithmetic and copies ran while one was open for 11% -> 24% of each run, Pallas kernels for 0% -> 9%
where the time goes in v3:
time: 264 us; the launch traced here: 262 us
  starting transfers between devices  129 us (49%)
  local copies, waits for them, and re-layouts  61.7 us (23%)
  Pallas kernels  49.4 us (19%)
  other arithmetic  13.2 us (5%)
  waiting for transfers between devices  7.91 us (3%)
    ppermute x35, starting transfers between devices, exchange(): got.append(lax.ppermute(pieces_for(d), axis, perm))  123 us
    pallas_call x2, Pallas kernels, attend(): pl.pallas_call(functools.partial(attend_kernel, heads=heads), out_shape=j...  49.4 us
    unnamed x46, local copies, waits for them, and re-layouts  30 us
    dynamic_slice x25, local copies, waits for them, and re-layouts, group_piece(): lax.dynamic_index_in_dim(array, (me + d) % n_head, axis=1, keepdims=False)  12.5 us
    ppermute x2, waiting for transfers between devices, from_behind(): lax.ppermute(value, axis, [(source, source + steps) for source in range(l...  6.8 us
    ppermute x2, starting transfers between devices, from_behind(): lax.ppermute(value, axis, [(source, source + steps) for source in range(l...  5.38 us
  transfers between devices with their start and end apart: 37, of which 3 were waited for; matrix products, arithmetic and copies ran while one was open for 24% of the time, Pallas kernels for 9%

profile of v3, /device:TPU:128, one launch (start us, length us, event | category | flops | bytes accessed | tf_op | source)
XLA Modules:
  0.0 261.7 jit_solution(7537401037219306824)
XLA Ops:
  0.0 1.2 copy.82
  1.2 1.1 copy.83
  3.1 4.3 %collective-permute-start.7 = (bf16[128,256]{1,0:T(8,128)(2,1)}, bf16[128,256]{1,0:T(8,128)(2,1)}, u32[]{:S(2)}, u32[]{:S(2)}) collective-permute-start(bf16[128,256]{1,0:T(8,128)(2,1)} %bitcast.28), channel_id=1, source_target_pairs={{0,1},{1,2},{2,3},{3,4},{4,5},{5,6},{6,7},{7,0},{8,9},{9,10},{10,1... | collective-permute-start | bytes 196616 | tf_op jit(solution)/shard_map/ppermute | solution.py:128
  8.1 3.4 %collective-permute-start.8 = (bf16[128,256]{1,0:T(8,128)(2,1)}, bf16[128,256]{1,0:T(8,128)(2,1)}, u32[]{:S(2)}, u32[]{:S(2)}) collective-permute-start(bf16[128,256]{1,0:T(8,128)(2,1)} %bitcast.30), channel_id=1, source_target_pairs={{0,2},{1,3},{2,4},{3,5},{4,6},{5,7},{6,0},{7,1},{8,10},{9,11},{10,... | collective-permute-start | bytes 196616 | tf_op jit(solution)/shard_map/ppermute | solution.py:128
  12.2 3.1 %collective-permute-start.9 = (bf16[128,256]{1,0:T(8,128)(2,1)}, bf16[128,256]{1,0:T(8,128)(2,1)}, u32[]{:S(2)}, u32[]{:S(2)}) collective-permute-start(bf16[128,256]{1,0:T(8,128)(2,1)} %bitcast.32), channel_id=1, source_target_pairs={{0,3},{1,4},{2,5},{3,6},{4,7},{5,0},{6,1},{7,2},{8,11},{9,12},{10,... | collective-permute-start | bytes 196616 | tf_op jit(solution)/shard_map/ppermute | solution.py:128
  16.1 3.9 %collective-permute-start.10 = (bf16[128,256]{1,0:T(8,128)(2,1)}, bf16[128,256]{1,0:T(8,128)(2,1)}, u32[]{:S(2)}, u32[]{:S(2)}) collective-permute-start(bf16[128,256]{1,0:T(8,128)(2,1)} %bitcast.34), channel_id=1, source_target_pairs={{0,4},{1,5},{2,6},{3,7},{4,0},{5,1},{6,2},{7,3},{8,12},{9,13},{10,... | collective-permute-start | bytes 196616 | tf_op jit(solution)/shard_map/ppermute | solution.py:128
  20.8 5.8 %collective-permute-start.11 = (bf16[128,256]{1,0:T(8,128)(2,1)}, bf16[128,256]{1,0:T(8,128)(2,1)}, u32[]{:S(2)}, u32[]{:S(2)}) collective-permute-start(bf16[128,256]{1,0:T(8,128)(2,1)} %bitcast.36), channel_id=1, source_target_pairs={{0,5},{1,6},{2,7},{3,0},{4,1},{5,2},{6,3},{7,4},{8,13},{9,14},{10,... | collective-permute-start | bytes 196616 | tf_op jit(solution)/shard_map/ppermute | solution.py:128
  31.4 3.2 %copy.73 = bf16[128,8192]{0,1:T(8,128)(2,1)S(1)} copy(bf16[128,8192]{1,0:T(8,128)(2,1)} %param.6) | data formatting | bytes 4194304 | tf_op args[0]
  41.5 1.2 pad_clamp_fusion.1
  46.3 1.0 copy.92.qid_ref
  47.3 3.3 %convert_reduce_fusion.3 = (s32[]{:T(128)}, s32[]{:T(128)}, s32[]{:T(128)}, s32[]{:T(128)}) fusion(s32[9,256]{1,0:T(8,128)S(1)} %reshape.158, s32[]{:T(128)} %bitcast, s32[]{:T(128)} %bitcast.6, s32[]{:T(128)} %bitcast.4, s32[]{:T(128)} %bitcast.2), kind=kLoop, calls=%fused_computation.117 | loop fusion | flops 56 | bytes 112 | tf_op jit(solution)/shard_map/reduce_sum | solution.py:173
  50.6 3.0 %pad_add_fusion.nback_ref = s32[4]{0:T(128)} fusion(s32[1]{0:T(128)} %bitcast.7, s32[1]{0:T(128)} %bitcast.5, s32[1]{0:T(128)} %bitcast.3, s32[1]{0:T(128)} %bitcast.1), kind=kLoop, calls=%fused_computation.131 | loop fusion | flops 12 | bytes 32 | tf_op jit(solution)/shard_map/stack | solution.py:174
  53.7 3.3 %collective-permute-start.12 = (bf16[128,256]{1,0:T(8,128)(2,1)}, bf16[128,256]{1,0:T(8,128)(2,1)S(1)}, u32[]{:S(2)}, u32[]{:S(2)}) collective-permute-start(bf16[128,256]{1,0:T(8,128)(2,1)} %bitcast.178), channel_id=1, source_target_pairs={{0,6},{1,7},{2,0},{3,1},{4,2},{5,3},{6,4},{7,5},{8,14},{9,15},{10,... | collective-permute-start | bytes 196616 | tf_op jit(solution)/shard_map/ppermute | solution.py:128
  57.9 1.9 collective-permute-start.13
  60.6 3.9 %collective-permute-start.23 = (bf16[128,512]{1,0:T(8,128)(2,1)}, bf16[128,512]{1,0:T(8,128)(2,1)S(1)}, u32[]{:S(2)}, u32[]{:S(2)}) collective-permute-start(bf16[128,512]{1,0:T(8,128)(2,1)} %bitcast.175), channel_id=1, source_target_pairs={{0,1},{1,2},{2,3},{3,4},{4,5},{5,6},{6,7},{7,0},{8,9},{9,10},{10,1... | collective-permute-start | bytes 393224 | tf_op jit(solution)/shard_map/ppermute | solution.py:128
  65.4 2.5 collective-permute-start.24
  68.7 1.9 collective-permute-start.25
  71.5 5.5 %collective-permute-start.26 = (bf16[128,512]{1,0:T(8,128)(2,1)}, bf16[128,512]{1,0:T(8,128)(2,1)}, u32[]{:S(2)}, u32[]{:S(2)}) collective-permute-start(bf16[128,512]{1,0:T(8,128)(2,1)} %bitcast.172), channel_id=1, source_target_pairs={{0,4},{1,5},{2,6},{3,7},{4,0},{5,1},{6,2},{7,3},{8,12},{9,13},{10,... | collective-permute-start | bytes 393224 | tf_op jit(solution)/shard_map/ppermute | solution.py:128
  77.0 3.6 %collective-permute-start.27 = (bf16[128,512]{1,0:T(8,128)(2,1)}, bf16[128,512]{1,0:T(8,128)(2,1)}, u32[]{:S(2)}, u32[]{:S(2)}) collective-permute-start(bf16[128,512]{1,0:T(8,128)(2,1)} %bitcast.171), channel_id=1, source_target_pairs={{0,5},{1,6},{2,7},{3,0},{4,1},{5,2},{6,3},{7,4},{8,13},{9,14},{10,... | collective-permute-start | bytes 393224 | tf_op jit(solution)/shard_map/ppermute | solution.py:128
  82.3 1.4 slice_select_fusion
  83.7 3.7 %collective-permute-start.28 = (bf16[128,512]{1,0:T(8,128)(2,1)S(1)}, bf16[128,512]{1,0:T(8,128)(2,1)S(1)}, u32[]{:S(2)}, u32[]{:S(2)}) collective-permute-start(bf16[128,512]{1,0:T(8,128)(2,1)S(1)} %bitcast.170), channel_id=1, source_target_pairs={{0,6},{1,7},{2,0},{3,1},{4,2},{5,3},{6,4},{7,5},{8,14},{9,15},{10,... | collective-permute-start | bytes 393224 | tf_op jit(solution)/shard_map/ppermute | solution.py:128
  87.4 1.9 collective-permute-start.29
  89.4 3.9 %collective-permute-start = (bf16[128,512]{1,0:T(8,128)(2,1)S(1)}, bf16[128,512]{1,0:T(8,128)(2,1)}, u32[]{:S(2)}, u32[]{:S(2)}) collective-permute-start(bf16[128,512]{1,0:T(8,128)(2,1)S(1)} %bitcast.168), channel_id=1, source_target_pairs={{0,1},{1,2},{2,3},{3,4},{4,5},{5,6},{6,7},{7,0},{8,9},{9,10},{10,1... | collective-permute-start | bytes 393224 | tf_op jit(solution)/shard_map/ppermute | solution.py:128
  93.3 2.7 %collective-permute-start.1 = (bf16[128,512]{1,0:T(8,128)(2,1)S(1)}, bf16[128,512]{1,0:T(8,128)(2,1)}, u32[]{:S(2)}, u32[]{:S(2)}) collective-permute-start(bf16[128,512]{1,0:T(8,128)(2,1)S(1)} %bitcast.167), channel_id=1, source_target_pairs={{0,2},{1,3},{2,4},{3,5},{4,6},{5,7},{6,0},{7,1},{8,10},{9,11},{10,... | collective-permute-start | bytes 393224 | tf_op jit(solution)/shard_map/ppermute | solution.py:128
  96.1 0.9 bitcast_dynamic-update-slice_fusion.10
  97.0 3.4 %collective-permute-start.2 = (bf16[128,512]{1,0:T(8,128)(2,1)S(1)}, bf16[128,512]{1,0:T(8,128)(2,1)}, u32[]{:S(2)}, u32[]{:S(2)}) collective-permute-start(bf16[128,512]{1,0:T(8,128)(2,1)S(1)} %bitcast.166), channel_id=1, source_target_pairs={{0,3},{1,4},{2,5},{3,6},{4,7},{5,0},{6,1},{7,2},{8,11},{9,12},{10,... | collective-permute-start | bytes 393224 | tf_op jit(solution)/shard_map/ppermute | solution.py:128
  100.4 0.9 bitcast_dynamic-update-slice_fusion.9
  101.4 5.1 %collective-permute-start.3 = (bf16[128,512]{1,0:T(8,128)(2,1)S(1)}, bf16[128,512]{1,0:T(8,128)(2,1)}, u32[]{:S(2)}, u32[]{:S(2)}) collective-permute-start(bf16[128,512]{1,0:T(8,128)(2,1)S(1)} %bitcast.165), channel_id=1, source_target_pairs={{0,4},{1,5},{2,6},{3,7},{4,0},{5,1},{6,2},{7,3},{8,12},{9,13},{10,... | collective-permute-start | bytes 393224 | tf_op jit(solution)/shard_map/ppermute | solution.py:128
  106.5 3.7 %collective-permute-start.4 = (bf16[128,512]{1,0:T(8,128)(2,1)}, bf16[128,512]{1,0:T(8,128)(2,1)}, u32[]{:S(2)}, u32[]{:S(2)}) collective-permute-start(bf16[128,512]{1,0:T(8,128)(2,1)} %bitcast.18), channel_id=1, source_target_pairs={{0,5},{1,6},{2,7},{3,0},{4,1},{5,2},{6,3},{7,4},{8,13},{9,14},{10,... | collective-permute-start | bytes 393224 | tf_op jit(solution)/shard_map/ppermute | solution.py:128
  110.9 4.5 %collective-permute-start.5 = (bf16[128,512]{1,0:T(8,128)(2,1)S(1)}, bf16[128,512]{1,0:T(8,128)(2,1)S(1)}, u32[]{:S(2)}, u32[]{:S(2)}) collective-permute-start(bf16[128,512]{1,0:T(8,128)(2,1)S(1)} %bitcast.164), channel_id=1, source_target_pairs={{0,6},{1,7},{2,0},{3,1},{4,2},{5,3},{6,4},{7,5},{8,14},{9,15},{10,... | collective-permute-start | bytes 393224 | tf_op jit(solution)/shard_map/ppermute | solution.py:128
  115.4 1.6 bitcast_dynamic-update-slice_fusion.28
  117.0 1.9 collective-permute-start.6
  118.9 1.6 bitcast_dynamic-update-slice_fusion.27
  120.5 1.9 collective-permute-start.15
  122.4 1.6 bitcast_dynamic-update-slice_fusion.26
  124.0 3.5 %collective-permute-start.14 = (bf16[256,256]{1,0:T(8,128)(2,1)}, bf16[256,256]{1,0:T(8,128)(2,1)S(1)}, u32[]{:S(2)}, u32[]{:S(2)}) collective-permute-start(bf16[256,256]{1,0:T(8,128)(2,1)} %bitcast.176), channel_id=1, source_target_pairs={{0,16},{8,24},{16,32},{24,40},{32,48},{40,56},{48,64},{56,72},{64,... | collective-permute-start | bytes 393224 | tf_op jit(solution)/shard_map/ppermute | solution.py:25
  127.5 1.6 bitcast_dynamic-update-slice_fusion.25
  129.0 1.6 bitcast_dynamic-update-slice_fusion.24
  131.9 1.8 gather_fusion.1
  133.8 1.6 broadcast_select_fusion.1
  135.4 6.5 %collective-permute-done.14 = bf16[256,256]{1,0:T(8,128)(2,1)S(1)} collective-permute-done((bf16[256,256]{1,0:T(8,128)(2,1)}, bf16[256,256]{1,0:T(8,128)(2,1)S(1)}, u32[]{:S(2)}, u32[]{:S(2)}) %collective-permute-start.14) | collective-permute-done | bytes 131104 | tf_op jit(solution)/shard_map/ppermute | solution.py:25
  142.3 1.1 fusion.12
  143.4 24.7 %shard_map.47 = bf16[1024,512]{1,0:T(8,128)(2,1)} custom-call(s32[4]{0:T(128)} %pad_add_fusion.nback_ref, bf16[1024,512]{1,0:T(8,128)(2,1)} %bitcast.160, bf16[2304,128]{1,0:T(8,128)(2,1)} %get-tuple-element.13.k_ref, bf16[2304,128]{1,0:T(8,128)(2,1)} %get-tuple-element.12.v_ref, s32[1024,1]{1,0:T(8,128)} %copy.92.qid_ref, s32[1,2304]{1,0:T(1,128)} %reshape.165.kid_ref), custom_call_target="tpu_custom_call" | custom-call | flops 2415919104 | bytes 2097152 | tf_op jit(solution)/shard_map/pallas_call | solution.py:110
  168.1 1.4 dynamic-slice_bitcast_fusion
  169.4 4.5 %collective-permute-start.30 = (bf16[128,512]{1,0:T(8,128)(2,1)S(1)}, bf16[128,512]{1,0:T(8,128)(2,1)}, u32[]{:S(2)}, u32[]{:S(2)}) collective-permute-start(bf16[128,512]{1,0:T(8,128)(2,1)S(1)} %get-tuple-element.36), channel_id=1, source_target_pairs={{0,1},{1,2},{2,3},{3,4},{4,5},{5,6},{6,7},{7,0},{8,9},{9,10},{10,1... | collective-permute-start | bytes 393224 | tf_op jit(solution)/shard_map/ppermute | solution.py:128
  173.9 1.9 collective-permute-start.31
  175.9 3.4 %collective-permute-start.32 = (bf16[128,512]{1,0:T(8,128)(2,1)S(1)}, bf16[128,512]{1,0:T(8,128)(2,1)}, u32[]{:S(2)}, u32[]{:S(2)}) collective-permute-start(bf16[128,512]{1,0:T(8,128)(2,1)S(1)} %get-tuple-element.34), channel_id=1, source_target_pairs={{0,3},{1,4},{2,5},{3,6},{4,7},{5,0},{6,1},{7,2},{8,11},{9,12},{10,... | collective-permute-start | bytes 393224 | tf_op jit(solution)/shard_map/ppermute | solution.py:128
  179.3 4.6 %collective-permute-start.33 = (bf16[128,512]{1,0:T(8,128)(2,1)S(1)}, bf16[128,512]{1,0:T(8,128)(2,1)}, u32[]{:S(2)}, u32[]{:S(2)}) collective-permute-start(bf16[128,512]{1,0:T(8,128)(2,1)S(1)} %get-tuple-element.33), channel_id=1, source_target_pairs={{0,4},{1,5},{2,6},{3,7},{4,0},{5,1},{6,2},{7,3},{8,12},{9,13},{10,... | collective-permute-start | bytes 393224 | tf_op jit(solution)/shard_map/ppermute | solution.py:128
  183.8 2.9 %collective-permute-start.34 = (bf16[128,512]{1,0:T(8,128)(2,1)S(1)}, bf16[128,512]{1,0:T(8,128)(2,1)S(1)}, u32[]{:S(2)}, u32[]{:S(2)}) collective-permute-start(bf16[128,512]{1,0:T(8,128)(2,1)S(1)} %get-tuple-element.32), channel_id=1, source_target_pairs={{0,5},{1,6},{2,7},{3,0},{4,1},{5,2},{6,3},{7,4},{8,13},{9,14},{10,... | collective-permute-start | bytes 393224 | tf_op jit(solution)/shard_map/ppermute | solution.py:128
  186.8 24.7 %shard_map.46 = bf16[1024,512]{1,0:T(8,128)(2,1)} custom-call(s32[4]{0:T(128)} %pad_add_fusion.nback_ref, bf16[1024,512]{1,0:T(8,128)(2,1)} %bitcast.159, bf16[2304,128]{1,0:T(8,128)(2,1)} %get-tuple-element.13.k_ref, bf16[2304,128]{1,0:T(8,128)(2,1)} %get-tuple-element.12.v_ref, s32[1024,1]{1,0:T(8,128)} %copy.92.qid_ref, s32[1,2304]{1,0:T(1,128)} %reshape.165.kid_ref), custom_call_target="tpu_custom_call" | custom-call | flops 2415919104 | bytes 2097152 | tf_op jit(solution)/shard_map/pallas_call | solution.py:110
  211.4 2.1 dynamic-slice_bitcast_fusion.7
  213.6 4.4 %collective-permute-start.35 = (bf16[128,512]{1,0:T(8,128)(2,1)S(1)}, bf16[128,512]{1,0:T(8,128)(2,1)S(1)}, u32[]{:S(2)}, u32[]{:S(2)}) collective-permute-start(bf16[128,512]{1,0:T(8,128)(2,1)S(1)} %get-tuple-element.31), channel_id=1, source_target_pairs={{0,6},{1,7},{2,0},{3,1},{4,2},{5,3},{6,4},{7,5},{8,14},{9,15},{10,... | collective-permute-start | bytes 393224 | tf_op jit(solution)/shard_map/ppermute | solution.py:128
  218.0 0.9 bitcast_dynamic-update-slice_fusion.6
  219.0 2.0 collective-permute-start.36
  221.9 3.9 %collective-permute-start.16 = (bf16[128,512]{1,0:T(8,128)(2,1)}, bf16[128,512]{1,0:T(8,128)(2,1)}, u32[]{:S(2)}, u32[]{:S(2)}) collective-permute-start(bf16[128,512]{1,0:T(8,128)(2,1)} %get-tuple-element.20), channel_id=1, source_target_pairs={{0,1},{1,2},{2,3},{3,4},{4,5},{5,6},{6,7},{7,0},{8,9},{9,10},{10,1... | collective-permute-start | bytes 393224 | tf_op jit(solution)/shard_map/ppermute | solution.py:128
  226.7 2.8 %collective-permute-start.17 = (bf16[128,512]{1,0:T(8,128)(2,1)}, bf16[128,512]{1,0:T(8,128)(2,1)}, u32[]{:S(2)}, u32[]{:S(2)}) collective-permute-start(bf16[128,512]{1,0:T(8,128)(2,1)} %get-tuple-element.19), channel_id=1, source_target_pairs={{0,2},{1,3},{2,4},{3,5},{4,6},{5,7},{6,0},{7,1},{8,10},{9,11},{10,... | collective-permute-start | bytes 393224 | tf_op jit(solution)/shard_map/ppermute | solution.py:128
  230.4 3.4 %collective-permute-start.18 = (bf16[128,512]{1,0:T(8,128)(2,1)}, bf16[128,512]{1,0:T(8,128)(2,1)}, u32[]{:S(2)}, u32[]{:S(2)}) collective-permute-start(bf16[128,512]{1,0:T(8,128)(2,1)} %get-tuple-element.18), channel_id=1, source_target_pairs={{0,3},{1,4},{2,5},{3,6},{4,7},{5,0},{6,1},{7,2},{8,11},{9,12},{10,... | collective-permute-start | bytes 393224 | tf_op jit(solution)/shard_map/ppermute | solution.py:128
  233.8 5.2 %collective-permute-start.19 = (bf16[128,512]{1,0:T(8,128)(2,1)}, bf16[128,512]{1,0:T(8,128)(2,1)}, u32[]{:S(2)}, u32[]{:S(2)}) collective-permute-start(bf16[128,512]{1,0:T(8,128)(2,1)} %get-tuple-element.17), channel_id=1, source_target_pairs={{0,4},{1,5},{2,6},{3,7},{4,0},{5,1},{6,2},{7,3},{8,12},{9,13},{10,... | collective-permute-start | bytes 393224 | tf_op jit(solution)/shard_map/ppermute | solution.py:128
  239.0 3.7 %collective-permute-start.20 = (bf16[128,512]{1,0:T(8,128)(2,1)S(1)}, bf16[128,512]{1,0:T(8,128)(2,1)}, u32[]{:S(2)}, u32[]{:S(2)}) collective-permute-start(bf16[128,512]{1,0:T(8,128)(2,1)S(1)} %get-tuple-element.16), channel_id=1, source_target_pairs={{0,5},{1,6},{2,7},{3,0},{4,1},{5,2},{6,3},{7,4},{8,13},{9,14},{10,... | collective-permute-start | bytes 393224 | tf_op jit(solution)/shard_map/ppermute | solution.py:128
  243.3 4.5 %collective-permute-start.21 = (bf16[128,512]{1,0:T(8,128)(2,1)S(1)}, bf16[128,512]{1,0:T(8,128)(2,1)S(1)}, u32[]{:S(2)}, u32[]{:S(2)}) collective-permute-start(bf16[128,512]{1,0:T(8,128)(2,1)S(1)} %get-tuple-element.15), channel_id=1, source_target_pairs={{0,6},{1,7},{2,0},{3,1},{4,2},{5,3},{6,4},{7,5},{8,14},{9,15},{10,... | collective-permute-start | bytes 393224 | tf_op jit(solution)/shard_map/ppermute | solution.py:128
  248.8 2.1 collective-permute-start.22
  254.6 1.0 collective-permute-done.22
  256.8 2.2 copy.102
  258.9 2.8 %reshape.169 = bf16[128,8192]{1,0:T(8,128)(2,1)} reshape(bf16[128,8,2,512]{3,2,1,0:T(2,128)(2,1)S(1)} %copy.102) | data formatting | bytes 4194304 | tf_op jit(solution)/shard_map/reshape | solution.py:184
  (123 shorter events, 36.1 us)
Async XLA Ops:
  0.0 28.5 %copy-start = (s32[65536]{0:T(1024)S(1)}, s32[65536]{0:T(1024)}, u32[]{:S(2)}) copy-start(s32[65536]{0:T(1024)} %param.9) | copy-start | bytes 786436
  3.1 50.6 %collective-permute-start.7 = (bf16[128,256]{1,0:T(8,128)(2,1)}, bf16[128,256]{1,0:T(8,128)(2,1)}, u32[]{:S(2)}, u32[]{:S(2)}) collective-permute-start(bf16[128,256]{1,0:T(8,128)(2,1)} %bitcast.28), channel_id=1, source_target_pairs={{0,1},{1,2},{2,3},{3,4},{4,5},{5,6},{6,7},{7,0},{8,9},{9,10},{10,1... | collective-permute-start | bytes 196616 | tf_op jit(solution)/shard_map/ppermute | solution.py:128
  8.1 49.7 %collective-permute-start.8 = (bf16[128,256]{1,0:T(8,128)(2,1)}, bf16[128,256]{1,0:T(8,128)(2,1)}, u32[]{:S(2)}, u32[]{:S(2)}) collective-permute-start(bf16[128,256]{1,0:T(8,128)(2,1)} %bitcast.30), channel_id=1, source_target_pairs={{0,2},{1,3},{2,4},{3,5},{4,6},{5,7},{6,0},{7,1},{8,10},{9,11},{10,... | collective-permute-start | bytes 196616 | tf_op jit(solution)/shard_map/ppermute | solution.py:128
  12.2 48.4 %collective-permute-start.9 = (bf16[128,256]{1,0:T(8,128)(2,1)}, bf16[128,256]{1,0:T(8,128)(2,1)}, u32[]{:S(2)}, u32[]{:S(2)}) collective-permute-start(bf16[128,256]{1,0:T(8,128)(2,1)} %bitcast.32), channel_id=1, source_target_pairs={{0,3},{1,4},{2,5},{3,6},{4,7},{5,0},{6,1},{7,2},{8,11},{9,12},{10,... | collective-permute-start | bytes 196616 | tf_op jit(solution)/shard_map/ppermute | solution.py:128
  16.1 49.3 %collective-permute-start.10 = (bf16[128,256]{1,0:T(8,128)(2,1)}, bf16[128,256]{1,0:T(8,128)(2,1)}, u32[]{:S(2)}, u32[]{:S(2)}) collective-permute-start(bf16[128,256]{1,0:T(8,128)(2,1)} %bitcast.34), channel_id=1, source_target_pairs={{0,4},{1,5},{2,6},{3,7},{4,0},{5,1},{6,2},{7,3},{8,12},{9,13},{10,... | collective-permute-start | bytes 196616 | tf_op jit(solution)/shard_map/ppermute | solution.py:128
  20.8 47.9 %collective-permute-start.11 = (bf16[128,256]{1,0:T(8,128)(2,1)}, bf16[128,256]{1,0:T(8,128)(2,1)}, u32[]{:S(2)}, u32[]{:S(2)}) collective-permute-start(bf16[128,256]{1,0:T(8,128)(2,1)} %bitcast.36), channel_id=1, source_target_pairs={{0,5},{1,6},{2,7},{3,0},{4,1},{5,2},{6,3},{7,4},{8,13},{9,14},{10,... | collective-permute-start | bytes 196616 | tf_op jit(solution)/shard_map/ppermute | solution.py:128
  26.7 0.7 copy-start.3
  44.8 38.8 %copy-start.1 = (bf16[128,1,1,512]{3,0,2,1:T(8,128)(2,1)S(1)}, bf16[128,1,1,512]{3,0,2,1:T(8,128)(2,1)}, u32[]{:S(2)}) copy-start(bf16[128,1,1,512]{3,0,2,1:T(8,128)(2,1)} %copy.99) | copy-start | bytes 393220
  53.7 17.8 %collective-permute-start.12 = (bf16[128,256]{1,0:T(8,128)(2,1)}, bf16[128,256]{1,0:T(8,128)(2,1)S(1)}, u32[]{:S(2)}, u32[]{:S(2)}) collective-permute-start(bf16[128,256]{1,0:T(8,128)(2,1)} %bitcast.178), channel_id=1, source_target_pairs={{0,6},{1,7},{2,0},{3,1},{4,2},{5,3},{6,4},{7,5},{8,14},{9,15},{10,... | collective-permute-start | bytes 196616 | tf_op jit(solution)/shard_map/ppermute | solution.py:128
  57.9 19.1 %collective-permute-start.13 = (bf16[128,256]{1,0:T(8,128)(2,1)}, bf16[128,256]{1,0:T(8,128)(2,1)S(1)}, u32[]{:S(2)}, u32[]{:S(2)}) collective-permute-start(bf16[128,256]{1,0:T(8,128)(2,1)} %bitcast.177), channel_id=1, source_target_pairs={{0,7},{1,0},{2,1},{3,2},{4,3},{5,4},{6,5},{7,6},{8,15},{9,8},{10,9... | collective-permute-start | bytes 196616 | tf_op jit(solution)/shard_map/ppermute | solution.py:128
  60.6 23.1 %collective-permute-start.23 = (bf16[128,512]{1,0:T(8,128)(2,1)}, bf16[128,512]{1,0:T(8,128)(2,1)S(1)}, u32[]{:S(2)}, u32[]{:S(2)}) collective-permute-start(bf16[128,512]{1,0:T(8,128)(2,1)} %bitcast.175), channel_id=1, source_target_pairs={{0,1},{1,2},{2,3},{3,4},{4,5},{5,6},{6,7},{7,0},{8,9},{9,10},{10,1... | collective-permute-start | bytes 393224 | tf_op jit(solution)/shard_map/ppermute | solution.py:128
  65.4 22.0 %collective-permute-start.24 = (bf16[128,512]{1,0:T(8,128)(2,1)}, bf16[128,512]{1,0:T(8,128)(2,1)S(1)}, u32[]{:S(2)}, u32[]{:S(2)}) collective-permute-start(bf16[128,512]{1,0:T(8,128)(2,1)} %bitcast.174), channel_id=1, source_target_pairs={{0,2},{1,3},{2,4},{3,5},{4,6},{5,7},{6,0},{7,1},{8,10},{9,11},{10,... | collective-permute-start | bytes 393224 | tf_op jit(solution)/shard_map/ppermute | solution.py:128
  68.7 20.6 %collective-permute-start.25 = (bf16[128,512]{1,0:T(8,128)(2,1)}, bf16[128,512]{1,0:T(8,128)(2,1)S(1)}, u32[]{:S(2)}, u32[]{:S(2)}) collective-permute-start(bf16[128,512]{1,0:T(8,128)(2,1)} %bitcast.173), channel_id=1, source_target_pairs={{0,3},{1,4},{2,5},{3,6},{4,7},{5,0},{6,1},{7,2},{8,11},{9,12},{10,... | collective-permute-start | bytes 393224 | tf_op jit(solution)/shard_map/ppermute | solution.py:128
  71.5 21.8 %collective-permute-start.26 = (bf16[128,512]{1,0:T(8,128)(2,1)}, bf16[128,512]{1,0:T(8,128)(2,1)}, u32[]{:S(2)}, u32[]{:S(2)}) collective-permute-start(bf16[128,512]{1,0:T(8,128)(2,1)} %bitcast.172), channel_id=1, source_target_pairs={{0,4},{1,5},{2,6},{3,7},{4,0},{5,1},{6,2},{7,3},{8,12},{9,13},{10,... | collective-permute-start | bytes 393224 | tf_op jit(solution)/shard_map/ppermute | solution.py:128
  77.0 20.0 %collective-permute-start.27 = (bf16[128,512]{1,0:T(8,128)(2,1)}, bf16[128,512]{1,0:T(8,128)(2,1)}, u32[]{:S(2)}, u32[]{:S(2)}) collective-permute-start(bf16[128,512]{1,0:T(8,128)(2,1)} %bitcast.171), channel_id=1, source_target_pairs={{0,5},{1,6},{2,7},{3,0},{4,1},{5,2},{6,3},{7,4},{8,13},{9,14},{10,... | collective-permute-start | bytes 393224 | tf_op jit(solution)/shard_map/ppermute | solution.py:128
  80.7 29.6 %copy-start.2 = (s32[1024]{0:T(1024)S(1)}, s32[1024]{0:T(1024)}, u32[]{:S(2)}) copy-start(s32[1024]{0:T(1024)} %pad_clamp_fusion.1) | copy-start | bytes 12292
  83.7 17.7 %collective-permute-start.28 = (bf16[128,512]{1,0:T(8,128)(2,1)S(1)}, bf16[128,512]{1,0:T(8,128)(2,1)S(1)}, u32[]{:S(2)}, u32[]{:S(2)}) collective-permute-start(bf16[128,512]{1,0:T(8,128)(2,1)S(1)} %bitcast.170), channel_id=1, source_target_pairs={{0,6},{1,7},{2,0},{3,1},{4,2},{5,3},{6,4},{7,5},{8,14},{9,15},{10,... | collective-permute-start | bytes 393224 | tf_op jit(solution)/shard_map/ppermute | solution.py:128
  87.4 19.1 %collective-permute-start.29 = (bf16[128,512]{1,0:T(8,128)(2,1)S(1)}, bf16[128,512]{1,0:T(8,128)(2,1)S(1)}, u32[]{:S(2)}, u32[]{:S(2)}) collective-permute-start(bf16[128,512]{1,0:T(8,128)(2,1)S(1)} %bitcast.169), channel_id=1, source_target_pairs={{0,7},{1,0},{2,1},{3,2},{4,3},{5,4},{6,5},{7,6},{8,15},{9,8},{10,9... | collective-permute-start | bytes 393224 | tf_op jit(solution)/shard_map/ppermute | solution.py:128
  89.4 21.5 %collective-permute-start = (bf16[128,512]{1,0:T(8,128)(2,1)S(1)}, bf16[128,512]{1,0:T(8,128)(2,1)}, u32[]{:S(2)}, u32[]{:S(2)}) collective-permute-start(bf16[128,512]{1,0:T(8,128)(2,1)S(1)} %bitcast.168), channel_id=1, source_target_pairs={{0,1},{1,2},{2,3},{3,4},{4,5},{5,6},{6,7},{7,0},{8,9},{9,10},{10,1... | collective-permute-start | bytes 393224 | tf_op jit(solution)/shard_map/ppermute | solution.py:128
  93.3 23.7 %collective-permute-start.1 = (bf16[128,512]{1,0:T(8,128)(2,1)S(1)}, bf16[128,512]{1,0:T(8,128)(2,1)}, u32[]{:S(2)}, u32[]{:S(2)}) collective-permute-start(bf16[128,512]{1,0:T(8,128)(2,1)S(1)} %bitcast.167), channel_id=1, source_target_pairs={{0,2},{1,3},{2,4},{3,5},{4,6},{5,7},{6,0},{7,1},{8,10},{9,11},{10,... | collective-permute-start | bytes 393224 | tf_op jit(solution)/shard_map/ppermute | solution.py:128
  97.0 23.5 %collective-permute-start.2 = (bf16[128,512]{1,0:T(8,128)(2,1)S(1)}, bf16[128,512]{1,0:T(8,128)(2,1)}, u32[]{:S(2)}, u32[]{:S(2)}) collective-permute-start(bf16[128,512]{1,0:T(8,128)(2,1)S(1)} %bitcast.166), channel_id=1, source_target_pairs={{0,3},{1,4},{2,5},{3,6},{4,7},{5,0},{6,1},{7,2},{8,11},{9,12},{10,... | collective-permute-start | bytes 393224 | tf_op jit(solution)/shard_map/ppermute | solution.py:128
  101.4 22.6 %collective-permute-start.3 = (bf16[128,512]{1,0:T(8,128)(2,1)S(1)}, bf16[128,512]{1,0:T(8,128)(2,1)}, u32[]{:S(2)}, u32[]{:S(2)}) collective-permute-start(bf16[128,512]{1,0:T(8,128)(2,1)S(1)} %bitcast.165), channel_id=1, source_target_pairs={{0,4},{1,5},{2,6},{3,7},{4,0},{5,1},{6,2},{7,3},{8,12},{9,13},{10,... | collective-permute-start | bytes 393224 | tf_op jit(solution)/shard_map/ppermute | solution.py:128
  106.5 22.5 %collective-permute-start.4 = (bf16[128,512]{1,0:T(8,128)(2,1)}, bf16[128,512]{1,0:T(8,128)(2,1)}, u32[]{:S(2)}, u32[]{:S(2)}) collective-permute-start(bf16[128,512]{1,0:T(8,128)(2,1)} %bitcast.18), channel_id=1, source_target_pairs={{0,5},{1,6},{2,7},{3,0},{4,1},{5,2},{6,3},{7,4},{8,13},{9,14},{10,... | collective-permute-start | bytes 393224 | tf_op jit(solution)/shard_map/ppermute | solution.py:128
  110.9 22.9 %copy-start.4 = (pred[8]{0:T(512)(128)(4,1)S(1)}, pred[8]{0:T(512)(128)(4,1)}, u32[]{:S(2)}) copy-start(pred[8]{0:T(512)(128)(4,1)} %copy-done.3) | copy-start | bytes 28
  110.9 19.7 %collective-permute-start.5 = (bf16[128,512]{1,0:T(8,128)(2,1)S(1)}, bf16[128,512]{1,0:T(8,128)(2,1)S(1)}, u32[]{:S(2)}, u32[]{:S(2)}) collective-permute-start(bf16[128,512]{1,0:T(8,128)(2,1)S(1)} %bitcast.164), channel_id=1, source_target_pairs={{0,6},{1,7},{2,0},{3,1},{4,2},{5,3},{6,4},{7,5},{8,14},{9,15},{10,... | collective-permute-start | bytes 393224 | tf_op jit(solution)/shard_map/ppermute | solution.py:128
  117.0 14.3 %collective-permute-start.6 = (bf16[128,512]{1,0:T(8,128)(2,1)S(1)}, bf16[128,512]{1,0:T(8,128)(2,1)S(1)}, u32[]{:S(2)}, u32[]{:S(2)}) collective-permute-start(bf16[128,512]{1,0:T(8,128)(2,1)S(1)} %bitcast.163), channel_id=1, source_target_pairs={{0,7},{1,0},{2,1},{3,2},{4,3},{5,4},{6,5},{7,6},{8,15},{9,8},{10,9... | collective-permute-start | bytes 393224 | tf_op jit(solution)/shard_map/ppermute | solution.py:128
  120.5 21.7 %collective-permute-start.15 = (bf16[1024,256]{1,0:T(8,128)(2,1)S(1)}, bf16[1024,256]{1,0:T(8,128)(2,1)S(1)}, u32[]{:S(2)}, u32[]{:S(2)}) collective-permute-start(bf16[1024,256]{1,0:T(8,128)(2,1)S(1)} %bitcast_select_fusion), channel_id=1, source_target_pairs={{0,8},{8,16},{16,24},{24,32},{32,40},{40,48},{48,56},{56,64},{64,7... | collective-permute-start | bytes 1572872 | tf_op jit(solution)/shard_map/ppermute | solution.py:25
  124.0 17.9 %collective-permute-start.14 = (bf16[256,256]{1,0:T(8,128)(2,1)}, bf16[256,256]{1,0:T(8,128)(2,1)S(1)}, u32[]{:S(2)}, u32[]{:S(2)}) collective-permute-start(bf16[256,256]{1,0:T(8,128)(2,1)} %bitcast.176), channel_id=1, source_target_pairs={{0,16},{8,24},{16,32},{24,40},{32,48},{40,56},{48,64},{56,72},{64,... | collective-permute-start | bytes 393224 | tf_op jit(solution)/shard_map/ppermute | solution.py:25
  169.4 44.1 %collective-permute-start.30 = (bf16[128,512]{1,0:T(8,128)(2,1)S(1)}, bf16[128,512]{1,0:T(8,128)(2,1)}, u32[]{:S(2)}, u32[]{:S(2)}) collective-permute-start(bf16[128,512]{1,0:T(8,128)(2,1)S(1)} %get-tuple-element.36), channel_id=1, source_target_pairs={{0,1},{1,2},{2,3},{3,4},{4,5},{5,6},{6,7},{7,0},{8,9},{9,10},{10,1... | collective-permute-start | bytes 393224 | tf_op jit(solution)/shard_map/ppermute | solution.py:128
  173.9 45.0 %collective-permute-start.31 = (bf16[128,512]{1,0:T(8,128)(2,1)S(1)}, bf16[128,512]{1,0:T(8,128)(2,1)}, u32[]{:S(2)}, u32[]{:S(2)}) collective-permute-start(bf16[128,512]{1,0:T(8,128)(2,1)S(1)} %get-tuple-element.35), channel_id=1, source_target_pairs={{0,2},{1,3},{2,4},{3,5},{4,6},{5,7},{6,0},{7,1},{8,10},{9,11},{10,... | collective-permute-start | bytes 393224 | tf_op jit(solution)/shard_map/ppermute | solution.py:128
  175.9 46.0 %collective-permute-start.32 = (bf16[128,512]{1,0:T(8,128)(2,1)S(1)}, bf16[128,512]{1,0:T(8,128)(2,1)}, u32[]{:S(2)}, u32[]{:S(2)}) collective-permute-start(bf16[128,512]{1,0:T(8,128)(2,1)S(1)} %get-tuple-element.34), channel_id=1, source_target_pairs={{0,3},{1,4},{2,5},{3,6},{4,7},{5,0},{6,1},{7,2},{8,11},{9,12},{10,... | collective-permute-start | bytes 393224 | tf_op jit(solution)/shard_map/ppermute | solution.py:128
  179.3 47.4 %collective-permute-start.33 = (bf16[128,512]{1,0:T(8,128)(2,1)S(1)}, bf16[128,512]{1,0:T(8,128)(2,1)}, u32[]{:S(2)}, u32[]{:S(2)}) collective-permute-start(bf16[128,512]{1,0:T(8,128)(2,1)S(1)} %get-tuple-element.33), channel_id=1, source_target_pairs={{0,4},{1,5},{2,6},{3,7},{4,0},{5,1},{6,2},{7,3},{8,12},{9,13},{10,... | collective-permute-start | bytes 393224 | tf_op jit(solution)/shard_map/ppermute | solution.py:128
  183.8 46.5 %collective-permute-start.34 = (bf16[128,512]{1,0:T(8,128)(2,1)S(1)}, bf16[128,512]{1,0:T(8,128)(2,1)S(1)}, u32[]{:S(2)}, u32[]{:S(2)}) collective-permute-start(bf16[128,512]{1,0:T(8,128)(2,1)S(1)} %get-tuple-element.32), channel_id=1, source_target_pairs={{0,5},{1,6},{2,7},{3,0},{4,1},{5,2},{6,3},{7,4},{8,13},{9,14},{10,... | collective-permute-start | bytes 393224 | tf_op jit(solution)/shard_map/ppermute | solution.py:128
  213.6 20.2 %collective-permute-start.35 = (bf16[128,512]{1,0:T(8,128)(2,1)S(1)}, bf16[128,512]{1,0:T(8,128)(2,1)S(1)}, u32[]{:S(2)}, u32[]{:S(2)}) collective-permute-start(bf16[128,512]{1,0:T(8,128)(2,1)S(1)} %get-tuple-element.31), channel_id=1, source_target_pairs={{0,6},{1,7},{2,0},{3,1},{4,2},{5,3},{6,4},{7,5},{8,14},{9,15},{10,... | collective-permute-start | bytes 393224 | tf_op jit(solution)/shard_map/ppermute | solution.py:128
  219.0 20.0 %collective-permute-start.36 = (bf16[128,512]{1,0:T(8,128)(2,1)S(1)}, bf16[128,512]{1,0:T(8,128)(2,1)S(1)}, u32[]{:S(2)}, u32[]{:S(2)}) collective-permute-start(bf16[128,512]{1,0:T(8,128)(2,1)S(1)} %get-tuple-element.30), channel_id=1, source_target_pairs={{0,7},{1,0},{2,1},{3,2},{4,3},{5,4},{6,5},{7,6},{8,15},{9,8},{10,9... | collective-permute-start | bytes 393224 | tf_op jit(solution)/shard_map/ppermute | solution.py:128
  221.9 21.5 %collective-permute-start.16 = (bf16[128,512]{1,0:T(8,128)(2,1)}, bf16[128,512]{1,0:T(8,128)(2,1)}, u32[]{:S(2)}, u32[]{:S(2)}) collective-permute-start(bf16[128,512]{1,0:T(8,128)(2,1)} %get-tuple-element.20), channel_id=1, source_target_pairs={{0,1},{1,2},{2,3},{3,4},{4,5},{5,6},{6,7},{7,0},{8,9},{9,10},{10,1... | collective-permute-start | bytes 393224 | tf_op jit(solution)/shard_map/ppermute | solution.py:128
  226.7 22.1 %collective-permute-start.17 = (bf16[128,512]{1,0:T(8,128)(2,1)}, bf16[128,512]{1,0:T(8,128)(2,1)}, u32[]{:S(2)}, u32[]{:S(2)}) collective-permute-start(bf16[128,512]{1,0:T(8,128)(2,1)} %get-tuple-element.19), channel_id=1, source_target_pairs={{0,2},{1,3},{2,4},{3,5},{4,6},{5,7},{6,0},{7,1},{8,10},{9,11},{10,... | collective-permute-start | bytes 393224 | tf_op jit(solution)/shard_map/ppermute | solution.py:128
  230.4 21.5 %collective-permute-start.18 = (bf16[128,512]{1,0:T(8,128)(2,1)}, bf16[128,512]{1,0:T(8,128)(2,1)}, u32[]{:S(2)}, u32[]{:S(2)}) collective-permute-start(bf16[128,512]{1,0:T(8,128)(2,1)} %get-tuple-element.18), channel_id=1, source_target_pairs={{0,3},{1,4},{2,5},{3,6},{4,7},{5,0},{6,1},{7,2},{8,11},{9,12},{10,... | collective-permute-start | bytes 393224 | tf_op jit(solution)/shard_map/ppermute | solution.py:128
  233.8 19.0 %collective-permute-start.19 = (bf16[128,512]{1,0:T(8,128)(2,1)}, bf16[128,512]{1,0:T(8,128)(2,1)}, u32[]{:S(2)}, u32[]{:S(2)}) collective-permute-start(bf16[128,512]{1,0:T(8,128)(2,1)} %get-tuple-element.17), channel_id=1, source_target_pairs={{0,4},{1,5},{2,6},{3,7},{4,0},{5,1},{6,2},{7,3},{8,12},{9,13},{10,... | collective-permute-start | bytes 393224 | tf_op jit(solution)/shard_map/ppermute | solution.py:128
  239.0 14.7 %collective-permute-start.20 = (bf16[128,512]{1,0:T(8,128)(2,1)S(1)}, bf16[128,512]{1,0:T(8,128)(2,1)}, u32[]{:S(2)}, u32[]{:S(2)}) collective-permute-start(bf16[128,512]{1,0:T(8,128)(2,1)S(1)} %get-tuple-element.16), channel_id=1, source_target_pairs={{0,5},{1,6},{2,7},{3,0},{4,1},{5,2},{6,3},{7,4},{8,13},{9,14},{10,... | collective-permute-start | bytes 393224 | tf_op jit(solution)/shard_map/ppermute | solution.py:128
  243.3 11.3 %collective-permute-start.21 = (bf16[128,512]{1,0:T(8,128)(2,1)S(1)}, bf16[128,512]{1,0:T(8,128)(2,1)S(1)}, u32[]{:S(2)}, u32[]{:S(2)}) collective-permute-start(bf16[128,512]{1,0:T(8,128)(2,1)S(1)} %get-tuple-element.15), channel_id=1, source_target_pairs={{0,6},{1,7},{2,0},{3,1},{4,2},{5,3},{6,4},{7,5},{8,14},{9,15},{10,... | collective-permute-start | bytes 393224 | tf_op jit(solution)/shard_map/ppermute | solution.py:128
  248.8 6.9 %collective-permute-start.22 = (bf16[128,512]{1,0:T(8,128)(2,1)S(1)}, bf16[128,512]{1,0:T(8,128)(2,1)S(1)}, u32[]{:S(2)}, u32[]{:S(2)}) collective-permute-start(bf16[128,512]{1,0:T(8,128)(2,1)S(1)} %get-tuple-element.14), channel_id=1, source_target_pairs={{0,7},{1,0},{2,1},{3,2},{4,3},{5,4},{6,5},{7,6},{8,15},{9,8},{10,9... | collective-permute-start | bytes 393224 | tf_op jit(solution)/shard_map/ppermute | solution.py:128

commit v4 on v2

--- a/solution.py
+++ b/solution.py
@@ -106,7 +106,7 @@
             pltpu.VMEM((heads, BLOCK, HD), jnp.float32),
         ],
     )
-    flops = 4 * rows * keys.shape[0] // 2 * HD * heads
+    flops = 40 * rows * keys.shape[0] // 2 * HD * heads
     return pl.pallas_call(
         functools.partial(attend_kernel, heads=heads),
         out_shape=jax.ShapeDtypeStruct((rows, width), queries.dtype),
@@ -117,16 +117,25 @@
     )(nback, queries, keys, values, qids, kids)
 
 
+SPLIT = 2
+
+
 def shards(queries, keys, values, doc_ids):
     range_rows = QBLK_DEV * BLOCK
     rows = queries.shape[0]
-    heads_axis = lax.axis_size("head")
+    n_head = lax.axis_size("head")
     ctx_pos = lax.axis_index("ctx")
-    paired = jnp.concatenate(
-        [keys.reshape(rows, heads_axis, -1), values.reshape(rows, heads_axis, -1)], axis=2)
-    local_pair = lax.all_to_all(paired, "head", split_axis=1, concat_axis=0, tiled=True)
-    local_queries = lax.all_to_all(queries, "head", split_axis=1, concat_axis=0, tiled=True)
-    local_pair = local_pair.reshape(range_rows, 2 * HD)
+    part = (QH // KVH) // SPLIT
+    grouped_q = queries.reshape(rows, n_head, SPLIT, part * HD)
+    first = jnp.concatenate(
+        [keys.reshape(rows, n_head, HD), values.reshape(rows, n_head, HD), grouped_q[:, :, 0]], axis=2)
+    first = lax.all_to_all(first, "head", split_axis=1, concat_axis=0, tiled=True)
+    first = first.reshape(range_rows, 2 * HD + part * HD)
+    local_pair = first[:, :2 * HD]
+    local_qs = [first[:, 2 * HD:]]
+    for s in range(1, SPLIT):
+        got = lax.all_to_all(grouped_q[:, :, s], "head", split_axis=1, concat_axis=0, tiled=True)
+        local_qs.append(got.reshape(range_rows, part * HD))
     prev1 = from_behind(local_pair, "ctx", 1)
     prev2 = from_behind(local_pair[range_rows - BLOCK:], "ctx", 2)
     window = jnp.concatenate([prev2, prev1, local_pair], axis=0)
@@ -144,10 +153,22 @@
         back = tile_last[lo:base + qb]
         counts.append(jnp.sum((back == first_q[qb]).astype(jnp.int32)))
     nback = jnp.stack(counts)
-    local_out = attend(
-        nback, local_queries, window[:, :HD], window[:, HD:],
-        range_ids.reshape(range_rows, 1), window_ids.reshape(1, -1))
-    return lax.all_to_all(local_out, "head", split_axis=0, concat_axis=1, tiled=True)
+    qids = range_ids.reshape(range_rows, 1)
+    kids = window_ids.reshape(1, -1)
+    window_keys, window_values = window[:, :HD], window[:, HD:]
+    outs = []
+    local_out = None
+    for s in range(SPLIT):
+        q_s = local_qs[s]
+        if local_out is not None:
+            outs.append(lax.all_to_all(
+                local_out.reshape(range_rows, 1, part * HD), "head", split_axis=0, concat_axis=1, tiled=True))
+            q_s, _ = lax.optimization_barrier((q_s, local_out))
+        local_out = attend(nback, q_s, window_keys, window_values, qids, kids)
+    outs.append(lax.all_to_all(
+        local_out.reshape(range_rows, 1, part * HD), "head", split_axis=0, concat_axis=1, tiled=True))
+    full = jnp.stack(outs, axis=2)
+    return full.reshape(rows, QH * HD)
 
 
 def solution(mesh):

time: 129 us -> 170 us (1.32)
  the two profiles are of different devices: /device:TPU:128 before, /device:TPU:409 now
where the time goes in v4:
time: 170 us; the launch traced here: 169 us
  Pallas kernels  49.4 us (29%)
  local copies, waits for them, and re-layouts  35.7 us (21%)
  blocking collectives  25.4 us (15%)
  waiting for transfers between devices  24.1 us (14%)
  starting transfers between devices  21.3 us (13%)
  other arithmetic  12.6 us (7%)
    pallas_call x2, Pallas kernels, attend(): pl.pallas_call(functools.partial(attend_kernel, heads=heads), out_shape=j...  49.4 us
    all_to_all x1, blocking collectives, shards(): lax.all_to_all(first, 'head', split_axis=1, concat_axis=0, tiled=True)  25.4 us
    all_to_all x2, waiting for transfers between devices, shards(): lax.all_to_all(local_out.reshape(range_rows, 1, part * HD), 'head', split...  24 us
    unnamed x16, local copies, waits for them, and re-layouts  13.3 us
    all_to_all x2, starting transfers between devices, shards(): lax.all_to_all(local_out.reshape(range_rows, 1, part * HD), 'head', split...  9.28 us
    ppermute x2, starting transfers between devices, from_behind(): lax.ppermute(value, axis, [(source, source + steps) for source in range(l...  8.46 us
    slice x1, local copies, waits for them, and re-layouts, shards(): grouped_q[:, :, 0]  4.69 us
    reshape x2, other arithmetic, shards(): local_out.reshape(range_rows, 1, part * HD)  4.07 us
  transfers between devices with their start and end apart: 5, of which 2 were waited for; matrix products, arithmetic and copies ran while one was open for 13% of the time, Pallas kernels for 15%

profile of v4, /device:TPU:409, one launch (start us, length us, event | category | flops | bytes accessed | tf_op | source)
XLA Modules:
  0.0 168.6 jit_solution(9657250932273088798)
XLA Ops:
  0.0 0.0 copy-start
  0.0 3.3 %reshape.68 = bf16[128,8,2,512]{3,2,1,0:T(2,128)(2,1)S(1)} reshape(bf16[128,8192]{1,0:T(8,128)(2,1)} %param.4) | data formatting | bytes 4194304 | tf_op jit(solution)/shard_map/reshape | solution.py:129
  3.3 4.7 %fusion = (bf16[128,8,1,512]{3,2,1,0:T(2,128)(2,1)S(1)}, bf16[128,8,1,512]{3,2,1,0:T(2,128)(2,1)S(1)}) fusion(bf16[128,8,2,512]{3,2,1,0:T(2,128)(2,1)S(1)} %reshape.68), kind=kLoop, calls=%fused_computation.17 | loop fusion | bytes 4194304 | tf_op jit(solution)/shard_map/slice | solution.py:131
  8.0 0.0 copy-start.3
  8.1 1.1 copy.83
  9.2 0.0 copy-done
  9.2 0.0 copy-done.3
  9.2 0.1 copy_bitcast_fusion.2
  9.3 0.1 pad_maximum_fusion.1
  9.5 25.4 %all_to_all.60 = bf16[128,8,768]{2,0,1:T(8,128)(2,1)S(1)} all-to-all(bf16[128,8,768]{2,0,1:T(8,128)(2,1)S(1)} %pad_maximum_fusion.1), channel_id=1, replica_groups=mesh['ctx'=64,'head'=8] {'head'}, dimensions={1} | all-to-all | bytes 3145728 | tf_op jit(solution)/shard_map/all_to_all | solution.py:132
  34.9 6.2 %collective-permute-start.1 = (bf16[1024,256]{1,0:T(8,128)(2,1)S(1)}, bf16[1024,256]{1,0:T(8,128)(2,1)}, u32[]{:S(2)}, u32[]{:S(2)}) collective-permute-start(bf16[1024,256]{1,0:T(8,128)(2,1)S(1)} %slice.90), channel_id=1, source_target_pairs={{0,8},{8,16},{16,24},{24,32},{32,40},{40,48},{48,56},{56,64},{64,7... | collective-permute-start | bytes 1572872 | tf_op jit(solution)/shard_map/ppermute | solution.py:25
  41.0 2.1 %copy.82 = bf16[128,8,1,512]{3,0,1,2:T(8,128)(2,1)} copy(bf16[128,8,1,512]{3,2,1,0:T(2,128)(2,1)S(1)} %get-tuple-element.12) | data formatting | bytes 2097152
  43.1 3.6 %all-to-all-start.2 = ((bf16[128,8,512]{2,0,1:T(8,128)(2,1)}), bf16[128,8,512]{2,0,1:T(8,128)(2,1)S(1)}, u32[]{:S(2)}, u32[]{:S(2)}) async-start(bf16[128,8,512]{2,0,1:T(8,128)(2,1)} %bitcast.42), calls=%async_computation.2 | async-start | bytes 2097152 | tf_op jit(solution)/shard_map/all_to_all | solution.py:137
  46.7 0.8 pad_dynamic-slice_fusion
  47.5 0.6 reshape.64
  48.1 0.7 dynamic_slice.7
  48.8 0.6 fusion.2
  49.4 0.7 slice.89
  50.1 2.3 %collective-permute-start = (bf16[256,256]{1,0:T(8,128)(2,1)}, bf16[256,256]{1,0:T(8,128)(2,1)S(1)}, u32[]{:S(2)}, u32[]{:S(2)}) collective-permute-start(bf16[256,256]{1,0:T(8,128)(2,1)} %slice.89), channel_id=1, source_target_pairs={{0,16},{8,24},{16,32},{24,40},{32,48},{40,56},{48,64},{56,72},{64,... | collective-permute-start | bytes 393224 | tf_op jit(solution)/shard_map/ppermute | solution.py:25
  52.4 4.1 %convert_reduce_fusion.3 = (s32[]{:T(128)}, s32[]{:T(128)}, s32[]{:T(128)}, s32[]{:T(128)}) fusion(s32[9,256]{1,0:T(8,128)} %reshape.64, s32[]{:T(128)} %bitcast, s32[]{:T(128)} %bitcast.6, s32[]{:T(128)} %bitcast.4, s32[]{:T(128)} %bitcast.2), kind=kLoop, calls=%fused_computation.15 | loop fusion | flops 56 | bytes 112 | tf_op jit(solution)/shard_map/reduce_sum | solution.py:154
  56.4 0.6 reshape.71.kid_ref
  57.0 1.0 copy.61.qid_ref
  58.0 3.0 %pad_add_fusion.nback_ref = s32[4]{0:T(128)} fusion(s32[1]{0:T(128)} %bitcast.7, s32[1]{0:T(128)} %bitcast.5, s32[1]{0:T(128)} %bitcast.3, s32[1]{0:T(128)} %bitcast.1), kind=kLoop, calls=%fused_computation.16 | loop fusion | flops 12 | bytes 32 | tf_op jit(solution)/shard_map/stack | solution.py:155
  61.1 1.1 slice.88.q_ref
  62.2 0.0 collective-permute-done
  62.2 0.0 collective-permute-done.1
  62.2 1.1 pad_maximum_fusion.2
  63.3 1.1 fusion.1
  64.5 24.7 %shard_map.46 = bf16[1024,512]{1,0:T(8,128)(2,1)} custom-call(s32[4]{0:T(128)} %pad_add_fusion.nback_ref, bf16[1024,512]{1,0:T(8,128)(2,1)} %slice.88.q_ref, bf16[2304,128]{1,0:T(8,128)(2,1)} %get-tuple-element.14.k_ref, bf16[2304,128]{1,0:T(8,128)(2,1)} %get-tuple-element.13.v_ref, s32[1024,1]{1,0:T(8,128)} %copy.61.qid_ref, s32[1,2304]{1,0:T(1,128)} %reshape.71.kid_ref), custom_call_target="tpu_custom_call" | custom-call | flops 24159191040 | bytes 2097152 | tf_op jit(solution)/shard_map/pallas_call | solution.py:110
  89.2 0.0 all-to-all-done.2
  89.2 0.0 copy-start.2
  89.2 1.0 copy-done.2
  90.1 24.7 %shard_map.47 = bf16[1024,512]{1,0:T(8,128)(2,1)} custom-call(s32[4]{0:T(128)} %pad_add_fusion.nback_ref, bf16[1024,512]{1,0:T(8,128)(2,1)} %bitcast.53, bf16[2304,128]{1,0:T(8,128)(2,1)} %get-tuple-element.14.k_ref, bf16[2304,128]{1,0:T(8,128)(2,1)} %get-tuple-element.13.v_ref, s32[1024,1]{1,0:T(8,128)} %copy.61.qid_ref, s32[1,2304]{1,0:T(1,128)} %reshape.71.kid_ref), custom_call_target="tpu_custom_call" | custom-call | flops 24159191040 | bytes 2097152 | tf_op jit(solution)/shard_map/pallas_call | solution.py:110
  114.8 0.5 broadcast.10
  115.3 2.6 %reduce.4 = bf16[1024,512]{1,0:T(8,128)(2,1)S(1)} reduce(bf16[1024,1,512]{2,0,1:T(8,128)(2,1)} %bitcast.52, bf16[]{:T(256)} %broadcast.10), dimensions={1}, to_apply=%copy.65.reduce_sub_computation | reduce | bytes 2097154 | tf_op jit(solution)/shard_map/reshape | solution.py:169
  118.0 0.0 copy-start.1
  118.0 1.6 reshape.76
  119.6 5.1 %all-to-all-start.3 = ((bf16[8,2,32768]{2,1,0:T(2,128)(2,1)}), bf16[8,2,32768]{2,1,0:T(2,128)(2,1)S(1)}, u32[]{:S(2)}, u32[]{:S(2)}) async-start(bf16[8,2,32768]{2,1,0:T(2,128)(2,1)} %reshape.76), calls=%async_computation.3 | async-start | bytes 2097152 | tf_op jit(solution)/shard_map/all_to_all | solution.py:168
  124.6 0.0 copy-done.1
  124.6 1.4 reduce.5
  126.1 1.6 reshape.78
  127.7 10.5 %all-to-all-done.3 = bf16[8,2,32768]{2,1,0:T(2,128)(2,1)S(1)} async-done(((bf16[8,2,32768]{2,1,0:T(2,128)(2,1)}), bf16[8,2,32768]{2,1,0:T(2,128)(2,1)S(1)}, u32[]{:S(2)}, u32[]{:S(2)}) %all-to-all-start.3) | async-done | bytes 1048608 | tf_op jit(solution)/shard_map/all_to_all | solution.py:168
  138.2 4.2 %all-to-all-start.1 = ((bf16[8,2,32768]{2,1,0:T(2,128)(2,1)}), bf16[8,2,32768]{2,1,0:T(2,128)(2,1)}, u32[]{:S(2)}, u32[]{:S(2)}) async-start(bf16[8,2,32768]{2,1,0:T(2,128)(2,1)} %reshape.78), calls=%async_computation.1 | async-start | bytes 2097152 | tf_op jit(solution)/shard_map/all_to_all | solution.py:164
  142.4 1.1 reshape.77
  143.5 0.3 copy.69
  143.8 13.5 %all-to-all-done.1 = bf16[8,2,32768]{2,1,0:T(2,128)(2,1)} async-done(((bf16[8,2,32768]{2,1,0:T(2,128)(2,1)}), bf16[8,2,32768]{2,1,0:T(2,128)(2,1)}, u32[]{:S(2)}, u32[]{:S(2)}) %all-to-all-start.1) | async-done | bytes 1048608 | tf_op jit(solution)/shard_map/all_to_all | solution.py:164
  157.3 4.3 %reshape.79 = bf16[1024,1,512]{2,1,0:T(2,128)(2,1)S(1)} reshape(bf16[8,2,32768]{2,1,0:T(2,128)(2,1)} %all-to-all-done.1) | data formatting | bytes 2097152
  161.6 0.3 copy.68
  161.9 0.2 pad_maximum_fusion
  162.1 2.4 %copy.66 = bf16[128,8,2,512]{0,3,2,1:T(8,128)(2,1)} copy(bf16[128,8,2,512]{3,0,1,2:T(8,128)(2,1)S(1)} %pad_maximum_fusion) | data formatting | bytes 4194304 | tf_op jit(solution)/shard_map/stack | solution.py:170
  164.5 4.1 %copy.67 = bf16[128,8192]{1,0:T(8,128)(2,1)} copy(bf16[128,8192]{0,1:T(8,128)(2,1)} %bitcast.44) | data formatting | bytes 4194304 | tf_op jit(solution)/shard_map/reshape | solution.py:171
  (2 shorter events, 0.0 us)
Async XLA Ops:
  0.0 9.2 %copy-start = (bf16[128,1024]{1,0:T(8,128)(2,1)S(1)}, bf16[128,1024]{1,0:T(8,128)(2,1)}, u32[]{:S(2)}) copy-start(bf16[128,1024]{1,0:T(8,128)(2,1)} %param.5) | copy-start | bytes 786436
  8.0 1.2 copy-start.3
  34.9 27.3 %collective-permute-start.1 = (bf16[1024,256]{1,0:T(8,128)(2,1)S(1)}, bf16[1024,256]{1,0:T(8,128)(2,1)}, u32[]{:S(2)}, u32[]{:S(2)}) collective-permute-start(bf16[1024,256]{1,0:T(8,128)(2,1)S(1)} %slice.90), channel_id=1, source_target_pairs={{0,8},{8,16},{16,24},{24,32},{32,40},{40,48},{48,56},{56,64},{64,7... | collective-permute-start | bytes 1572872 | tf_op jit(solution)/shard_map/ppermute | solution.py:25
  43.1 46.0 %all-to-all-start.2 = ((bf16[128,8,512]{2,0,1:T(8,128)(2,1)}), bf16[128,8,512]{2,0,1:T(8,128)(2,1)S(1)}, u32[]{:S(2)}, u32[]{:S(2)}) async-start(bf16[128,8,512]{2,0,1:T(8,128)(2,1)} %bitcast.42), calls=%async_computation.2 | async-start | bytes 2097152 | tf_op jit(solution)/shard_map/all_to_all | solution.py:137
  50.1 12.1 %collective-permute-start = (bf16[256,256]{1,0:T(8,128)(2,1)}, bf16[256,256]{1,0:T(8,128)(2,1)S(1)}, u32[]{:S(2)}, u32[]{:S(2)}) collective-permute-start(bf16[256,256]{1,0:T(8,128)(2,1)} %slice.89), channel_id=1, source_target_pairs={{0,16},{8,24},{16,32},{24,40},{32,48},{40,56},{48,64},{56,72},{64,... | collective-permute-start | bytes 393224 | tf_op jit(solution)/shard_map/ppermute | solution.py:25
  89.2 1.0 copy-start.2
  118.0 6.7 %copy-start.1 = (bf16[1024,512]{1,0:T(8,128)(2,1)S(1)}, bf16[1024,512]{1,0:T(8,128)(2,1)}, u32[]{:S(2)}) copy-start(bf16[1024,512]{1,0:T(8,128)(2,1)} %shard_map.46) | copy-start | bytes 3145732
  119.6 18.6 %all-to-all-start.3 = ((bf16[8,2,32768]{2,1,0:T(2,128)(2,1)}), bf16[8,2,32768]{2,1,0:T(2,128)(2,1)S(1)}, u32[]{:S(2)}, u32[]{:S(2)}) async-start(bf16[8,2,32768]{2,1,0:T(2,128)(2,1)} %reshape.76), calls=%async_computation.3 | async-start | bytes 2097152 | tf_op jit(solution)/shard_map/all_to_all | solution.py:168
  138.2 19.1 %all-to-all-start.1 = ((bf16[8,2,32768]{2,1,0:T(2,128)(2,1)}), bf16[8,2,32768]{2,1,0:T(2,128)(2,1)}, u32[]{:S(2)}, u32[]{:S(2)}) async-start(bf16[8,2,32768]{2,1,0:T(2,128)(2,1)} %reshape.78), calls=%async_computation.1 | async-start | bytes 2097152 | tf_op jit(solution)/shard_map/all_to_all | solution.py:164

commit v5 on v2

--- a/solution.py
+++ b/solution.py
@@ -14,6 +14,7 @@
 DOC_BLOCKS = 5
 QBLK_DEV = 4
 PREV = 2
+MXU_SUM = True
 
 
 floor_score = -1e30
@@ -32,7 +33,7 @@
     return jnp.concatenate(pieces[::-1] + [paired], axis=1)
 
 
-def attend_kernel(nback_ref, q_ref, k_ref, v_ref, qid_ref, kid_ref, o_ref, m_scr, l_scr, acc_scr, *, heads):
+def attend_kernel(nback_ref, full_ref, q_ref, k_ref, v_ref, qid_ref, kid_ref, o_ref, m_scr, l_scr, acc_scr, *, heads, n_steps, mxu_sum):
     qb = pl.program_id(0)
     step = pl.program_id(1)
     last = pl.num_programs(1) - 1
@@ -40,12 +41,15 @@
     @pl.when(step == 0)
     def _init():
         m_scr[...] = jnp.full(m_scr.shape, floor_score, jnp.float32)
-        l_scr[...] = jnp.zeros(l_scr.shape, jnp.float32)
+        if not mxu_sum:
+            l_scr[...] = jnp.zeros(l_scr.shape, jnp.float32)
         acc_scr[...] = jnp.zeros(acc_scr.shape, jnp.float32)
 
     def body(masked):
         k = k_ref[...]
         v = v_ref[...]
+        if mxu_sum:
+            v = jnp.concatenate([v, jnp.ones_like(v)], axis=1)
         if masked:
             allowed = qid_ref[...] == kid_ref[...]
             rows = lax.broadcasted_iota(jnp.int32, (BLOCK, BLOCK), 0)
@@ -61,60 +65,74 @@
             m_new = jnp.maximum(m_old, jnp.max(s, axis=-1, keepdims=True))
             factor = jnp.exp(m_old - m_new)
             p = jnp.exp(s - jnp.tile(m_new, (1, BLOCK // 128)))
-            l_scr[j] = l_scr[j] * factor + jnp.sum(p, axis=-1, keepdims=True)
-            acc_scr[j] = acc_scr[j] * factor + jnp.dot(
-                p.astype(jnp.bfloat16), v, preferred_element_type=jnp.float32)
+            pv = jnp.dot(p.astype(jnp.bfloat16), v, preferred_element_type=jnp.float32)
+            if mxu_sum:
+                acc_scr[j] = acc_scr[j] * jnp.tile(factor, (1, 2)) + pv
+            else:
+                l_scr[j] = l_scr[j] * factor + jnp.sum(p, axis=-1, keepdims=True)
+                acc_scr[j] = acc_scr[j] * factor + pv
             m_scr[j] = m_new
 
-    @pl.when(step <= nback_ref[qb])
-    def _compute():
+    live = step <= nback_ref[qb]
+    full = full_ref[qb * n_steps + step] > 0
+
+    @pl.when(live & full)
+    def _plain():
+        body(False)
+
+    @pl.when(live & jnp.logical_not(full))
+    def _masked():
         body(True)
 
     @pl.when(step == last)
     def _finish():
         for j in range(heads):
-            o_ref[:, j * HD:(j + 1) * HD] = (acc_scr[j] / l_scr[j]).astype(o_ref.dtype)
+            if mxu_sum:
+                total = acc_scr[j, :, HD:]
+                o_ref[:, j * HD:(j + 1) * HD] = (acc_scr[j, :, :HD] / total).astype(o_ref.dtype)
+            else:
+                o_ref[:, j * HD:(j + 1) * HD] = (acc_scr[j] / l_scr[j]).astype(o_ref.dtype)
 
 
-def attend(nback, queries, keys, values, qids, kids):
+def attend(nback, full, queries, keys, values, qids, kids, mxu_sum=MXU_SUM):
     rows, width = queries.shape
     heads = width // HD
     n_q = rows // BLOCK
     base = keys.shape[0] // BLOCK - n_q
     n_steps = DOC_BLOCKS + 1
 
-    def kv_map(qb, step, nback_ref):
+    def kv_map(qb, step, nback_ref, full_ref):
         return (base + qb - jnp.minimum(step, nback_ref[qb]), 0)
 
-    def kid_map(qb, step, nback_ref):
+    def kid_map(qb, step, nback_ref, full_ref):
         return (0, base + qb - jnp.minimum(step, nback_ref[qb]))
 
     grid_spec = pltpu.PrefetchScalarGridSpec(
-        num_scalar_prefetch=1,
+        num_scalar_prefetch=2,
         grid=(n_q, n_steps),
         in_specs=[
-            pl.BlockSpec((BLOCK, width), lambda qb, step, nb: (qb, 0)),
+            pl.BlockSpec((BLOCK, width), lambda qb, step, nb, fl: (qb, 0)),
             pl.BlockSpec((BLOCK, HD), kv_map),
             pl.BlockSpec((BLOCK, HD), kv_map),
-            pl.BlockSpec((BLOCK, 1), lambda qb, step, nb: (qb, 0)),
+            pl.BlockSpec((BLOCK, 1), lambda qb, step, nb, fl: (qb, 0)),
             pl.BlockSpec((1, BLOCK), kid_map),
         ],
-        out_specs=pl.BlockSpec((BLOCK, width), lambda qb, step, nb: (qb, 0)),
+        out_specs=pl.BlockSpec((BLOCK, width), lambda qb, step, nb, fl: (qb, 0)),
         scratch_shapes=[
             pltpu.VMEM((heads, BLOCK, 128), jnp.float32),
             pltpu.VMEM((heads, BLOCK, 128), jnp.float32),
-            pltpu.VMEM((heads, BLOCK, HD), jnp.float32),
+            pltpu.VMEM((heads, BLOCK, 2 * HD if mxu_sum else HD), jnp.float32),
         ],
     )
-    flops = 4 * rows * keys.shape[0] // 2 * HD * heads
+    flops = 40 * rows * keys.shape[0] // 2 * HD * heads
     return pl.pallas_call(
-        functools.partial(attend_kernel, heads=heads),
+        functools.partial(attend_kernel, heads=heads, n_steps=n_steps, mxu_sum=mxu_sum),
         out_shape=jax.ShapeDtypeStruct((rows, width), queries.dtype),
         grid_spec=grid_spec,
         compiler_params=pltpu.CompilerParams(dimension_semantics=("arbitrary", "arbitrary")),
         cost_estimate=pl.CostEstimate(
-            flops=flops, transcendentals=flops // (2 * HD), bytes_accessed=4 * rows * width),
-    )(nback, queries, keys, values, qids, kids)
+            flops=flops, transcendentals=flops // (20 * HD), bytes_accessed=4 * rows * width),
+    )(nback, full, queries, keys, values, qids, kids)
 
 
 def shards(queries, keys, values, doc_ids):
@@ -144,8 +162,19 @@
         back = tile_last[lo:base + qb]
         counts.append(jnp.sum((back == first_q[qb]).astype(jnp.int32)))
     nback = jnp.stack(counts)
+    tile_first = window_ids.reshape(-1, BLOCK)[:, 0]
+    last_q = range_ids.reshape(-1, BLOCK)[:, BLOCK - 1]
+    flags = []
+    for qb in range(n_q):
+        for step in range(DOC_BLOCKS + 1):
+            tile = base + qb - step
+            if step == 0 or tile < 0:
+                flags.append(jnp.zeros((), jnp.int32))
+            else:
+                flags.append((tile_first[tile] == last_q[qb]).astype(jnp.int32))
+    full = jnp.stack(flags)
     local_out = attend(
-        nback, local_queries, window[:, :HD], window[:, HD:],
+        nback, full, local_queries, window[:, :HD], window[:, HD:],
         range_ids.reshape(range_rows, 1), window_ids.reshape(1, -1))
     return lax.all_to_all(local_out, "head", split_axis=0, concat_axis=1, tiled=True)
 

time: 129 us -> 136 us (1.054)
  the two profiles are of different devices: /device:TPU:128 before, /device:TPU:185 now
where the time goes in v5:
time: 136 us; the launch traced here: 135 us
  Pallas kernels  30.5 us (22%)
  blocking collectives  30.5 us (22%)
  between operations  25.3 us (19%)
  starting transfers between devices  19.7 us (14%)
  local copies, waits for them, and re-layouts  12.2 us (9%)
  other arithmetic  8.7 us (6%)
  waiting for transfers between devices  7.61 us (6%)
    all_to_all x1, blocking collectives, shards(): lax.all_to_all(local_out, 'head', split_axis=0, concat_axis=1, tiled=True)  30.5 us
    pallas_call x1, Pallas kernels, attend(): pl.pallas_call(functools.partial(attend_kernel, heads=heads, n_steps=n_st...  30.5 us
    ppermute x2, starting transfers between devices, from_behind(): lax.ppermute(value, axis, [(source, source + steps) for source in range(l...  10.3 us
    all_to_all x1, waiting for transfers between devices, shards(): lax.all_to_all(paired, 'head', split_axis=1, concat_axis=0, tiled=True)  7.61 us
    all_to_all x1, starting transfers between devices, shards(): lax.all_to_all(paired, 'head', split_axis=1, concat_axis=0, tiled=True)  5.83 us
    reduce_sum x1, other arithmetic, shards(): counts.append(jnp.sum((back == first_q[qb]).astype(jnp.int32)))  4.22 us
    all_to_all x1, starting transfers between devices, shards(): lax.all_to_all(queries, 'head', split_axis=1, concat_axis=0, tiled=True)  3.61 us
    another operation x1, other arithmetic, shards(): nback = jnp.stack(counts)  3.05 us
  transfers between devices with their start and end apart: 4, of which 1 were waited for; matrix products, arithmetic and copies ran while one was open for 11% of the time, Pallas kernels for 0%

profile of v5, /device:TPU:185, one launch (start us, length us, event | category | flops | bytes accessed | tf_op | source)
XLA Modules:
  0.0 134.5 jit_solution(4516504453086480556)
XLA Ops:
  0.0 0.0 copy-start
  0.0 0.0 copy-start.1
  0.0 0.9 copy-done
  1.0 1.1 copy_bitcast_fusion.1
  2.0 0.9 pad_maximum_fusion.1
  2.9 5.8 %all-to-all-start.1 = ((bf16[128,8,256]{2,0,1:T(8,128)(2,1)}), bf16[128,8,256]{2,0,1:T(8,128)(2,1)S(1)}, u32[]{:S(2)}, u32[]{:S(2)}) async-start(bf16[128,8,256]{2,0,1:T(8,128)(2,1)} %pad_maximum_fusion.1), calls=%async_computation.1 | async-start | bytes 1048576 | tf_op jit(solution)/shard_map/all_to_all | solution.py:145
  8.7 0.0 copy-done.1
  8.7 1.6 %copy.39 = bf16[16,8,8,1024]{3,2,0,1:T(8,128)(2,1)} copy(bf16[16,8,8,1024]{3,2,1,0:T(8,128)(2,1)S(1)} %bitcast.60) | data formatting | bytes 4194304 | tf_op jit(solution)/shard_map/all_to_all | solution.py:146
  10.3 7.6 %all-to-all-done.1 = bf16[128,8,256]{2,0,1:T(8,128)(2,1)S(1)} async-done(((bf16[128,8,256]{2,0,1:T(8,128)(2,1)}), bf16[128,8,256]{2,0,1:T(8,128)(2,1)S(1)}, u32[]{:S(2)}, u32[]{:S(2)}) %all-to-all-start.1) | async-done | bytes 524320 | tf_op jit(solution)/shard_map/all_to_all | solution.py:145
  17.9 3.6 %all-to-all-start = ((bf16[128,8,1024]{2,0,1:T(8,128)(2,1)}), bf16[128,8,1024]{2,0,1:T(8,128)(2,1)S(1)}, u32[]{:S(2)}, u32[]{:S(2)}) async-start(bf16[128,8,1024]{2,0,1:T(8,128)(2,1)} %bitcast.55), calls=%async_computation | async-start | bytes 4194304 | tf_op jit(solution)/shard_map/all_to_all | solution.py:146
  21.5 7.1 %collective-permute-start.1 = (bf16[1024,256]{1,0:T(8,128)(2,1)S(1)}, bf16[1024,256]{1,0:T(8,128)(2,1)S(1)}, u32[]{:S(2)}, u32[]{:S(2)}) collective-permute-start(bf16[1024,256]{1,0:T(8,128)(2,1)S(1)} %bitcast.57), channel_id=1, source_target_pairs={{0,8},{8,16},{16,24},{24,32},{32,40},{40,48},{48,56},{56,64},{64,7... | collective-permute-start | bytes 1572872 | tf_op jit(solution)/shard_map/ppermute | solution.py:26
  28.6 0.8 pad_dynamic-slice_fusion
  29.4 0.0 copy-start.3
  29.4 0.7 dynamic_slice.7
  30.1 0.7 fusion.1
  30.8 0.7 slice.188
  31.5 0.0 copy-done.3
  31.5 3.2 %collective-permute-start = (bf16[256,256]{1,0:T(8,128)(2,1)}, bf16[256,256]{1,0:T(8,128)(2,1)S(1)}, u32[]{:S(2)}, u32[]{:S(2)}) collective-permute-start(bf16[256,256]{1,0:T(8,128)(2,1)} %bitcast.32), channel_id=1, source_target_pairs={{0,16},{8,24},{16,32},{24,40},{32,48},{40,56},{48,64},{56,72},{64,... | collective-permute-start | bytes 393224 | tf_op jit(solution)/shard_map/ppermute | solution.py:26
  34.7 4.2 %convert_reduce_fusion.3 = (s32[]{:T(128)}, s32[]{:T(128)}, s32[]{:T(128)}, s32[]{:T(128)}) fusion(s32[9,256]{1,0:T(8,128)} %copy-done.3, s32[]{:T(128)} %bitcast, s32[]{:T(128)} %bitcast.6, s32[]{:T(128)} %bitcast.4, s32[]{:T(128)} %bitcast.2), kind=kLoop, calls=%fused_computation.13 | loop fusion | flops 56 | bytes 112 | tf_op jit(solution)/shard_map/reduce_sum | solution.py:163
  61.6 0.6 reshape.145.kid_ref
  64.7 0.1 stack.125
  64.8 0.5 stack.126.full_ref
  65.3 1.0 copy.26.qid_ref
  66.3 3.1 %pad_add_fusion.nback_ref = s32[4]{0:T(128)} fusion(s32[1]{0:T(128)} %bitcast.7, s32[1]{0:T(128)} %bitcast.5, s32[1]{0:T(128)} %bitcast.3, s32[1]{0:T(128)} %bitcast.1), kind=kLoop, calls=%fused_computation.14 | loop fusion | flops 12 | bytes 32 | tf_op jit(solution)/shard_map/stack | solution.py:164
  69.4 0.0 collective-permute-done
  69.4 0.0 collective-permute-done.1
  69.4 0.1 pad_maximum_fusion
  69.5 1.1 fusion
  70.6 0.0 all-to-all-done
  70.6 0.0 copy-start.2
  70.6 1.3 copy-done.2
  71.9 30.5 %shard_map.46 = bf16[1024,1024]{1,0:T(8,128)(2,1)} custom-call(s32[4]{0:T(128)} %pad_add_fusion.nback_ref, s32[24]{0:T(128)} %stack.126.full_ref, bf16[1024,1024]{1,0:T(8,128)(2,1)} %bitcast.61, bf16[2304,128]{1,0:T(8,128)(2,1)} %get-tuple-element.10.k_ref, bf16[2304,128]{1,0:T(8,128)(2,1)} %get-tuple-element.9.v_ref, s32[1024,1]{1,0:T(8,128)} %copy.26.qid_ref, ...), custom_call_target="tpu_custom_call" | custom-call | flops 48318382080 | bytes 4194304 | tf_op jit(solution)/shard_map/pallas_call | solution.py:128
  102.4 30.5 %all_to_all.53 = bf16[8,128,1024]{2,1,0:T(8,128)(2,1)S(1)} all-to-all(bf16[8,128,1024]{2,1,0:T(8,128)(2,1)} %bitcast.62), channel_id=1, replica_groups=mesh['ctx'=64,'head'=8] {'head'}, dimensions={0} | all-to-all | bytes 4194304 | tf_op jit(solution)/shard_map/all_to_all | solution.py:179
  133.0 1.6 %copy.35 = bf16[8,16,8,1024]{3,2,0,1:T(8,128)(2,1)} copy(bf16[8,16,8,1024]{3,2,1,0:T(8,128)(2,1)S(1)} %bitcast.56) | data formatting | bytes 4194304 | tf_op jit(solution)/shard_map/all_to_all | solution.py:179
  (2 shorter events, 0.0 us)
Async XLA Ops:
  0.0 1.0 copy-start
  0.0 8.7 %copy-start.1 = (bf16[128,8192]{1,0:T(8,128)(2,1)S(1)}, bf16[128,8192]{1,0:T(8,128)(2,1)}, u32[]{:S(2)}) copy-start(bf16[128,8192]{1,0:T(8,128)(2,1)} %param.4) | copy-start | bytes 6291460
  2.9 15.0 %all-to-all-start.1 = ((bf16[128,8,256]{2,0,1:T(8,128)(2,1)}), bf16[128,8,256]{2,0,1:T(8,128)(2,1)S(1)}, u32[]{:S(2)}, u32[]{:S(2)}) async-start(bf16[128,8,256]{2,0,1:T(8,128)(2,1)} %pad_maximum_fusion.1), calls=%async_computation.1 | async-start | bytes 1048576 | tf_op jit(solution)/shard_map/all_to_all | solution.py:145
  17.9 52.7 %all-to-all-start = ((bf16[128,8,1024]{2,0,1:T(8,128)(2,1)}), bf16[128,8,1024]{2,0,1:T(8,128)(2,1)S(1)}, u32[]{:S(2)}, u32[]{:S(2)}) async-start(bf16[128,8,1024]{2,0,1:T(8,128)(2,1)} %bitcast.55), calls=%async_computation | async-start | bytes 4194304 | tf_op jit(solution)/shard_map/all_to_all | solution.py:146
  21.5 47.9 %collective-permute-start.1 = (bf16[1024,256]{1,0:T(8,128)(2,1)S(1)}, bf16[1024,256]{1,0:T(8,128)(2,1)S(1)}, u32[]{:S(2)}, u32[]{:S(2)}) collective-permute-start(bf16[1024,256]{1,0:T(8,128)(2,1)S(1)} %bitcast.57), channel_id=1, source_target_pairs={{0,8},{8,16},{16,24},{24,32},{32,40},{40,48},{48,56},{56,64},{64,7... | collective-permute-start | bytes 1572872 | tf_op jit(solution)/shard_map/ppermute | solution.py:26
  29.4 2.0 %copy-start.3 = (s32[9,256]{1,0:T(8,128)}, s32[9,256]{1,0:T(8,128)S(1)}, u32[]{:S(2)}) copy-start(s32[9,256]{1,0:T(8,128)S(1)} %reshape.139) | copy-start | bytes 27652
  31.5 37.9 %collective-permute-start = (bf16[256,256]{1,0:T(8,128)(2,1)}, bf16[256,256]{1,0:T(8,128)(2,1)S(1)}, u32[]{:S(2)}, u32[]{:S(2)}) collective-permute-start(bf16[256,256]{1,0:T(8,128)(2,1)} %bitcast.32), channel_id=1, source_target_pairs={{0,16},{8,24},{16,32},{24,40},{32,48},{40,56},{48,64},{56,72},{64,... | collective-permute-start | bytes 393224 | tf_op jit(solution)/shard_map/ppermute | solution.py:26
  70.6 1.3 copy-start.2

commit v6 on v5

--- a/solution.py
+++ b/solution.py
@@ -1,4 +1,6 @@
 import functools
+
+import numpy as np
 
 import jax
 import jax.numpy as jnp
@@ -149,30 +151,24 @@
     prev2 = from_behind(local_pair[range_rows - BLOCK:], "ctx", 2)
     window = jnp.concatenate([prev2, prev1, local_pair], axis=0)
     reach = BLOCK + range_rows
-    padded_ids = jnp.concatenate([jnp.full((reach,), -1, jnp.int32), doc_ids])
-    window_ids = lax.dynamic_slice_in_dim(padded_ids, ctx_pos * range_rows, reach + range_rows)
-    range_ids = lax.dynamic_slice_in_dim(doc_ids, ctx_pos * range_rows, range_rows)
+    n_q = range_rows // BLOCK
+    n_steps = DOC_BLOCKS + 1
+    base = reach // BLOCK
+    window_start = ctx_pos * range_rows - reach
+    positions = window_start + jnp.arange(reach + range_rows, dtype=jnp.int32)
+    window_ids = lax.dynamic_slice_in_dim(doc_ids, jnp.maximum(window_start, 0), reach + range_rows)
+    shift = jnp.minimum(window_start, 0)
+    window_ids = jnp.where(positions < 0, -1, jnp.roll(window_ids, -shift))
+    range_ids = window_ids[reach:]
+    tile_first = window_ids.reshape(-1, BLOCK)[:, 0]
     tile_last = window_ids.reshape(-1, BLOCK)[:, BLOCK - 1]
     first_q = range_ids.reshape(-1, BLOCK)[:, 0]
-    n_q = range_rows // BLOCK
-    base = reach // BLOCK
-    counts = []
-    for qb in range(n_q):
-        lo = max(0, base + qb - DOC_BLOCKS)
-        back = tile_last[lo:base + qb]
-        counts.append(jnp.sum((back == first_q[qb]).astype(jnp.int32)))
-    nback = jnp.stack(counts)
-    tile_first = window_ids.reshape(-1, BLOCK)[:, 0]
     last_q = range_ids.reshape(-1, BLOCK)[:, BLOCK - 1]
-    flags = []
-    for qb in range(n_q):
-        for step in range(DOC_BLOCKS + 1):
-            tile = base + qb - step
-            if step == 0 or tile < 0:
-                flags.append(jnp.zeros((), jnp.int32))
-            else:
-                flags.append((tile_first[tile] == last_q[qb]).astype(jnp.int32))
-    full = jnp.stack(flags)
+    steps = np.arange(n_steps)
+    tiles = base + np.arange(n_q)[:, None] - steps[None, :]
+    live = (tile_last[tiles] == first_q[:, None]) & (steps[None, :] > 0)
+    nback = jnp.sum(live.astype(jnp.int32), axis=1)
+    full = ((tile_first[tiles] == last_q[:, None]) & (steps[None, :] > 0)).astype(jnp.int32).reshape(-1)
     local_out = attend(
         nback, full, local_queries, window[:, :HD], window[:, HD:],
         range_ids.reshape(range_rows, 1), window_ids.reshape(1, -1))

time: 136 us -> 126 us (0.926)
  the two profiles are of different devices: /device:TPU:185 before, /device:TPU:128 now
where the time goes in v6:
time: 126 us; the launch traced here: 125 us
  blocking collectives  34.3 us (27%)
  waiting for transfers between devices  33 us (26%)
  Pallas kernels  26.6 us (21%)
  starting transfers between devices  15.2 us (12%)
  local copies, waits for them, and re-layouts  13.2 us (10%)
  other arithmetic  2.77 us (2%)
    all_to_all x1, blocking collectives, shards(): lax.all_to_all(local_out, 'head', split_axis=0, concat_axis=1, tiled=True)  34.3 us
    pallas_call x1, Pallas kernels, attend(): pl.pallas_call(functools.partial(attend_kernel, heads=heads, n_steps=n_st...  26.6 us
    all_to_all x1, waiting for transfers between devices, shards(): lax.all_to_all(queries, 'head', split_axis=1, concat_axis=0, tiled=True)  13.5 us
    ppermute x2, waiting for transfers between devices, from_behind(): lax.ppermute(value, axis, [(source, source + steps) for source in range(l...  11 us
    all_to_all x1, waiting for transfers between devices, shards(): lax.all_to_all(paired, 'head', split_axis=1, concat_axis=0, tiled=True)  8.52 us
    all_to_all x1, starting transfers between devices, shards(): lax.all_to_all(paired, 'head', split_axis=1, concat_axis=0, tiled=True)  6.11 us
    ppermute x2, starting transfers between devices, from_behind(): lax.ppermute(value, axis, [(source, source + steps) for source in range(l...  5.39 us
    all_to_all x1, starting transfers between devices, shards(): lax.all_to_all(queries, 'head', split_axis=1, concat_axis=0, tiled=True)  3.74 us
  transfers between devices with their start and end apart: 4, of which 4 were waited for; matrix products, arithmetic and copies ran while one was open for 8% of the time, Pallas kernels for 0%

profile of v6, /device:TPU:128, one launch (start us, length us, event | category | flops | bytes accessed | tf_op | source)
XLA Modules:
  0.0 125.4 jit_solution(15973108953626131593)
XLA Ops:
  0.0 0.0 copy-start
  0.0 0.0 copy-start.1
  0.0 0.9 copy-done
  1.0 1.1 copy_bitcast_fusion.1
  2.0 0.8 pad_maximum_fusion.1
  2.9 6.1 %all-to-all-start.1 = ((bf16[128,8,256]{2,0,1:T(8,128)(2,1)}), bf16[128,8,256]{2,0,1:T(8,128)(2,1)S(1)}, u32[]{:S(2)}, u32[]{:S(2)}) async-start(bf16[128,8,256]{2,0,1:T(8,128)(2,1)} %pad_maximum_fusion.1), calls=%async_computation.1 | async-start | bytes 1048576 | tf_op jit(solution)/shard_map/all_to_all | solution.py:147
  9.0 0.0 copy-done.1
  9.0 1.6 %copy.31 = bf16[16,8,8,1024]{3,2,0,1:T(8,128)(2,1)} copy(bf16[16,8,8,1024]{3,2,1,0:T(8,128)(2,1)S(1)} %bitcast.32) | data formatting | bytes 4194304 | tf_op jit(solution)/shard_map/all_to_all | solution.py:148
  10.6 8.5 %all-to-all-done.1 = bf16[128,8,256]{2,0,1:T(8,128)(2,1)S(1)} async-done(((bf16[128,8,256]{2,0,1:T(8,128)(2,1)}), bf16[128,8,256]{2,0,1:T(8,128)(2,1)S(1)}, u32[]{:S(2)}, u32[]{:S(2)}) %all-to-all-start.1) | async-done | bytes 524320 | tf_op jit(solution)/shard_map/all_to_all | solution.py:147
  19.1 0.0 copy-start.4
  19.1 3.7 %all-to-all-start = ((bf16[128,8,1024]{2,0,1:T(8,128)(2,1)}), bf16[128,8,1024]{2,0,1:T(8,128)(2,1)S(1)}, u32[]{:S(2)}, u32[]{:S(2)}) async-start(bf16[128,8,1024]{2,0,1:T(8,128)(2,1)} %bitcast.27), calls=%async_computation | async-start | bytes 4194304 | tf_op jit(solution)/shard_map/all_to_all | solution.py:148
  22.8 0.0 copy-start.3
  22.9 0.8 dynamic_slice.7
  23.7 0.1 fusion.1
  23.8 0.2 slice_reduce_fusion
  24.0 1.9 %collective-permute-start.1 = (bf16[1024,256]{1,0:T(8,128)(2,1)S(1)}, bf16[1024,256]{1,0:T(8,128)(2,1)S(1)}, u32[]{:S(2)}, u32[]{:S(2)}) collective-permute-start(bf16[1024,256]{1,0:T(8,128)(2,1)S(1)} %bitcast.29), channel_id=1, source_target_pairs={{0,8},{8,16},{16,24},{24,32},{32,40},{40,48},{48,56},{56,64},{64,7... | collective-permute-start | bytes 1572872 | tf_op jit(solution)/shard_map/ppermute | solution.py:28
  25.9 0.0 copy-done.4
  25.9 0.7 gather_fusion.1
  26.6 0.1 reshape.61
  26.7 0.2 slice_reduce_fusion.2
  26.9 0.7 slice.56
  27.5 3.5 %collective-permute-start = (bf16[256,256]{1,0:T(8,128)(2,1)}, bf16[256,256]{1,0:T(8,128)(2,1)}, u32[]{:S(2)}, u32[]{:S(2)}) collective-permute-start(bf16[256,256]{1,0:T(8,128)(2,1)} %bitcast.4), channel_id=1, source_target_pairs={{0,16},{8,24},{16,32},{24,40},{32,48},{40,56},{48,64},{56,72},{64,... | collective-permute-start | bytes 393224 | tf_op jit(solution)/shard_map/ppermute | solution.py:28
  31.0 0.0 copy-done.3
  31.0 0.1 and_convert_fusion
  31.1 0.6 reshape.50.kid_ref
  31.7 0.7 gather_fusion
  32.4 0.1 reshape.53
  32.5 0.6 reshape.51.full_ref
  33.1 1.0 copy.22.qid_ref
  34.1 0.8 convert_reduce_fusion.nback_ref
  34.9 10.7 %collective-permute-done = bf16[256,256]{1,0:T(8,128)(2,1)} collective-permute-done((bf16[256,256]{1,0:T(8,128)(2,1)}, bf16[256,256]{1,0:T(8,128)(2,1)}, u32[]{:S(2)}, u32[]{:S(2)}) %collective-permute-start) | collective-permute-done | bytes 131104 | tf_op jit(solution)/shard_map/ppermute | solution.py:28
  45.6 0.3 collective-permute-done.1
  46.0 1.0 pad_maximum_fusion
  46.9 1.1 fusion.2
  48.0 13.5 %all-to-all-done = bf16[128,8,1024]{2,0,1:T(8,128)(2,1)S(1)} async-done(((bf16[128,8,1024]{2,0,1:T(8,128)(2,1)}), bf16[128,8,1024]{2,0,1:T(8,128)(2,1)S(1)}, u32[]{:S(2)}, u32[]{:S(2)}) %all-to-all-start) | async-done | bytes 2097184 | tf_op jit(solution)/shard_map/all_to_all | solution.py:148
  61.5 0.0 copy-start.2
  61.5 1.3 %copy-done.2 = bf16[128,8,1024]{2,0,1:T(8,128)(2,1)} copy-done((bf16[128,8,1024]{2,0,1:T(8,128)(2,1)}, bf16[128,8,1024]{2,0,1:T(8,128)(2,1)S(1)}, u32[]{:S(2)}) %copy-start.2) | copy-done | bytes 2097176
  62.8 26.6 %shard_map.91 = bf16[1024,1024]{1,0:T(8,128)(2,1)} custom-call(s32[4]{0:T(128)} %convert_reduce_fusion.nback_ref, s32[24]{0:T(128)} %reshape.51.full_ref, bf16[1024,1024]{1,0:T(8,128)(2,1)} %bitcast.33, bf16[2304,128]{1,0:T(8,128)(2,1)} %get-tuple-element.10.k_ref, bf16[2304,128]{1,0:T(8,128)(2,1)} %get-tuple-element.9.v_ref, s32[1024,1]{1,0:T(8,128)} %copy.22.qid_ref, ...), custom_call_target="tpu_custom_call" | custom-call | flops 48318382080 | bytes 4194304 | tf_op jit(solution)/shard_map/pallas_call | solution.py:130
  89.5 34.3 %all_to_all.53 = bf16[8,128,1024]{2,1,0:T(8,128)(2,1)S(1)} all-to-all(bf16[8,128,1024]{2,1,0:T(8,128)(2,1)} %bitcast.34), channel_id=1, replica_groups=mesh['ctx'=64,'head'=8] {'head'}, dimensions={0} | all-to-all | bytes 4194304 | tf_op jit(solution)/shard_map/all_to_all | solution.py:175
  123.8 1.6 %copy.27 = bf16[8,16,8,1024]{3,2,0,1:T(8,128)(2,1)} copy(bf16[8,16,8,1024]{3,2,1,0:T(8,128)(2,1)S(1)} %bitcast.28) | data formatting | bytes 4194304 | tf_op jit(solution)/shard_map/all_to_all | solution.py:175
  (4 shorter events, 0.0 us)
Async XLA Ops:
  0.0 1.0 copy-start
  0.0 9.0 %copy-start.1 = (bf16[128,8192]{1,0:T(8,128)(2,1)S(1)}, bf16[128,8192]{1,0:T(8,128)(2,1)}, u32[]{:S(2)}) copy-start(bf16[128,8192]{1,0:T(8,128)(2,1)} %param.9) | copy-start | bytes 6291460
  2.9 16.2 %all-to-all-start.1 = ((bf16[128,8,256]{2,0,1:T(8,128)(2,1)}), bf16[128,8,256]{2,0,1:T(8,128)(2,1)S(1)}, u32[]{:S(2)}, u32[]{:S(2)}) async-start(bf16[128,8,256]{2,0,1:T(8,128)(2,1)} %pad_maximum_fusion.1), calls=%async_computation.1 | async-start | bytes 1048576 | tf_op jit(solution)/shard_map/all_to_all | solution.py:147
  19.1 6.8 %copy-start.4 = (s32[24]{0:T(128)S(1)}, s32[24]{0:T(128)}, u32[]{:S(2)}) copy-start(s32[24]{0:T(128)} %constant.52) | copy-start | bytes 292
  19.1 42.5 %all-to-all-start = ((bf16[128,8,1024]{2,0,1:T(8,128)(2,1)}), bf16[128,8,1024]{2,0,1:T(8,128)(2,1)S(1)}, u32[]{:S(2)}, u32[]{:S(2)}) async-start(bf16[128,8,1024]{2,0,1:T(8,128)(2,1)} %bitcast.27), calls=%async_computation | async-start | bytes 4194304 | tf_op jit(solution)/shard_map/all_to_all | solution.py:148
  22.8 8.2 %copy-start.3 = (pred[6]{0:T(512)(128)(4,1)S(1)}, pred[6]{0:T(512)(128)(4,1)}, u32[]{:S(2)}) copy-start(pred[6]{0:T(512)(128)(4,1)} %constant.51) | copy-start | bytes 22
  24.0 22.0 %collective-permute-start.1 = (bf16[1024,256]{1,0:T(8,128)(2,1)S(1)}, bf16[1024,256]{1,0:T(8,128)(2,1)S(1)}, u32[]{:S(2)}, u32[]{:S(2)}) collective-permute-start(bf16[1024,256]{1,0:T(8,128)(2,1)S(1)} %bitcast.29), channel_id=1, source_target_pairs={{0,8},{8,16},{16,24},{24,32},{32,40},{40,48},{48,56},{56,64},{64,7... | collective-permute-start | bytes 1572872 | tf_op jit(solution)/shard_map/ppermute | solution.py:28
  27.5 18.1 %collective-permute-start = (bf16[256,256]{1,0:T(8,128)(2,1)}, bf16[256,256]{1,0:T(8,128)(2,1)}, u32[]{:S(2)}, u32[]{:S(2)}) collective-permute-start(bf16[256,256]{1,0:T(8,128)(2,1)} %bitcast.4), channel_id=1, source_target_pairs={{0,16},{8,24},{16,32},{24,40},{32,48},{40,56},{48,64},{56,72},{64,... | collective-permute-start | bytes 393224 | tf_op jit(solution)/shard_map/ppermute | solution.py:28
  61.5 1.3 %copy-start.2 = (bf16[128,8,1024]{2,0,1:T(8,128)(2,1)}, bf16[128,8,1024]{2,0,1:T(8,128)(2,1)S(1)}, u32[]{:S(2)}) copy-start(bf16[128,8,1024]{2,0,1:T(8,128)(2,1)S(1)} %all-to-all-done) | copy-start | bytes 6291460

commit v7 on v6

--- a/solution.py
+++ b/solution.py
@@ -17,6 +17,7 @@
 QBLK_DEV = 4
 PREV = 2
 MXU_SUM = True
+SPLIT = 2
 
 
 floor_score = -1e30
@@ -96,8 +97,9 @@
                 o_ref[:, j * HD:(j + 1) * HD] = (acc_scr[j] / l_scr[j]).astype(o_ref.dtype)
 
 
-def attend(nback, full, queries, keys, values, qids, kids, mxu_sum=MXU_SUM):
+def attend(nback, full, queries, keys, values, qids, kids, half, halves, mxu_sum=MXU_SUM):
     rows, width = queries.shape
+    width = width // halves
     heads = width // HD
     n_q = rows // BLOCK
     base = keys.shape[0] // BLOCK - n_q
@@ -113,7 +115,7 @@
         num_scalar_prefetch=2,
         grid=(n_q, n_steps),
         in_specs=[
-            pl.BlockSpec((BLOCK, width), lambda qb, step, nb, fl: (qb, 0)),
+            pl.BlockSpec((BLOCK, width), lambda qb, step, nb, fl: (qb, half)),
             pl.BlockSpec((BLOCK, HD), kv_map),
             pl.BlockSpec((BLOCK, HD), kv_map),
             pl.BlockSpec((BLOCK, 1), lambda qb, step, nb, fl: (qb, 0)),
@@ -169,10 +171,14 @@
     live = (tile_last[tiles] == first_q[:, None]) & (steps[None, :] > 0)
     nback = jnp.sum(live.astype(jnp.int32), axis=1)
     full = ((tile_first[tiles] == last_q[:, None]) & (steps[None, :] > 0)).astype(jnp.int32).reshape(-1)
-    local_out = attend(
-        nback, full, local_queries, window[:, :HD], window[:, HD:],
-        range_ids.reshape(range_rows, 1), window_ids.reshape(1, -1))
-    return lax.all_to_all(local_out, "head", split_axis=0, concat_axis=1, tiled=True)
+    window_keys, window_values = window[:, :HD], window[:, HD:]
+    qids, kids = range_ids.reshape(range_rows, 1), window_ids.reshape(1, -1)
+    outs = []
+    for half in range(SPLIT):
+        local_out = attend(nback, full, local_queries, window_keys, window_values, qids, kids, half, SPLIT)
+        outs.append(lax.all_to_all(
+            local_out.reshape(range_rows, 1, -1), "head", split_axis=0, concat_axis=1, tiled=True))
+    return jnp.stack(outs, axis=2).reshape(rows, QH * HD)
 
 
 def solution(mesh):

time: 126 us -> 150 us (1.19)
  blocking collectives: 34.3 us -> 0 us
  local copies, waits for them, and re-layouts: 13.2 us -> 27.7 us
  waiting for transfers between devices: 33 us -> 46.3 us
  Pallas kernels: 26.6 us -> 38.7 us
  starting transfers between devices: 15.2 us -> 27.2 us
  other arithmetic: 2.77 us -> 8.1 us
    all_to_all x1 -> x0, blocking collectives: 34.3 us -> none  [shards(): lax.all_to_all(local_out, 'head', split_axis=0, concat_axis=1, tiled=True)]
    all_to_all x0 -> x2, waiting for transfers between devices: none -> 13.2 us  [shards(): lax.all_to_all(local_out.reshape(range_rows, 1, -1), 'head', split_axis=0...]
    pallas_call x1 -> x2, Pallas kernels: 26.6 us -> 38.7 us  [attend(): pl.pallas_call(functools.partial(attend_kernel, heads=heads, n_steps=n_st...]
    all_to_all x0 -> x2, starting transfers between devices: none -> 12 us  [shards(): lax.all_to_all(local_out.reshape(range_rows, 1, -1), 'head', split_axis=0...]
    unnamed x10 -> x16, local copies, waits for them, and re-layouts: 2.28 us -> 11.4 us
    reshape x0 -> x2, other arithmetic: none -> 5.21 us  [shards(): local_out.reshape(range_rows, 1, -1)]
    reshape x2 -> x4, local copies, waits for them, and re-layouts: 1.63 us -> 6.2 us  [the longest x1 4.06 us: shards(): return jnp.stack(outs, axis=2).reshape(rows, QH * HD)]
    another operation x0 -> x1, local copies, waits for them, and re-layouts: none -> 2.39 us  [shards(): return jnp.stack(outs, axis=2).reshape(rows, QH * HD)]
  transfers between devices with their start and end apart: 4 -> 6, of which waited for: 4 -> 5; matrix products, arithmetic and copies ran while one was open for 8% -> 11% of each run, Pallas kernels for 0% -> 13%
where the time goes in v7:
time: 150 us; the launch traced here: 148 us
  waiting for transfers between devices  46.3 us (31%)
  Pallas kernels  38.7 us (26%)
  local copies, waits for them, and re-layouts  27.7 us (18%)
  starting transfers between devices  27.2 us (18%)
  other arithmetic  8.1 us (5%)
    pallas_call x2, Pallas kernels, attend(): pl.pallas_call(functools.partial(attend_kernel, heads=heads, n_steps=n_st...  38.7 us
    all_to_all x1, waiting for transfers between devices, shards(): lax.all_to_all(queries, 'head', split_axis=1, concat_axis=0, tiled=True)  13.5 us
    all_to_all x2, waiting for transfers between devices, shards(): lax.all_to_all(local_out.reshape(range_rows, 1, -1), 'head', split_axis=0...  13.2 us
    all_to_all x2, starting transfers between devices, shards(): lax.all_to_all(local_out.reshape(range_rows, 1, -1), 'head', split_axis=0...  12 us
    unnamed x16, local copies, waits for them, and re-layouts  11.4 us
    ppermute x2, waiting for transfers between devices, from_behind(): lax.ppermute(value, axis, [(source, source + steps) for source in range(l...  11.1 us
    all_to_all x1, waiting for transfers between devices, shards(): lax.all_to_all(paired, 'head', split_axis=1, concat_axis=0, tiled=True)  8.58 us
    all_to_all x1, starting transfers between devices, shards(): lax.all_to_all(paired, 'head', split_axis=1, concat_axis=0, tiled=True)  6.11 us
  transfers between devices with their start and end apart: 6, of which 5 were waited for; matrix products, arithmetic and copies ran while one was open for 11% of the time, Pallas kernels for 13%

profile of v7, /device:TPU:128, one launch (start us, length us, event | category | flops | bytes accessed | tf_op | source)
XLA Modules:
  0.0 148.3 jit_solution(8429641670870440451)
XLA Ops:
  0.0 0.0 copy-start
  0.0 0.0 copy-start.1
  0.0 0.9 copy-done
  1.0 1.1 copy_bitcast_fusion.1
  2.0 0.9 pad_maximum_fusion.2
  2.9 6.1 %all-to-all-start.1 = ((bf16[128,8,256]{2,0,1:T(8,128)(2,1)}), bf16[128,8,256]{2,0,1:T(8,128)(2,1)S(1)}, u32[]{:S(2)}, u32[]{:S(2)}) async-start(bf16[128,8,256]{2,0,1:T(8,128)(2,1)} %pad_maximum_fusion.2), calls=%async_computation.1 | async-start | bytes 1048576 | tf_op jit(solution)/shard_map/all_to_all | solution.py:149
  9.0 0.0 copy-done.1
  9.0 1.5 %copy.58 = bf16[16,8,8,1024]{3,2,0,1:T(8,128)(2,1)} copy(bf16[16,8,8,1024]{3,2,1,0:T(8,128)(2,1)S(1)} %bitcast.39) | data formatting | bytes 4194304 | tf_op jit(solution)/shard_map/all_to_all | solution.py:150
  10.5 8.6 %all-to-all-done.1 = bf16[128,8,256]{2,0,1:T(8,128)(2,1)S(1)} async-done(((bf16[128,8,256]{2,0,1:T(8,128)(2,1)}), bf16[128,8,256]{2,0,1:T(8,128)(2,1)S(1)}, u32[]{:S(2)}, u32[]{:S(2)}) %all-to-all-start.1) | async-done | bytes 524320 | tf_op jit(solution)/shard_map/all_to_all | solution.py:149
  19.1 0.0 copy-start.4
  19.1 3.7 %all-to-all-start = ((bf16[128,8,1024]{2,0,1:T(8,128)(2,1)}), bf16[128,8,1024]{2,0,1:T(8,128)(2,1)S(1)}, u32[]{:S(2)}, u32[]{:S(2)}) async-start(bf16[128,8,1024]{2,0,1:T(8,128)(2,1)} %bitcast.32), calls=%async_computation | async-start | bytes 4194304 | tf_op jit(solution)/shard_map/all_to_all | solution.py:150
  22.8 0.0 copy-start.3
  22.9 0.8 dynamic_slice.7
  23.7 0.1 fusion.1
  23.8 0.2 slice_reduce_fusion
  24.0 1.9 %collective-permute-start.1 = (bf16[1024,256]{1,0:T(8,128)(2,1)S(1)}, bf16[1024,256]{1,0:T(8,128)(2,1)S(1)}, u32[]{:S(2)}, u32[]{:S(2)}) collective-permute-start(bf16[1024,256]{1,0:T(8,128)(2,1)S(1)} %bitcast.36), channel_id=1, source_target_pairs={{0,8},{8,16},{16,24},{24,32},{32,40},{40,48},{48,56},{56,64},{64,7... | collective-permute-start | bytes 1572872 | tf_op jit(solution)/shard_map/ppermute | solution.py:29
  25.9 0.0 copy-done.4
  25.9 0.7 gather_fusion.1
  26.6 0.1 reshape.72
  26.7 0.2 slice_reduce_fusion.2
  26.9 0.7 slice.56
  27.5 3.5 %collective-permute-start = (bf16[256,256]{1,0:T(8,128)(2,1)}, bf16[256,256]{1,0:T(8,128)(2,1)}, u32[]{:S(2)}, u32[]{:S(2)}) collective-permute-start(bf16[256,256]{1,0:T(8,128)(2,1)} %bitcast.4), channel_id=1, source_target_pairs={{0,16},{8,24},{16,32},{24,40},{32,48},{40,56},{48,64},{56,72},{64,... | collective-permute-start | bytes 393224 | tf_op jit(solution)/shard_map/ppermute | solution.py:29
  31.0 0.0 copy-done.3
  31.0 0.1 and_convert_fusion
  31.1 0.6 reshape.58.kid_ref
  31.7 0.7 gather_fusion
  32.4 0.1 reshape.64
  32.5 0.7 reshape.62.full_ref
  33.2 1.0 copy.44.qid_ref
  34.2 0.7 convert_reduce_fusion.nback_ref
  34.9 10.7 %collective-permute-done = bf16[256,256]{1,0:T(8,128)(2,1)} collective-permute-done((bf16[256,256]{1,0:T(8,128)(2,1)}, bf16[256,256]{1,0:T(8,128)(2,1)}, u32[]{:S(2)}, u32[]{:S(2)}) %collective-permute-start) | collective-permute-done | bytes 131104 | tf_op jit(solution)/shard_map/ppermute | solution.py:29
  45.6 0.4 collective-permute-done.1
  46.0 1.0 pad_maximum_fusion.1
  46.9 1.1 fusion.2
  48.1 13.5 %all-to-all-done = bf16[128,8,1024]{2,0,1:T(8,128)(2,1)S(1)} async-done(((bf16[128,8,1024]{2,0,1:T(8,128)(2,1)}), bf16[128,8,1024]{2,0,1:T(8,128)(2,1)S(1)}, u32[]{:S(2)}, u32[]{:S(2)}) %all-to-all-start) | async-done | bytes 2097184 | tf_op jit(solution)/shard_map/all_to_all | solution.py:150
  61.5 0.0 copy-start.2
  61.5 1.3 copy-done.2
  62.8 19.4 %shard_map.91 = bf16[1024,512]{1,0:T(8,128)(2,1)} custom-call(s32[4]{0:T(128)} %convert_reduce_fusion.nback_ref, s32[24]{0:T(128)} %reshape.62.full_ref, bf16[1024,1024]{1,0:T(8,128)(2,1)} %bitcast.40, bf16[2304,128]{1,0:T(8,128)(2,1)} %get-tuple-element.10.k_ref, bf16[2304,128]{1,0:T(8,128)(2,1)} %get-tuple-element.9.v_ref, s32[1024,1]{1,0:T(8,128)} %copy.44.qid_ref, ...), custom_call_target="tpu_custom_call" | custom-call | flops 24159191040 | bytes 2097152 | tf_op jit(solution)/shard_map/pallas_call | solution.py:132
  82.2 0.5 broadcast.18
  82.7 2.6 %reduce.9 = bf16[1024,512]{1,0:T(8,128)(2,1)S(1)} reduce(bf16[1024,1,512]{2,0,1:T(8,128)(2,1)} %bitcast.43, bf16[]{:T(256)} %broadcast.18), dimensions={1}, to_apply=%copy.45.reduce_sub_computation | reduce | bytes 2097154 | tf_op jit(solution)/shard_map/reshape | solution.py:180
  85.3 1.6 %reshape.87 = bf16[8,2,32768]{2,1,0:T(2,128)(2,1)} reshape(bf16[1024,512]{1,0:T(8,128)(2,1)S(1)} %reduce.9) | data formatting | bytes 2097152
  86.9 6.3 %all-to-all-start.2 = ((bf16[8,2,32768]{2,1,0:T(2,128)(2,1)}), bf16[8,2,32768]{2,1,0:T(2,128)(2,1)S(1)}, u32[]{:S(2)}, u32[]{:S(2)}) async-start(bf16[8,2,32768]{2,1,0:T(2,128)(2,1)} %reshape.87), calls=%async_computation.2 | async-start | bytes 2097152 | tf_op jit(solution)/shard_map/all_to_all | solution.py:179
  93.3 19.3 %shard_map.92 = bf16[1024,512]{1,0:T(8,128)(2,1)} custom-call(s32[4]{0:T(128)} %convert_reduce_fusion.nback_ref, s32[24]{0:T(128)} %reshape.62.full_ref, bf16[1024,1024]{1,0:T(8,128)(2,1)} %bitcast.41, bf16[2304,128]{1,0:T(8,128)(2,1)} %get-tuple-element.10.k_ref, bf16[2304,128]{1,0:T(8,128)(2,1)} %get-tuple-element.9.v_ref, s32[1024,1]{1,0:T(8,128)} %copy.44.qid_ref, ...), custom_call_target="tpu_custom_call" | custom-call | flops 24159191040 | bytes 2097152 | tf_op jit(solution)/shard_map/pallas_call | solution.py:132
  112.6 2.6 %reduce.8 = bf16[1024,512]{1,0:T(8,128)(2,1)S(1)} reduce(bf16[1024,1,512]{2,0,1:T(8,128)(2,1)} %bitcast.42, bf16[]{:T(256)} %broadcast.18), dimensions={1}, to_apply=%copy.47.reduce_sub_computation | reduce | bytes 2097154 | tf_op jit(solution)/shard_map/reshape | solution.py:180
  115.2 1.6 %reshape.85 = bf16[8,2,32768]{2,1,0:T(2,128)(2,1)} reshape(bf16[1024,512]{1,0:T(8,128)(2,1)S(1)} %reduce.8) | data formatting | bytes 2097152
  116.8 0.0 all-to-all-done.2
  116.8 5.7 %all-to-all-start.3 = ((bf16[8,2,32768]{2,1,0:T(2,128)(2,1)}), bf16[8,2,32768]{2,1,0:T(2,128)(2,1)}, u32[]{:S(2)}, u32[]{:S(2)}) async-start(bf16[8,2,32768]{2,1,0:T(2,128)(2,1)} %reshape.85), calls=%async_computation.3 | async-start | bytes 2097152 | tf_op jit(solution)/shard_map/all_to_all | solution.py:179
  122.5 1.0 reshape.88
  123.5 0.3 copy.50
  123.8 13.2 %all-to-all-done.3 = bf16[8,2,32768]{2,1,0:T(2,128)(2,1)} async-done(((bf16[8,2,32768]{2,1,0:T(2,128)(2,1)}), bf16[8,2,32768]{2,1,0:T(2,128)(2,1)}, u32[]{:S(2)}, u32[]{:S(2)}) %all-to-all-start.3) | async-done | bytes 1048608 | tf_op jit(solution)/shard_map/all_to_all | solution.py:179
  137.0 4.3 %reshape.86 = bf16[1024,1,512]{2,1,0:T(2,128)(2,1)S(1)} reshape(bf16[8,2,32768]{2,1,0:T(2,128)(2,1)} %all-to-all-done.3) | data formatting | bytes 2097152
  141.3 0.3 copy.51
  141.6 0.2 pad_maximum_fusion
  141.8 2.4 %copy.48 = bf16[128,8,2,512]{0,3,2,1:T(8,128)(2,1)} copy(bf16[128,8,2,512]{3,0,1,2:T(8,128)(2,1)S(1)} %pad_maximum_fusion) | data formatting | bytes 4194304 | tf_op jit(solution)/shard_map/stack | solution.py:181
  144.2 4.1 %copy.49 = bf16[128,8192]{1,0:T(8,128)(2,1)} copy(bf16[128,8192]{0,1:T(8,128)(2,1)} %bitcast.33) | data formatting | bytes 4194304 | tf_op jit(solution)/shard_map/reshape | solution.py:181
  (4 shorter events, 0.0 us)
Async XLA Ops:
  0.0 1.0 copy-start
  0.0 9.0 %copy-start.1 = (bf16[128,8192]{1,0:T(8,128)(2,1)S(1)}, bf16[128,8192]{1,0:T(8,128)(2,1)}, u32[]{:S(2)}) copy-start(bf16[128,8192]{1,0:T(8,128)(2,1)} %param.9) | copy-start | bytes 6291460
  2.9 16.2 %all-to-all-start.1 = ((bf16[128,8,256]{2,0,1:T(8,128)(2,1)}), bf16[128,8,256]{2,0,1:T(8,128)(2,1)S(1)}, u32[]{:S(2)}, u32[]{:S(2)}) async-start(bf16[128,8,256]{2,0,1:T(8,128)(2,1)} %pad_maximum_fusion.2), calls=%async_computation.1 | async-start | bytes 1048576 | tf_op jit(solution)/shard_map/all_to_all | solution.py:149
  19.1 6.8 %copy-start.4 = (s32[24]{0:T(128)S(1)}, s32[24]{0:T(128)}, u32[]{:S(2)}) copy-start(s32[24]{0:T(128)} %constant.52) | copy-start | bytes 292
  19.1 42.5 %all-to-all-start = ((bf16[128,8,1024]{2,0,1:T(8,128)(2,1)}), bf16[128,8,1024]{2,0,1:T(8,128)(2,1)S(1)}, u32[]{:S(2)}, u32[]{:S(2)}) async-start(bf16[128,8,1024]{2,0,1:T(8,128)(2,1)} %bitcast.32), calls=%async_computation | async-start | bytes 4194304 | tf_op jit(solution)/shard_map/all_to_all | solution.py:150
  22.8 8.2 %copy-start.3 = (pred[6]{0:T(512)(128)(4,1)S(1)}, pred[6]{0:T(512)(128)(4,1)}, u32[]{:S(2)}) copy-start(pred[6]{0:T(512)(128)(4,1)} %constant.51) | copy-start | bytes 22
  24.0 22.0 %collective-permute-start.1 = (bf16[1024,256]{1,0:T(8,128)(2,1)S(1)}, bf16[1024,256]{1,0:T(8,128)(2,1)S(1)}, u32[]{:S(2)}, u32[]{:S(2)}) collective-permute-start(bf16[1024,256]{1,0:T(8,128)(2,1)S(1)} %bitcast.36), channel_id=1, source_target_pairs={{0,8},{8,16},{16,24},{24,32},{32,40},{40,48},{48,56},{56,64},{64,7... | collective-permute-start | bytes 1572872 | tf_op jit(solution)/shard_map/ppermute | solution.py:29
  27.5 18.1 %collective-permute-start = (bf16[256,256]{1,0:T(8,128)(2,1)}, bf16[256,256]{1,0:T(8,128)(2,1)}, u32[]{:S(2)}, u32[]{:S(2)}) collective-permute-start(bf16[256,256]{1,0:T(8,128)(2,1)} %bitcast.4), channel_id=1, source_target_pairs={{0,16},{8,24},{16,32},{24,40},{32,48},{40,56},{48,64},{56,72},{64,... | collective-permute-start | bytes 393224 | tf_op jit(solution)/shard_map/ppermute | solution.py:29
  61.5 1.3 copy-start.2
  86.9 29.9 %all-to-all-start.2 = ((bf16[8,2,32768]{2,1,0:T(2,128)(2,1)}), bf16[8,2,32768]{2,1,0:T(2,128)(2,1)S(1)}, u32[]{:S(2)}, u32[]{:S(2)}) async-start(bf16[8,2,32768]{2,1,0:T(2,128)(2,1)} %reshape.87), calls=%async_computation.2 | async-start | bytes 2097152 | tf_op jit(solution)/shard_map/all_to_all | solution.py:179
  116.8 20.2 %all-to-all-start.3 = ((bf16[8,2,32768]{2,1,0:T(2,128)(2,1)}), bf16[8,2,32768]{2,1,0:T(2,128)(2,1)}, u32[]{:S(2)}, u32[]{:S(2)}) async-start(bf16[8,2,32768]{2,1,0:T(2,128)(2,1)} %reshape.85), calls=%async_computation.3 | async-start | bytes 2097152 | tf_op jit(solution)/shard_map/all_to_all | solution.py:179

commit v8 on v6

--- a/solution.py
+++ b/solution.py
@@ -39,24 +39,37 @@
     qb = pl.program_id(0)
     step = pl.program_id(1)
     last = pl.num_programs(1) - 1
+    half = BLOCK // 2
+
+    def augmented(v):
+        return jnp.concatenate([v, jnp.ones_like(v)], axis=1)
 
     @pl.when(step == 0)
-    def _init():
-        m_scr[...] = jnp.full(m_scr.shape, floor_score, jnp.float32)
-        if not mxu_sum:
-            l_scr[...] = jnp.zeros(l_scr.shape, jnp.float32)
-        acc_scr[...] = jnp.zeros(acc_scr.shape, jnp.float32)
+    def _diagonal():
+        k = k_ref[...]
+        v = augmented(v_ref[...])
+        same = qid_ref[...] == kid_ref[...]
+        rows = lax.broadcasted_iota(jnp.int32, (BLOCK, BLOCK), 0)
+        cols = lax.broadcasted_iota(jnp.int32, (BLOCK, BLOCK), 1)
+        allowed = same & (cols <= rows)
+        for j in range(heads):
+            q = q_ref[:, j * HD:(j + 1) * HD]
+            for lo, width in ((0, half), (half, BLOCK)):
+                s = lax.dot_general(q[lo:lo + half], k[:width], (((1,), (1,)), ((), ())),
+                                    preferred_element_type=jnp.float32)
+                s = s * HD ** (-0.5)
+                s = jnp.where(allowed[lo:lo + half, :width], s, floor_score)
+                m_new = jnp.max(s, axis=-1, keepdims=True)
+                p = jnp.exp(s - m_new)
+                acc_scr[j, lo:lo + half] = jnp.dot(
+                    p.astype(jnp.bfloat16), v[:width], preferred_element_type=jnp.float32)
+                m_scr[j, lo:lo + half] = jnp.broadcast_to(m_new, (half, 128))
 
     def body(masked):
         k = k_ref[...]
-        v = v_ref[...]
-        if mxu_sum:
-            v = jnp.concatenate([v, jnp.ones_like(v)], axis=1)
+        v = augmented(v_ref[...])
         if masked:
             allowed = qid_ref[...] == kid_ref[...]
-            rows = lax.broadcasted_iota(jnp.int32, (BLOCK, BLOCK), 0)
-            cols = lax.broadcasted_iota(jnp.int32, (BLOCK, BLOCK), 1)
-            allowed = allowed & ((cols <= rows) | (step > 0))
         for j in range(heads):
             q = q_ref[:, j * HD:(j + 1) * HD]
             s = lax.dot_general(q, k, (((1,), (1,)), ((), ())), preferred_element_type=jnp.float32)
@@ -68,14 +81,10 @@
             factor = jnp.exp(m_old - m_new)
             p = jnp.exp(s - jnp.tile(m_new, (1, BLOCK // 128)))
             pv = jnp.dot(p.astype(jnp.bfloat16), v, preferred_element_type=jnp.float32)
-            if mxu_sum:
-                acc_scr[j] = acc_scr[j] * jnp.tile(factor, (1, 2)) + pv
-            else:
-                l_scr[j] = l_scr[j] * factor + jnp.sum(p, axis=-1, keepdims=True)
-                acc_scr[j] = acc_scr[j] * factor + pv
+            acc_scr[j] = acc_scr[j] * jnp.tile(factor, (1, 2)) + pv
             m_scr[j] = m_new
 
-    live = step <= nback_ref[qb]
+    live = (step > 0) & (step <= nback_ref[qb])
     full = full_ref[qb * n_steps + step] > 0
 
     @pl.when(live & full)
@@ -89,11 +98,8 @@
     @pl.when(step == last)
     def _finish():
         for j in range(heads):
-            if mxu_sum:
-                total = acc_scr[j, :, HD:]
-                o_ref[:, j * HD:(j + 1) * HD] = (acc_scr[j, :, :HD] / total).astype(o_ref.dtype)
-            else:
-                o_ref[:, j * HD:(j + 1) * HD] = (acc_scr[j] / l_scr[j]).astype(o_ref.dtype)
+            total = acc_scr[j, :, HD:]
+            o_ref[:, j * HD:(j + 1) * HD] = (acc_scr[j, :, :HD] / total).astype(o_ref.dtype)
 
 
 def attend(nback, full, queries, keys, values, qids, kids, mxu_sum=MXU_SUM):

time: 126 us -> 122 us (0.968)
  Pallas kernels: 26.6 us -> 24.3 us
  blocking collectives: 34.3 us -> 32.3 us
    pallas_call x1, Pallas kernels: 26.6 us -> 24.3 us  [attend(): pl.pallas_call(functools.partial(attend_kernel, heads=heads, n_steps=n_st...]
    all_to_all x1, blocking collectives: 34.3 us -> 32.3 us  [shards(): lax.all_to_all(local_out, 'head', split_axis=0, concat_axis=1, tiled=True)]
where the time goes in v8:
time: 122 us; the launch traced here: 121 us
  waiting for transfers between devices  33 us (27%)
  blocking collectives  32.3 us (26%)
  Pallas kernels  24.3 us (20%)
  starting transfers between devices  15.2 us (12%)
  local copies, waits for them, and re-layouts  13.2 us (11%)
  other arithmetic  2.77 us (2%)
    all_to_all x1, blocking collectives, shards(): lax.all_to_all(local_out, 'head', split_axis=0, concat_axis=1, tiled=True)  32.3 us
    pallas_call x1, Pallas kernels, attend(): pl.pallas_call(functools.partial(attend_kernel, heads=heads, n_steps=n_st...  24.3 us
    all_to_all x1, waiting for transfers between devices, shards(): lax.all_to_all(queries, 'head', split_axis=1, concat_axis=0, tiled=True)  13.5 us
    ppermute x2, waiting for transfers between devices, from_behind(): lax.ppermute(value, axis, [(source, source + steps) for source in range(l...  11 us
    all_to_all x1, waiting for transfers between devices, shards(): lax.all_to_all(paired, 'head', split_axis=1, concat_axis=0, tiled=True)  8.52 us
    all_to_all x1, starting transfers between devices, shards(): lax.all_to_all(paired, 'head', split_axis=1, concat_axis=0, tiled=True)  6.11 us
    ppermute x2, starting transfers between devices, from_behind(): lax.ppermute(value, axis, [(source, source + steps) for source in range(l...  5.39 us
    all_to_all x1, starting transfers between devices, shards(): lax.all_to_all(queries, 'head', split_axis=1, concat_axis=0, tiled=True)  3.74 us
  transfers between devices with their start and end apart: 4, of which 4 were waited for; matrix products, arithmetic and copies ran while one was open for 8% of the time, Pallas kernels for 0%

profile of v8, /device:TPU:128, one launch (start us, length us, event | category | flops | bytes accessed | tf_op | source)
XLA Modules:
  0.0 121.0 jit_solution(1472010516355288745)
XLA Ops:
  0.0 0.0 copy-start
  0.0 0.0 copy-start.1
  0.0 0.9 copy-done
  1.0 1.1 copy_bitcast_fusion.1
  2.0 0.8 pad_maximum_fusion.1
  2.9 6.1 %all-to-all-start.1 = ((bf16[128,8,256]{2,0,1:T(8,128)(2,1)}), bf16[128,8,256]{2,0,1:T(8,128)(2,1)S(1)}, u32[]{:S(2)}, u32[]{:S(2)}) async-start(bf16[128,8,256]{2,0,1:T(8,128)(2,1)} %pad_maximum_fusion.1), calls=%async_computation.1 | async-start | bytes 1048576 | tf_op jit(solution)/shard_map/all_to_all | solution.py:153
  9.0 0.0 copy-done.1
  9.0 1.6 %copy.31 = bf16[16,8,8,1024]{3,2,0,1:T(8,128)(2,1)} copy(bf16[16,8,8,1024]{3,2,1,0:T(8,128)(2,1)S(1)} %bitcast.32) | data formatting | bytes 4194304 | tf_op jit(solution)/shard_map/all_to_all | solution.py:154
  10.6 8.5 %all-to-all-done.1 = bf16[128,8,256]{2,0,1:T(8,128)(2,1)S(1)} async-done(((bf16[128,8,256]{2,0,1:T(8,128)(2,1)}), bf16[128,8,256]{2,0,1:T(8,128)(2,1)S(1)}, u32[]{:S(2)}, u32[]{:S(2)}) %all-to-all-start.1) | async-done | bytes 524320 | tf_op jit(solution)/shard_map/all_to_all | solution.py:153
  19.1 0.0 copy-start.4
  19.1 3.7 %all-to-all-start = ((bf16[128,8,1024]{2,0,1:T(8,128)(2,1)}), bf16[128,8,1024]{2,0,1:T(8,128)(2,1)S(1)}, u32[]{:S(2)}, u32[]{:S(2)}) async-start(bf16[128,8,1024]{2,0,1:T(8,128)(2,1)} %bitcast.27), calls=%async_computation | async-start | bytes 4194304 | tf_op jit(solution)/shard_map/all_to_all | solution.py:154
  22.8 0.0 copy-start.3
  22.9 0.8 dynamic_slice.7
  23.7 0.1 fusion.1
  23.8 0.2 slice_reduce_fusion
  24.0 1.9 %collective-permute-start.1 = (bf16[1024,256]{1,0:T(8,128)(2,1)S(1)}, bf16[1024,256]{1,0:T(8,128)(2,1)S(1)}, u32[]{:S(2)}, u32[]{:S(2)}) collective-permute-start(bf16[1024,256]{1,0:T(8,128)(2,1)S(1)} %bitcast.29), channel_id=1, source_target_pairs={{0,8},{8,16},{16,24},{24,32},{32,40},{40,48},{48,56},{56,64},{64,7... | collective-permute-start | bytes 1572872 | tf_op jit(solution)/shard_map/ppermute | solution.py:28
  25.9 0.0 copy-done.4
  25.9 0.7 gather_fusion.1
  26.6 0.1 reshape.61
  26.7 0.2 slice_reduce_fusion.2
  26.9 0.7 slice.56
  27.5 3.5 %collective-permute-start = (bf16[256,256]{1,0:T(8,128)(2,1)}, bf16[256,256]{1,0:T(8,128)(2,1)}, u32[]{:S(2)}, u32[]{:S(2)}) collective-permute-start(bf16[256,256]{1,0:T(8,128)(2,1)} %bitcast.4), channel_id=1, source_target_pairs={{0,16},{8,24},{16,32},{24,40},{32,48},{40,56},{48,64},{56,72},{64,... | collective-permute-start | bytes 393224 | tf_op jit(solution)/shard_map/ppermute | solution.py:28
  31.0 0.0 copy-done.3
  31.0 0.1 and_convert_fusion
  31.1 0.6 reshape.50.kid_ref
  31.7 0.7 gather_fusion
  32.4 0.1 reshape.53
  32.5 0.6 reshape.51.full_ref
  33.1 1.0 copy.22.qid_ref
  34.1 0.8 convert_reduce_fusion.nback_ref
  34.9 10.7 %collective-permute-done = bf16[256,256]{1,0:T(8,128)(2,1)} collective-permute-done((bf16[256,256]{1,0:T(8,128)(2,1)}, bf16[256,256]{1,0:T(8,128)(2,1)}, u32[]{:S(2)}, u32[]{:S(2)}) %collective-permute-start) | collective-permute-done | bytes 131104 | tf_op jit(solution)/shard_map/ppermute | solution.py:28
  45.6 0.3 collective-permute-done.1
  46.0 1.0 pad_maximum_fusion
  46.9 1.1 fusion.2
  48.0 13.5 %all-to-all-done = bf16[128,8,1024]{2,0,1:T(8,128)(2,1)S(1)} async-done(((bf16[128,8,1024]{2,0,1:T(8,128)(2,1)}), bf16[128,8,1024]{2,0,1:T(8,128)(2,1)S(1)}, u32[]{:S(2)}, u32[]{:S(2)}) %all-to-all-start) | async-done | bytes 2097184 | tf_op jit(solution)/shard_map/all_to_all | solution.py:154
  61.5 0.0 copy-start.2
  61.5 1.3 %copy-done.2 = bf16[128,8,1024]{2,0,1:T(8,128)(2,1)} copy-done((bf16[128,8,1024]{2,0,1:T(8,128)(2,1)}, bf16[128,8,1024]{2,0,1:T(8,128)(2,1)S(1)}, u32[]{:S(2)}) %copy-start.2) | copy-done | bytes 2097176
  62.8 24.3 %shard_map.91 = bf16[1024,1024]{1,0:T(8,128)(2,1)} custom-call(s32[4]{0:T(128)} %convert_reduce_fusion.nback_ref, s32[24]{0:T(128)} %reshape.51.full_ref, bf16[1024,1024]{1,0:T(8,128)(2,1)} %bitcast.33, bf16[2304,128]{1,0:T(8,128)(2,1)} %get-tuple-element.10.k_ref, bf16[2304,128]{1,0:T(8,128)(2,1)} %get-tuple-element.9.v_ref, s32[1024,1]{1,0:T(8,128)} %copy.22.qid_ref, ...), custom_call_target="tpu_custom_call" | custom-call | flops 48318382080 | bytes 4194304 | tf_op jit(solution)/shard_map/pallas_call | solution.py:136
  87.2 32.3 %all_to_all.53 = bf16[8,128,1024]{2,1,0:T(8,128)(2,1)S(1)} all-to-all(bf16[8,128,1024]{2,1,0:T(8,128)(2,1)} %bitcast.34), channel_id=1, replica_groups=mesh['ctx'=64,'head'=8] {'head'}, dimensions={0} | all-to-all | bytes 4194304 | tf_op jit(solution)/shard_map/all_to_all | solution.py:181
  119.4 1.6 %copy.27 = bf16[8,16,8,1024]{3,2,0,1:T(8,128)(2,1)} copy(bf16[8,16,8,1024]{3,2,1,0:T(8,128)(2,1)S(1)} %bitcast.28) | data formatting | bytes 4194304 | tf_op jit(solution)/shard_map/all_to_all | solution.py:181
  (4 shorter events, 0.0 us)
Async XLA Ops:
  0.0 1.0 copy-start
  0.0 9.0 %copy-start.1 = (bf16[128,8192]{1,0:T(8,128)(2,1)S(1)}, bf16[128,8192]{1,0:T(8,128)(2,1)}, u32[]{:S(2)}) copy-start(bf16[128,8192]{1,0:T(8,128)(2,1)} %param.9) | copy-start | bytes 6291460
  2.9 16.2 %all-to-all-start.1 = ((bf16[128,8,256]{2,0,1:T(8,128)(2,1)}), bf16[128,8,256]{2,0,1:T(8,128)(2,1)S(1)}, u32[]{:S(2)}, u32[]{:S(2)}) async-start(bf16[128,8,256]{2,0,1:T(8,128)(2,1)} %pad_maximum_fusion.1), calls=%async_computation.1 | async-start | bytes 1048576 | tf_op jit(solution)/shard_map/all_to_all | solution.py:153
  19.1 6.8 %copy-start.4 = (s32[24]{0:T(128)S(1)}, s32[24]{0:T(128)}, u32[]{:S(2)}) copy-start(s32[24]{0:T(128)} %constant.52) | copy-start | bytes 292
  19.1 42.5 %all-to-all-start = ((bf16[128,8,1024]{2,0,1:T(8,128)(2,1)}), bf16[128,8,1024]{2,0,1:T(8,128)(2,1)S(1)}, u32[]{:S(2)}, u32[]{:S(2)}) async-start(bf16[128,8,1024]{2,0,1:T(8,128)(2,1)} %bitcast.27), calls=%async_computation | async-start | bytes 4194304 | tf_op jit(solution)/shard_map/all_to_all | solution.py:154
  22.8 8.2 %copy-start.3 = (pred[6]{0:T(512)(128)(4,1)S(1)}, pred[6]{0:T(512)(128)(4,1)}, u32[]{:S(2)}) copy-start(pred[6]{0:T(512)(128)(4,1)} %constant.51) | copy-start | bytes 22
  24.0 22.0 %collective-permute-start.1 = (bf16[1024,256]{1,0:T(8,128)(2,1)S(1)}, bf16[1024,256]{1,0:T(8,128)(2,1)S(1)}, u32[]{:S(2)}, u32[]{:S(2)}) collective-permute-start(bf16[1024,256]{1,0:T(8,128)(2,1)S(1)} %bitcast.29), channel_id=1, source_target_pairs={{0,8},{8,16},{16,24},{24,32},{32,40},{40,48},{48,56},{56,64},{64,7... | collective-permute-start | bytes 1572872 | tf_op jit(solution)/shard_map/ppermute | solution.py:28
  27.5 18.1 %collective-permute-start = (bf16[256,256]{1,0:T(8,128)(2,1)}, bf16[256,256]{1,0:T(8,128)(2,1)}, u32[]{:S(2)}, u32[]{:S(2)}) collective-permute-start(bf16[256,256]{1,0:T(8,128)(2,1)} %bitcast.4), channel_id=1, source_target_pairs={{0,16},{8,24},{16,32},{24,40},{32,48},{40,56},{48,64},{56,72},{64,... | collective-permute-start | bytes 393224 | tf_op jit(solution)/shard_map/ppermute | solution.py:28
  61.5 1.3 %copy-start.2 = (bf16[128,8,1024]{2,0,1:T(8,128)(2,1)}, bf16[128,8,1024]{2,0,1:T(8,128)(2,1)S(1)}, u32[]{:S(2)}) copy-start(bf16[128,8,1024]{2,0,1:T(8,128)(2,1)S(1)} %all-to-all-done) | copy-start | bytes 6291460

commit v9 on v8

--- a/solution.py
+++ b/solution.py
@@ -151,10 +151,11 @@
     paired = jnp.concatenate(
         [keys.reshape(rows, heads_axis, -1), values.reshape(rows, heads_axis, -1)], axis=2)
     local_pair = lax.all_to_all(paired, "head", split_axis=1, concat_axis=0, tiled=True)
-    local_queries = lax.all_to_all(queries, "head", split_axis=1, concat_axis=0, tiled=True)
     local_pair = local_pair.reshape(range_rows, 2 * HD)
     prev1 = from_behind(local_pair, "ctx", 1)
     prev2 = from_behind(local_pair[range_rows - BLOCK:], "ctx", 2)
+    queries, prev1, prev2 = lax.optimization_barrier((queries, prev1, prev2))
+    local_queries = lax.all_to_all(queries, "head", split_axis=1, concat_axis=0, tiled=True)
     window = jnp.concatenate([prev2, prev1, local_pair], axis=0)
     reach = BLOCK + range_rows
     n_q = range_rows // BLOCK

time: 122 us -> 133 us (1.090)
  the two profiles are of different devices: /device:TPU:128 before, /device:TPU:257 now
where the time goes in v9:
time: 133 us; the launch traced here: 132 us
  blocking collectives  43.7 us (33%)
  waiting for transfers between devices  32.5 us (24%)
  Pallas kernels  25 us (19%)
  local copies, waits for them, and re-layouts  16.9 us (13%)
  starting transfers between devices  11.9 us (9%)
  other arithmetic  2.34 us (2%)
    all_to_all x1, blocking collectives, shards(): lax.all_to_all(local_out, 'head', split_axis=0, concat_axis=1, tiled=True)  29.7 us
    pallas_call x1, Pallas kernels, attend(): pl.pallas_call(functools.partial(attend_kernel, heads=heads, n_steps=n_st...  25 us
    ppermute x2, waiting for transfers between devices, from_behind(): lax.ppermute(value, axis, [(source, source + steps) for source in range(l...  18.3 us
    all_to_all x1, waiting for transfers between devices, shards(): lax.all_to_all(queries, 'head', split_axis=1, concat_axis=0, tiled=True)  14.2 us
    all_to_all x1, blocking collectives, shards(): lax.all_to_all(paired, 'head', split_axis=1, concat_axis=0, tiled=True)  13.9 us
    ppermute x2, starting transfers between devices, from_behind(): lax.ppermute(value, axis, [(source, source + steps) for source in range(l...  8.15 us
    all_to_all x1, starting transfers between devices, shards(): lax.all_to_all(queries, 'head', split_axis=1, concat_axis=0, tiled=True)  3.74 us
    unnamed x12, local copies, waits for them, and re-layouts  2.91 us
  transfers between devices with their start and end apart: 3, of which 2 were waited for; matrix products, arithmetic and copies ran while one was open for 9% of the time, Pallas kernels for 0%

profile of v9, /device:TPU:257, one launch (start us, length us, event | category | flops | bytes accessed | tf_op | source)
XLA Modules:
  0.0 132.3 jit_solution(10889285714048093581)
XLA Ops:
  0.0 0.0 copy-start
  0.0 0.0 copy-start.1
  0.0 0.9 copy-done
  1.0 1.1 copy_bitcast_fusion.1
  2.0 0.1 pad_maximum_fusion.1
  2.1 13.9 %all_to_all.53 = bf16[128,8,256]{2,0,1:T(8,128)(2,1)S(1)} all-to-all(bf16[128,8,256]{2,0,1:T(8,128)(2,1)S(1)} %pad_maximum_fusion.1), channel_id=1, replica_groups=mesh['ctx'=64,'head'=8] {'head'}, dimensions={1} | all-to-all | bytes 1048576 | tf_op jit(solution)/shard_map/all_to_all | solution.py:153
  16.0 4.9 %collective-permute-start = (bf16[1024,256]{1,0:T(8,128)(2,1)S(1)}, bf16[1024,256]{1,0:T(8,128)(2,1)S(1)}, u32[]{:S(2)}, u32[]{:S(2)}) collective-permute-start(bf16[1024,256]{1,0:T(8,128)(2,1)S(1)} %bitcast.29), channel_id=1, source_target_pairs={{0,8},{8,16},{16,24},{24,32},{32,40},{40,48},{48,56},{56,64},{64,7... | collective-permute-start | bytes 1572872 | tf_op jit(solution)/shard_map/ppermute | solution.py:28
  21.0 3.2 %collective-permute-start.1 = (bf16[256,256]{1,0:T(8,128)(2,1)S(1)}, bf16[256,256]{1,0:T(8,128)(2,1)S(1)}, u32[]{:S(2)}, u32[]{:S(2)}) collective-permute-start(bf16[256,256]{1,0:T(8,128)(2,1)S(1)} %bitcast.35), channel_id=1, source_target_pairs={{0,16},{8,24},{16,32},{24,40},{32,48},{40,56},{48,64},{56,72},{64,... | collective-permute-start | bytes 393224 | tf_op jit(solution)/shard_map/ppermute | solution.py:28
  24.2 18.3 %collective-permute-done.1 = bf16[256,256]{1,0:T(8,128)(2,1)S(1)} collective-permute-done((bf16[256,256]{1,0:T(8,128)(2,1)S(1)}, bf16[256,256]{1,0:T(8,128)(2,1)S(1)}, u32[]{:S(2)}, u32[]{:S(2)}) %collective-permute-start.1) | collective-permute-done | bytes 131104 | tf_op jit(solution)/shard_map/ppermute | solution.py:28
  42.5 0.0 copy-start.3
  42.5 0.0 collective-permute-done
  42.5 0.6 copy-done.3
  43.2 0.0 copy-done.1
  43.2 1.6 %copy.31 = bf16[16,8,8,1024]{3,2,0,1:T(8,128)(2,1)} copy(bf16[16,8,8,1024]{3,2,1,0:T(8,128)(2,1)S(1)} %bitcast.32) | data formatting | bytes 4194304 | tf_op jit(solution)/shard_map/all_to_all | solution.py:158
  44.7 0.0 copy-start.5
  44.7 3.7 %all-to-all-start.1 = ((bf16[128,8,1024]{2,0,1:T(8,128)(2,1)}), bf16[128,8,1024]{2,0,1:T(8,128)(2,1)S(1)}, u32[]{:S(2)}, u32[]{:S(2)}) async-start(bf16[128,8,1024]{2,0,1:T(8,128)(2,1)} %bitcast.27), calls=%async_computation.1 | async-start | bytes 4194304 | tf_op jit(solution)/shard_map/all_to_all | solution.py:158
  48.5 0.8 dynamic_slice.7
  49.3 0.1 fusion.1
  49.4 0.6 reshape.50.kid_ref
  50.0 0.0 copy-done.5
  50.0 0.2 slice_reduce_fusion
  50.2 0.0 copy-start.4
  50.2 1.3 gather_fusion
  51.5 1.3 %reshape.53 = s32[4,6]{1,0:T(4,128)} reshape(s32[24]{0:T(128)} %gather_fusion) | data formatting | bytes 192 | tf_op jit(solution)/shard_map/gather | solution.py:176
  52.8 1.3 gather_fusion.1
  54.1 0.7 reshape.61
  54.8 0.7 slice_reduce_fusion.2
  55.5 0.7 and_convert_fusion
  56.3 0.7 reshape.51.full_ref
  57.0 1.0 copy.22.qid_ref
  58.0 1.4 %convert_reduce_fusion.nback_ref = s32[4]{0:T(128)} fusion(s32[4,6]{1,0:T(4,128)} %reshape.53, s32[4]{0:T(128)} %get-tuple-element.14, pred[6]{0:T(512)(128)(4,1)} %constant.51), kind=kLoop, calls=%fused_computation.17 | loop fusion | flops 92 | bytes 134 | tf_op jit(solution)/shard_map/reduce_sum | solution.py:177
  59.3 0.0 copy-done.4
  59.3 0.1 pad_maximum_fusion
  59.4 1.1 fusion.2
  60.5 14.2 %all-to-all-done.1 = bf16[128,8,1024]{2,0,1:T(8,128)(2,1)S(1)} async-done(((bf16[128,8,1024]{2,0,1:T(8,128)(2,1)}), bf16[128,8,1024]{2,0,1:T(8,128)(2,1)S(1)}, u32[]{:S(2)}, u32[]{:S(2)}) %all-to-all-start.1) | async-done | bytes 2097184 | tf_op jit(solution)/shard_map/all_to_all | solution.py:158
  74.8 0.0 copy-start.2
  74.8 1.3 copy-done.2
  76.1 25.0 %shard_map.91 = bf16[1024,1024]{1,0:T(8,128)(2,1)} custom-call(s32[4]{0:T(128)} %convert_reduce_fusion.nback_ref, s32[24]{0:T(128)} %reshape.51.full_ref, bf16[1024,1024]{1,0:T(8,128)(2,1)} %bitcast.33, bf16[2304,128]{1,0:T(8,128)(2,1)} %get-tuple-element.16.k_ref, bf16[2304,128]{1,0:T(8,128)(2,1)} %get-tuple-element.15.v_ref, s32[1024,1]{1,0:T(8,128)} %copy.22.qid_ref, ...), custom_call_target="tpu_custom_call" | custom-call | flops 48318382080 | bytes 4194304 | tf_op jit(solution)/shard_map/pallas_call | solution.py:136
  101.0 29.7 %all_to_all.54 = bf16[8,128,1024]{2,1,0:T(8,128)(2,1)S(1)} all-to-all(bf16[8,128,1024]{2,1,0:T(8,128)(2,1)} %bitcast.34), channel_id=1, replica_groups=mesh['ctx'=64,'head'=8] {'head'}, dimensions={0} | all-to-all | bytes 4194304 | tf_op jit(solution)/shard_map/all_to_all | solution.py:182
  130.8 1.6 %copy.27 = bf16[8,16,8,1024]{3,2,0,1:T(8,128)(2,1)} copy(bf16[8,16,8,1024]{3,2,1,0:T(8,128)(2,1)S(1)} %bitcast.28) | data formatting | bytes 4194304 | tf_op jit(solution)/shard_map/all_to_all | solution.py:182
  (5 shorter events, 0.0 us)
Async XLA Ops:
  0.0 1.0 copy-start
  0.0 43.2 %copy-start.1 = (bf16[128,8192]{1,0:T(8,128)(2,1)S(1)}, bf16[128,8192]{1,0:T(8,128)(2,1)}, u32[]{:S(2)}) copy-start(bf16[128,8192]{1,0:T(8,128)(2,1)} %param.9) | copy-start | bytes 6291460
  16.0 26.5 %collective-permute-start = (bf16[1024,256]{1,0:T(8,128)(2,1)S(1)}, bf16[1024,256]{1,0:T(8,128)(2,1)S(1)}, u32[]{:S(2)}, u32[]{:S(2)}) collective-permute-start(bf16[1024,256]{1,0:T(8,128)(2,1)S(1)} %bitcast.29), channel_id=1, source_target_pairs={{0,8},{8,16},{16,24},{24,32},{32,40},{40,48},{48,56},{56,64},{64,7... | collective-permute-start | bytes 1572872 | tf_op jit(solution)/shard_map/ppermute | solution.py:28
  21.0 21.5 %collective-permute-start.1 = (bf16[256,256]{1,0:T(8,128)(2,1)S(1)}, bf16[256,256]{1,0:T(8,128)(2,1)S(1)}, u32[]{:S(2)}, u32[]{:S(2)}) collective-permute-start(bf16[256,256]{1,0:T(8,128)(2,1)S(1)} %bitcast.35), channel_id=1, source_target_pairs={{0,16},{8,24},{16,32},{24,40},{32,48},{40,56},{48,64},{56,72},{64,... | collective-permute-start | bytes 393224 | tf_op jit(solution)/shard_map/ppermute | solution.py:28
  42.5 0.6 copy-start.3
  44.7 5.3 %copy-start.5 = (s32[24]{0:T(128)S(1)}, s32[24]{0:T(128)}, u32[]{:S(2)}) copy-start(s32[24]{0:T(128)} %constant.52) | copy-start | bytes 292
  44.7 30.0 %all-to-all-start.1 = ((bf16[128,8,1024]{2,0,1:T(8,128)(2,1)}), bf16[128,8,1024]{2,0,1:T(8,128)(2,1)S(1)}, u32[]{:S(2)}, u32[]{:S(2)}) async-start(bf16[128,8,1024]{2,0,1:T(8,128)(2,1)} %bitcast.27), calls=%async_computation.1 | async-start | bytes 4194304 | tf_op jit(solution)/shard_map/all_to_all | solution.py:158
  50.2 9.2 %copy-start.4 = (bf16[256,256]{1,0:T(8,128)(2,1)S(1)}, bf16[256,256]{1,0:T(8,128)(2,1)}, u32[]{:S(2)}) copy-start(bf16[256,256]{1,0:T(8,128)(2,1)} %copy-done.3) | copy-start | bytes 393220
  74.8 1.3 copy-start.2

commit v10 on v6

--- a/solution.py
+++ b/solution.py
@@ -35,28 +35,21 @@
     return jnp.concatenate(pieces[::-1] + [paired], axis=1)
 
 
-def attend_kernel(nback_ref, full_ref, q_ref, k_ref, v_ref, qid_ref, kid_ref, o_ref, m_scr, l_scr, acc_scr, *, heads, n_steps, mxu_sum):
+def attend_kernel(nback_ref, full_ref, q_ref, k_ref, v_ref, qid_ref, kid_ref, o_ref, m_scr, acc_scr, *, heads, n_steps, base):
     qb = pl.program_id(0)
-    step = pl.program_id(1)
-    last = pl.num_programs(1) - 1
+    diag = base + qb
 
-    @pl.when(step == 0)
-    def _init():
-        m_scr[...] = jnp.full(m_scr.shape, floor_score, jnp.float32)
-        if not mxu_sum:
-            l_scr[...] = jnp.zeros(l_scr.shape, jnp.float32)
-        acc_scr[...] = jnp.zeros(acc_scr.shape, jnp.float32)
-
-    def body(masked):
-        k = k_ref[...]
-        v = v_ref[...]
-        if mxu_sum:
-            v = jnp.concatenate([v, jnp.ones_like(v)], axis=1)
+    def visit(tile, masked, causal):
+        start = pl.multiple_of(tile * BLOCK, BLOCK)
+        k = k_ref[pl.ds(start, BLOCK), :]
+        v = v_ref[pl.ds(start, BLOCK), :]
+        v = jnp.concatenate([v, jnp.ones_like(v)], axis=1)
         if masked:
-            allowed = qid_ref[...] == kid_ref[...]
-            rows = lax.broadcasted_iota(jnp.int32, (BLOCK, BLOCK), 0)
-            cols = lax.broadcasted_iota(jnp.int32, (BLOCK, BLOCK), 1)
-            allowed = allowed & ((cols <= rows) | (step > 0))
+            allowed = qid_ref[...] == kid_ref[:, pl.ds(start, BLOCK)]
+            if causal:
+                rows = lax.broadcasted_iota(jnp.int32, (BLOCK, BLOCK), 0)
+                cols = lax.broadcasted_iota(jnp.int32, (BLOCK, BLOCK), 1)
+                allowed = allowed & (cols <= rows)
         for j in range(heads):
             q = q_ref[:, j * HD:(j + 1) * HD]
             s = lax.dot_general(q, k, (((1,), (1,)), ((), ())), preferred_element_type=jnp.float32)
@@ -68,70 +61,64 @@
             factor = jnp.exp(m_old - m_new)
             p = jnp.exp(s - jnp.tile(m_new, (1, BLOCK // 128)))
             pv = jnp.dot(p.astype(jnp.bfloat16), v, preferred_element_type=jnp.float32)
-            if mxu_sum:
-                acc_scr[j] = acc_scr[j] * jnp.tile(factor, (1, 2)) + pv
-            else:
-                l_scr[j] = l_scr[j] * factor + jnp.sum(p, axis=-1, keepdims=True)
-                acc_scr[j] = acc_scr[j] * factor + pv
+            acc_scr[j] = acc_scr[j] * jnp.tile(factor, (1, 2)) + pv
             m_scr[j] = m_new
 
-    live = step <= nback_ref[qb]
-    full = full_ref[qb * n_steps + step] > 0
+    m_scr[...] = jnp.full(m_scr.shape, floor_score, jnp.float32)
+    acc_scr[...] = jnp.zeros(acc_scr.shape, jnp.float32)
+    visit(diag, True, True)
 
-    @pl.when(live & full)
-    def _plain():
-        body(False)
+    def back(step, carry):
+        tile = diag - step
+        full = full_ref[qb * n_steps + step] > 0
 
-    @pl.when(live & jnp.logical_not(full))
-    def _masked():
-        body(True)
+        @pl.when(full)
+        def _plain():
+            visit(tile, False, False)
 
-    @pl.when(step == last)
-    def _finish():
-        for j in range(heads):
-            if mxu_sum:
-                total = acc_scr[j, :, HD:]
-                o_ref[:, j * HD:(j + 1) * HD] = (acc_scr[j, :, :HD] / total).astype(o_ref.dtype)
-            else:
-                o_ref[:, j * HD:(j + 1) * HD] = (acc_scr[j] / l_scr[j]).astype(o_ref.dtype)
+        @pl.when(jnp.logical_not(full))
+        def _masked():
+            visit(tile, True, False)
+
+        return carry
+
+    lax.fori_loop(1, nback_ref[qb] + 1, back, 0)
+    for j in range(heads):
+        total = acc_scr[j, :, HD:]
+        o_ref[:, j * HD:(j + 1) * HD] = (acc_scr[j, :, :HD] / total).astype(o_ref.dtype)
 
 
-def attend(nback, full, queries, keys, values, qids, kids, mxu_sum=MXU_SUM):
+def attend(nback, full, queries, keys, values, qids, kids):
     rows, width = queries.shape
     heads = width // HD
     n_q = rows // BLOCK
-    base = keys.shape[0] // BLOCK - n_q
+    span = keys.shape[0]
+    base = span // BLOCK - n_q
     n_steps = DOC_BLOCKS + 1
 
-    def kv_map(qb, step, nback_ref, full_ref):
-        return (base + qb - jnp.minimum(step, nback_ref[qb]), 0)
-
-    def kid_map(qb, step, nback_ref, full_ref):
-        return (0, base + qb - jnp.minimum(step, nback_ref[qb]))
-
+    whole = lambda qb, nb, fl: (0, 0)
     grid_spec = pltpu.PrefetchScalarGridSpec(
         num_scalar_prefetch=2,
-        grid=(n_q, n_steps),
+        grid=(n_q,),
         in_specs=[
-            pl.BlockSpec((BLOCK, width), lambda qb, step, nb, fl: (qb, 0)),
-            pl.BlockSpec((BLOCK, HD), kv_map),
-            pl.BlockSpec((BLOCK, HD), kv_map),
-            pl.BlockSpec((BLOCK, 1), lambda qb, step, nb, fl: (qb, 0)),
-            pl.BlockSpec((1, BLOCK), kid_map),
+            pl.BlockSpec((BLOCK, width), lambda qb, nb, fl: (qb, 0)),
+            pl.BlockSpec((span, HD), whole),
+            pl.BlockSpec((span, HD), whole),
+            pl.BlockSpec((BLOCK, 1), lambda qb, nb, fl: (qb, 0)),
+            pl.BlockSpec((1, span), whole),
         ],
-        out_specs=pl.BlockSpec((BLOCK, width), lambda qb, step, nb, fl: (qb, 0)),
+        out_specs=pl.BlockSpec((BLOCK, width), lambda qb, nb, fl: (qb, 0)),
         scratch_shapes=[
             pltpu.VMEM((heads, BLOCK, 128), jnp.float32),
-            pltpu.VMEM((heads, BLOCK, 128), jnp.float32),
-            pltpu.VMEM((heads, BLOCK, 2 * HD if mxu_sum else HD), jnp.float32),
+            pltpu.VMEM((heads, BLOCK, 2 * HD), jnp.float32),
         ],
     )
-    flops = 40 * rows * keys.shape[0] // 2 * HD * heads
+    flops = 40 * rows * span // 2 * HD * heads
     return pl.pallas_call(
-        functools.partial(attend_kernel, heads=heads, n_steps=n_steps, mxu_sum=mxu_sum),
+        functools.partial(attend_kernel, heads=heads, n_steps=n_steps, base=base),
         out_shape=jax.ShapeDtypeStruct((rows, width), queries.dtype),
         grid_spec=grid_spec,
-        compiler_params=pltpu.CompilerParams(dimension_semantics=("arbitrary", "arbitrary")),
+        compiler_params=pltpu.CompilerParams(dimension_semantics=("arbitrary",)),
         cost_estimate=pl.CostEstimate(
             flops=flops, transcendentals=flops // (20 * HD), bytes_accessed=4 * rows * width),
     )(nback, full, queries, keys, values, qids, kids)

time: 126 us -> 119 us (0.944)
  the two profiles are of different devices: /device:TPU:128 before, /device:TPU:256 now
where the time goes in v10:
time: 119 us
  waiting for transfers between devices  33 us (28%)
  blocking collectives  32.2 us (27%)
  Pallas kernels  23.6 us (20%)
  starting transfers between devices  14.3 us (12%)
  local copies, waits for them, and re-layouts  13.2 us (11%)
  other arithmetic  2.77 us (2%)
    all_to_all x1, blocking collectives, shards(): lax.all_to_all(local_out, 'head', split_axis=0, concat_axis=1, tiled=True)  32.2 us
    pallas_call x1, Pallas kernels, attend(): pl.pallas_call(functools.partial(attend_kernel, heads=heads, n_steps=n_st...  23.6 us
    ppermute x2, waiting for transfers between devices, from_behind(): lax.ppermute(value, axis, [(source, source + steps) for source in range(l...  13.1 us
    all_to_all x1, waiting for transfers between devices, shards(): lax.all_to_all(queries, 'head', split_axis=1, concat_axis=0, tiled=True)  11.4 us
    all_to_all x1, waiting for transfers between devices, shards(): lax.all_to_all(paired, 'head', split_axis=1, concat_axis=0, tiled=True)  8.52 us
    ppermute x2, starting transfers between devices, from_behind(): lax.ppermute(value, axis, [(source, source + steps) for source in range(l...  5.39 us
    all_to_all x1, starting transfers between devices, shards(): lax.all_to_all(paired, 'head', split_axis=1, concat_axis=0, tiled=True)  5.21 us
    all_to_all x1, starting transfers between devices, shards(): lax.all_to_all(queries, 'head', split_axis=1, concat_axis=0, tiled=True)  3.74 us
  transfers between devices with their start and end apart: 4, of which 4 were waited for; matrix products, arithmetic and copies ran while one was open for 9% of the time, Pallas kernels for 0%

profile of v10, /device:TPU:256, one launch (start us, length us, event | category | flops | bytes accessed | tf_op | source)
XLA Modules:
  0.0 119.3 jit_solution(5390343358972355018)
XLA Ops:
  0.0 0.0 copy-start
  0.0 0.0 copy-start.1
  0.0 0.9 copy-done
  1.0 1.1 copy_bitcast_fusion.1
  2.0 0.8 pad_maximum_fusion.1
  2.9 5.2 %all-to-all-start.1 = ((bf16[128,8,256]{2,0,1:T(8,128)(2,1)}), bf16[128,8,256]{2,0,1:T(8,128)(2,1)S(1)}, u32[]{:S(2)}, u32[]{:S(2)}) async-start(bf16[128,8,256]{2,0,1:T(8,128)(2,1)} %pad_maximum_fusion.1), calls=%async_computation.1 | async-start | bytes 1048576 | tf_op jit(solution)/shard_map/all_to_all | solution.py:134
  8.1 0.0 copy-done.1
  8.1 1.6 %copy.31 = bf16[16,8,8,1024]{3,2,0,1:T(8,128)(2,1)} copy(bf16[16,8,8,1024]{3,2,1,0:T(8,128)(2,1)S(1)} %bitcast.32) | data formatting | bytes 4194304 | tf_op jit(solution)/shard_map/all_to_all | solution.py:135
  9.7 8.5 %all-to-all-done.1 = bf16[128,8,256]{2,0,1:T(8,128)(2,1)S(1)} async-done(((bf16[128,8,256]{2,0,1:T(8,128)(2,1)}), bf16[128,8,256]{2,0,1:T(8,128)(2,1)S(1)}, u32[]{:S(2)}, u32[]{:S(2)}) %all-to-all-start.1) | async-done | bytes 524320 | tf_op jit(solution)/shard_map/all_to_all | solution.py:134
  18.2 0.0 copy-start.4
  18.2 3.7 %all-to-all-start = ((bf16[128,8,1024]{2,0,1:T(8,128)(2,1)}), bf16[128,8,1024]{2,0,1:T(8,128)(2,1)S(1)}, u32[]{:S(2)}, u32[]{:S(2)}) async-start(bf16[128,8,1024]{2,0,1:T(8,128)(2,1)} %bitcast.27), calls=%async_computation | async-start | bytes 4194304 | tf_op jit(solution)/shard_map/all_to_all | solution.py:135
  21.9 0.0 copy-start.3
  22.0 0.8 dynamic_slice.7
  22.8 0.1 fusion.1
  22.9 0.2 slice_reduce_fusion
  23.1 1.9 %collective-permute-start.1 = (bf16[1024,256]{1,0:T(8,128)(2,1)S(1)}, bf16[1024,256]{1,0:T(8,128)(2,1)S(1)}, u32[]{:S(2)}, u32[]{:S(2)}) collective-permute-start(bf16[1024,256]{1,0:T(8,128)(2,1)S(1)} %bitcast.29), channel_id=1, source_target_pairs={{0,8},{8,16},{16,24},{24,32},{32,40},{40,48},{48,56},{56,64},{64,7... | collective-permute-start | bytes 1572872 | tf_op jit(solution)/shard_map/ppermute | solution.py:28
  25.0 0.0 copy-done.4
  25.0 0.7 gather_fusion.1
  25.7 0.1 reshape.61
  25.8 0.2 slice_reduce_fusion.2
  26.0 0.7 slice.56
  26.6 3.5 %collective-permute-start = (bf16[256,256]{1,0:T(8,128)(2,1)}, bf16[256,256]{1,0:T(8,128)(2,1)}, u32[]{:S(2)}, u32[]{:S(2)}) collective-permute-start(bf16[256,256]{1,0:T(8,128)(2,1)} %bitcast.4), channel_id=1, source_target_pairs={{0,16},{8,24},{16,32},{24,40},{32,48},{40,56},{48,64},{56,72},{64,... | collective-permute-start | bytes 393224 | tf_op jit(solution)/shard_map/ppermute | solution.py:28
  30.1 0.0 copy-done.3
  30.1 0.1 and_convert_fusion
  30.2 0.6 reshape.50.kid_ref
  30.8 0.7 gather_fusion
  31.5 0.1 reshape.53
  31.6 0.6 reshape.51.full_ref
  32.2 1.0 copy.22.qid_ref
  33.2 0.8 convert_reduce_fusion.nback_ref
  34.0 11.3 %collective-permute-done = bf16[256,256]{1,0:T(8,128)(2,1)} collective-permute-done((bf16[256,256]{1,0:T(8,128)(2,1)}, bf16[256,256]{1,0:T(8,128)(2,1)}, u32[]{:S(2)}, u32[]{:S(2)}) %collective-permute-start) | collective-permute-done | bytes 131104 | tf_op jit(solution)/shard_map/ppermute | solution.py:28
  45.3 1.8 %collective-permute-done.1 = bf16[1024,256]{1,0:T(8,128)(2,1)S(1)} collective-permute-done((bf16[1024,256]{1,0:T(8,128)(2,1)S(1)}, bf16[1024,256]{1,0:T(8,128)(2,1)S(1)}, u32[]{:S(2)}, u32[]{:S(2)}) %collective-permute-start.1) | collective-permute-done | bytes 524320 | tf_op jit(solution)/shard_map/ppermute | solution.py:28
  47.1 1.0 pad_maximum_fusion
  48.1 1.1 fusion.2
  49.2 11.4 %all-to-all-done = bf16[128,8,1024]{2,0,1:T(8,128)(2,1)S(1)} async-done(((bf16[128,8,1024]{2,0,1:T(8,128)(2,1)}), bf16[128,8,1024]{2,0,1:T(8,128)(2,1)S(1)}, u32[]{:S(2)}, u32[]{:S(2)}) %all-to-all-start) | async-done | bytes 2097184 | tf_op jit(solution)/shard_map/all_to_all | solution.py:135
  60.6 0.0 copy-start.2
  60.6 1.3 %copy-done.2 = bf16[128,8,1024]{2,0,1:T(8,128)(2,1)} copy-done((bf16[128,8,1024]{2,0,1:T(8,128)(2,1)}, bf16[128,8,1024]{2,0,1:T(8,128)(2,1)S(1)}, u32[]{:S(2)}) %copy-start.2) | copy-done | bytes 2097176
  61.9 23.6 %shard_map.91 = bf16[1024,1024]{1,0:T(8,128)(2,1)} custom-call(s32[4]{0:T(128)} %convert_reduce_fusion.nback_ref, s32[24]{0:T(128)} %reshape.51.full_ref, bf16[1024,1024]{1,0:T(8,128)(2,1)} %bitcast.33, bf16[2304,128]{1,0:T(8,128)(2,1)} %get-tuple-element.10.k_ref, bf16[2304,128]{1,0:T(8,128)(2,1)} %get-tuple-element.9.v_ref, s32[1024,1]{1,0:T(8,128)} %copy.22.qid_ref, ...), custom_call_target="tpu_custom_call" | custom-call | flops 48318382080 | bytes 4194304 | tf_op jit(solution)/shard_map/pallas_call | solution.py:117
  85.5 32.2 %all_to_all.53 = bf16[8,128,1024]{2,1,0:T(8,128)(2,1)S(1)} all-to-all(bf16[8,128,1024]{2,1,0:T(8,128)(2,1)} %bitcast.34), channel_id=1, replica_groups=mesh['ctx'=64,'head'=8] {'head'}, dimensions={0} | all-to-all | bytes 4194304 | tf_op jit(solution)/shard_map/all_to_all | solution.py:162
  117.7 1.6 %copy.27 = bf16[8,16,8,1024]{3,2,0,1:T(8,128)(2,1)} copy(bf16[8,16,8,1024]{3,2,1,0:T(8,128)(2,1)S(1)} %bitcast.28) | data formatting | bytes 4194304 | tf_op jit(solution)/shard_map/all_to_all | solution.py:162
  (4 shorter events, 0.0 us)
Async XLA Ops:
  0.0 1.0 copy-start
  0.0 8.1 %copy-start.1 = (bf16[128,8192]{1,0:T(8,128)(2,1)S(1)}, bf16[128,8192]{1,0:T(8,128)(2,1)}, u32[]{:S(2)}) copy-start(bf16[128,8192]{1,0:T(8,128)(2,1)} %param.9) | copy-start | bytes 6291460
  2.9 15.3 %all-to-all-start.1 = ((bf16[128,8,256]{2,0,1:T(8,128)(2,1)}), bf16[128,8,256]{2,0,1:T(8,128)(2,1)S(1)}, u32[]{:S(2)}, u32[]{:S(2)}) async-start(bf16[128,8,256]{2,0,1:T(8,128)(2,1)} %pad_maximum_fusion.1), calls=%async_computation.1 | async-start | bytes 1048576 | tf_op jit(solution)/shard_map/all_to_all | solution.py:134
  18.2 6.8 %copy-start.4 = (s32[24]{0:T(128)S(1)}, s32[24]{0:T(128)}, u32[]{:S(2)}) copy-start(s32[24]{0:T(128)} %constant.52) | copy-start | bytes 292
  18.2 42.5 %all-to-all-start = ((bf16[128,8,1024]{2,0,1:T(8,128)(2,1)}), bf16[128,8,1024]{2,0,1:T(8,128)(2,1)S(1)}, u32[]{:S(2)}, u32[]{:S(2)}) async-start(bf16[128,8,1024]{2,0,1:T(8,128)(2,1)} %bitcast.27), calls=%async_computation | async-start | bytes 4194304 | tf_op jit(solution)/shard_map/all_to_all | solution.py:135
  21.9 8.2 %copy-start.3 = (pred[6]{0:T(512)(128)(4,1)S(1)}, pred[6]{0:T(512)(128)(4,1)}, u32[]{:S(2)}) copy-start(pred[6]{0:T(512)(128)(4,1)} %constant.51) | copy-start | bytes 22
  23.1 24.0 %collective-permute-start.1 = (bf16[1024,256]{1,0:T(8,128)(2,1)S(1)}, bf16[1024,256]{1,0:T(8,128)(2,1)S(1)}, u32[]{:S(2)}, u32[]{:S(2)}) collective-permute-start(bf16[1024,256]{1,0:T(8,128)(2,1)S(1)} %bitcast.29), channel_id=1, source_target_pairs={{0,8},{8,16},{16,24},{24,32},{32,40},{40,48},{48,56},{56,64},{64,7... | collective-permute-start | bytes 1572872 | tf_op jit(solution)/shard_map/ppermute | solution.py:28
  26.6 18.7 %collective-permute-start = (bf16[256,256]{1,0:T(8,128)(2,1)}, bf16[256,256]{1,0:T(8,128)(2,1)}, u32[]{:S(2)}, u32[]{:S(2)}) collective-permute-start(bf16[256,256]{1,0:T(8,128)(2,1)} %bitcast.4), channel_id=1, source_target_pairs={{0,16},{8,24},{16,32},{24,40},{32,48},{40,56},{48,64},{56,72},{64,... | collective-permute-start | bytes 393224 | tf_op jit(solution)/shard_map/ppermute | solution.py:28
  60.6 1.3 %copy-start.2 = (bf16[128,8,1024]{2,0,1:T(8,128)(2,1)}, bf16[128,8,1024]{2,0,1:T(8,128)(2,1)S(1)}, u32[]{:S(2)}) copy-start(bf16[128,8,1024]{2,0,1:T(8,128)(2,1)S(1)} %all-to-all-done) | copy-start | bytes 6291460
